TPU v7x, 128 devices: a whole 4x4x4 slice. The times are simulated.
128 devices in a mesh: src: 16 (over y_hi, z, core), tgt: 8 (over y_lo, x).
Axes of the slice: x: 4, y: 4 (y_hi: 2, y_lo: 2; y = y_hi * 2 + y_lo), z: 4, core: 2. Of those that a mesh axis runs over, the one named last changes fastest.
Arguments:
- positions: float32 [3, 16384], P(None, ('src', 'tgt')), as said below
- contact_bodies: int32 [2, 131072], P(None, ('src', 'tgt')), may hold values from 0 to 16383, as said below
- contact_frame: float32 [9, 131072], P(None, ('src', 'tgt')), as said below
- gaps: float32 [131072], P(('src', 'tgt')), may hold values from -1 to 1
- impulse_now: float32 [131072], P(('src', 'tgt')), may hold values from 0 to 1
- impulse_prev: float32 [131072], P(('src', 'tgt')), may hold values from 0 to 1
- step_sizes: float32 [2], replicated, may hold values from 0.05 to 0.2
Outputs:
- impulse: float32 [131072], P(('src', 'tgt'))
- body_velocity: float32 [6, 16384], P(None, ('src', 'tgt'))
Inputs may be any that keep to these rules, and one draw needn't show every extreme that they name: `contact_bodies`: each contact joins a body i with body i + 1, i + 32 or i + 1024, modulo 16384. `positions`: body k lies within 0.45 of the point 3 (k mod 32, k // 32 mod 32, k // 1024) along each coordinate. `contact_frame`: rows 0 to 2 of each column are a unit vector; rows 3 to 8 lie in -2 to 2.
All inputs are finite; a program needn't handle non-finite values.
Results may differ from a plain program's by a relative error of at most 0.0003.
Values sent between devices are 32-bit elements; how exact they have to be, the bound alone decides.
No kernel may reach another device: no remote copies, remote signals or barrier semaphores. Data moves between devices by JAX's collectives and lax.ppermute only.
A program may use at most 64 MiB of HBM per device.

v0:
```python
import math

import jax
import jax.numpy as jnp
from jax import lax
from jax.sharding import PartitionSpec as P

ITERS = 2


MOMENTUM = 0.4


def cross_product(first, second):
    return jnp.stack(
        [
            first[1] * second[2] - first[2] * second[1],
            first[2] * second[0] - first[0] * second[2],
            first[0] * second[1] - first[1] * second[0],
        ]
    )


def contact_rows(frame):
    normal = frame[0:3]
    lever_first = cross_product(frame[3:6], normal)
    lever_second = cross_product(frame[6:9], normal)
    return (jnp.concatenate([-normal, -lever_first]), jnp.concatenate([normal, lever_second]))


def pair_block(target_pos, target_ids, source_pos, source_ids, forces):
    delta_x = target_pos[0][:, None] - source_pos[0][None, :]
    delta_y = target_pos[1][:, None] - source_pos[1][None, :]
    delta_z = target_pos[2][:, None] - source_pos[2][None, :]
    coincide = target_ids[:, None] == source_ids[None, :]
    dist_sq = jnp.where(coincide, 1.0, delta_x * delta_x + delta_y * delta_y + delta_z * delta_z)
    inverse = jnp.where(coincide, 0.0, lax.rsqrt(dist_sq))
    self_term = jnp.where(coincide, 1.0, 0.0)
    unit_x = delta_x * inverse
    unit_y = delta_y * inverse
    unit_z = delta_z * inverse
    force_x, force_y, force_z = (forces[0][None, :], forces[1][None, :], forces[2][None, :])
    torque_x, torque_y, torque_z = (forces[3][None, :], forces[4][None, :], forces[5][None, :])
    inverse_sq = inverse * inverse
    c_one = 0.75 * inverse
    c_two = 0.75 * inverse_sq
    c_three = 0.375 * inverse_sq * inverse
    along_force = unit_x * force_x + unit_y * force_y + unit_z * force_z
    along_torque = unit_x * torque_x + unit_y * torque_y + unit_z * torque_z
    isotropic = c_one * (1.0 + inverse_sq * (2.0 / 3.0)) + self_term
    dyadic = c_one * (1.0 - 2.0 * inverse_sq) * along_force
    vel_x = isotropic * force_x + dyadic * unit_x + c_two * (torque_y * unit_z - torque_z * unit_y)
    vel_y = isotropic * force_y + dyadic * unit_y + c_two * (torque_z * unit_x - torque_x * unit_z)
    vel_z = isotropic * force_z + dyadic * unit_z + c_two * (torque_x * unit_y - torque_y * unit_x)
    spin_self = 0.75 * self_term - c_three
    spin_x = (
        c_two * (force_y * unit_z - force_z * unit_y)
        + c_three * 3.0 * unit_x * along_torque
        + spin_self * torque_x
    )
    spin_y = (
        c_two * (force_z * unit_x - force_x * unit_z)
        + c_three * 3.0 * unit_y * along_torque
        + spin_self * torque_y
    )
    spin_z = (
        c_two * (force_x * unit_y - force_y * unit_x)
        + c_three * 3.0 * unit_z * along_torque
        + spin_self * torque_z
    )
    return jnp.stack(
        [
            jnp.sum(vel_x, 1),
            jnp.sum(vel_y, 1),
            jnp.sum(vel_z, 1),
            jnp.sum(spin_x, 1),
            jnp.sum(spin_y, 1),
            jnp.sum(spin_z, 1),
        ]
    )


def assemble(slots_first, slots_second, first_rows, second_rows, shifted, body_count):
    forces = jnp.zeros((6, body_count), jnp.float32)
    forces = forces.at[:, slots_first].add(first_rows * shifted[None, :])
    return forces.at[:, slots_second].add(second_rows * shifted[None, :])


def per_device(
    positions, contact_bodies, contact_frame, gaps, impulse_now, impulse_prev, step_sizes
):
    src_count = lax.axis_size("src")
    tgt_count = lax.axis_size("tgt")
    own_rows = positions.shape[1]
    src_place = lax.axis_index("src")
    tgt_place = lax.axis_index("tgt")
    body_count = own_rows * src_count * tgt_count
    target_pos = lax.all_gather(positions, "tgt", axis=1, tiled=True)
    source_pos = lax.all_gather(positions, "src", axis=1, tiled=True)
    target_ids = src_place * tgt_count * own_rows + jnp.arange(
        tgt_count * own_rows, dtype=jnp.int32
    )
    gathered_index = jnp.arange(src_count * own_rows, dtype=jnp.int32)
    source_ids = (
        gathered_index // own_rows * tgt_count + tgt_place
    ) * own_rows + gathered_index % own_rows
    first_rows, second_rows = contact_rows(contact_frame)
    empty = jnp.zeros((6, tgt_count * own_rows), jnp.float32)
    current = impulse_now
    shifted = impulse_now + MOMENTUM * (impulse_now - impulse_prev)
    own_velocity = jnp.zeros((6, own_rows), jnp.float32)
    for k in range(ITERS):
        forces = assemble(
            contact_bodies[0], contact_bodies[1], first_rows, second_rows, shifted, body_count
        )
        mine = lax.psum_scatter(forces, ("src", "tgt"), scatter_dimension=1, tiled=True)
        shard_piece = lax.all_gather(mine, "src", axis=1, tiled=True)
        length = shard_piece.shape[1]
        block_width = math.gcd(length, 256)
        blocks = length // block_width

        def one_block(block_index, running_sum):
            inner = block_index * block_width
            force_block = lax.dynamic_slice_in_dim(shard_piece, inner, block_width, 1)
            place_block = lax.dynamic_slice_in_dim(source_pos, inner, block_width, 1)
            ids_block = lax.dynamic_slice_in_dim(source_ids, inner, block_width, 0)
            return running_sum + pair_block(
                target_pos, target_ids, place_block, ids_block, force_block
            )

        partial_value = lax.fori_loop(0, blocks, one_block, empty)
        own_velocity = lax.psum_scatter(partial_value, "tgt", scatter_dimension=1, tiled=True)
        gathered = lax.all_gather(own_velocity, ("src", "tgt"), axis=1, tiled=True)
        normal_rate = jnp.sum(first_rows * gathered[:, contact_bodies[0]], 0) + jnp.sum(
            second_rows * gathered[:, contact_bodies[1]], 0
        )
        updated = jnp.maximum(shifted - step_sizes[k] * (gaps + normal_rate), 0.0)
        shifted = updated + MOMENTUM * (updated - current)
        current = updated
    return (current, own_velocity)


def solution(mesh):
    placed = (
        P(None, ("src", "tgt")),
        P(None, ("src", "tgt")),
        P(None, ("src", "tgt")),
        P(("src", "tgt")),
        P(("src", "tgt")),
        P(("src", "tgt")),
        P(),
    )
    return jax.shard_map(
        per_device,
        mesh=mesh,
        in_specs=placed,
        out_specs=(P(("src", "tgt")), P(None, ("src", "tgt"))),
        check_vma=False,
    )
```

profile of v0, /device:TPU:1, one launch (start us, length us, event | category | flops | bytes accessed | tf_op | source)
XLA Modules:
  0.0 2345.2 jit_solution(6802810388750866491)
XLA Ops:
  7.2 1.1 multiply_subtract_fusion.2
  8.3 1.0 multiply_subtract_fusion.1
  9.3 0.7 multiply_add_fusion.3
  10.0 0.8 fusion.39
  11.1 0.8 compare_select_fusion.6
  12.1 9.7 scatter_custom_fusion
  21.8 12.0 scatter_fusion
  34.0 20.7 all_gather.18
  54.7 30.2 %all_gather.19 = f32[3,2048]{1,0:T(4,128)S(1)} all-gather(f32[3,128]{1,0:T(4,128)S(1)} %copy-done.4), channel_id=1, replica_groups=mesh['src'=16,'tgt'=8] {'src'}, dimensions={1}, use_global_device_ids=true | all-gather | bytes 26112 | tf_op jit(solution)/shard_map/all_gather | solution.py:99
  84.9 589.0 %reduce-scatter.5.cloned.1.call-done = f32[6,128]{0,1:T(8,128)} async-done(((f32[6,16384]{0,1:T(8,128)}), f32[6,128]{0,1:T(8,128)}) %reduce-scatter.5.cloned.1.call-update) | async-done | bytes 3088 | tf_op jit(solution)/shard_map/reduce_scatter | solution.py:116
  673.9 39.6 %all_gather.20 = f32[6,2048]{0,1:T(8,128)S(1)} all-gather(f32[6,128]{0,1:T(8,128)} %reduce-scatter.5.cloned.1.call-done), channel_id=1, replica_groups=mesh['src'=16,'tgt'=8] {'src'}, dimensions={1}, use_global_device_ids=true | all-gather | bytes 52224 | tf_op jit(solution)/shard_map/all_gather | solution.py:117
  713.5 0.3 copy.66
  713.8 48.1 %while.28 = (s32[]{:T(128)}, f32[6,1024]{1,0:T(8,128)S(1)}, s32[2048]{0:T(1024)S(1)}, f32[3,1024]{1,0:T(4,128)S(1)}, f32[3,2048]{1,0:T(4,128)S(1)}, /*index=5*/f...) while((s32[]{:T(128)}, f32[6,1024]{1,0:T(8,128)S(1)}, ...), condition=%wide.region_10.11_spmd.clone, body=%wide.region_3.10_spmd.clone.sunk | while | flops 25697292 | bytes 223529 | solution.py:131
  714.0 5.7 add_reduce_fusion.14
  720.1 5.7 add_reduce_fusion.14
  726.1 5.7 add_reduce_fusion.14
  732.1 5.7 add_reduce_fusion.14
  738.1 5.7 add_reduce_fusion.14
  744.1 5.7 add_reduce_fusion.14
  750.1 5.7 add_reduce_fusion.14
  756.1 5.7 add_reduce_fusion.14
  761.9 1.0 copy.67
  763.1 0.6 fusion.40
  764.1 25.7 %reduce-scatter.7.cloned.1.call-done = f32[6,128]{0,1:T(8,128)} async-done(((f32[6,1024]{0,1:T(8,128)}), f32[6,128]{0,1:T(8,128)}) %reduce-scatter.7.cloned.1.call-update) | async-done | bytes 3088 | tf_op jit(solution)/shard_map/reduce_scatter | solution.py:132
  789.8 368.0 %all_gather.21 = f32[6,16384]{0,1:T(8,128)} all-gather(f32[6,128]{0,1:T(8,128)} %reduce-scatter.7.cloned.1.call-done), channel_id=1, replica_groups=mesh['src'=16,'tgt'=8] {'src','tgt'}, dimensions={1}, use_global_device_ids=true | all-gather | bytes 396288 | tf_op jit(solution)/shard_map/all_gather | solution.py:133
  1157.8 6.2 gather_fusion.1
  1164.0 6.2 gather_fusion
  1170.6 0.6 multiply_add_fusion.2
  1171.4 9.7 scatter_custom_fusion.2
  1181.4 12.0 scatter_fusion.1
  1193.5 646.0 %reduce-scatter.9.cloned.1.call-done = f32[6,128]{0,1:T(8,128)} async-done(((f32[6,16384]{0,1:T(8,128)}), f32[6,128]{0,1:T(8,128)}) %reduce-scatter.9.cloned.1.call-update) | async-done | bytes 3088 | tf_op jit(solution)/shard_map/reduce_scatter | solution.py:116
  1839.5 39.7 %all_gather.22 = f32[6,2048]{0,1:T(8,128)S(1)} all-gather(f32[6,128]{0,1:T(8,128)} %reduce-scatter.9.cloned.1.call-done), channel_id=1, replica_groups=mesh['src'=16,'tgt'=8] {'src'}, dimensions={1}, use_global_device_ids=true | all-gather | bytes 52224 | tf_op jit(solution)/shard_map/all_gather | solution.py:117
  1879.5 48.2 %while.29 = (s32[]{:T(128)}, f32[6,1024]{1,0:T(8,128)S(1)}, s32[2048]{0:T(1024)S(1)}, f32[3,1024]{1,0:T(4,128)S(1)}, f32[3,2048]{1,0:T(4,128)S(1)}, /*index=5*/f...) while((s32[]{:T(128)}, f32[6,1024]{1,0:T(8,128)S(1)}, ...), condition=%wide.region_24.25_spmd.clone, body=%wide.region_17.24_spmd.clone.sunk | while | flops 25697292 | bytes 223529 | solution.py:131
  1879.7 5.7 add_reduce_fusion.15
  1885.8 5.7 add_reduce_fusion.15
  1891.8 5.7 add_reduce_fusion.15
  1897.8 5.7 add_reduce_fusion.15
  1903.9 5.7 add_reduce_fusion.15
  1909.9 5.7 add_reduce_fusion.15
  1915.9 5.7 add_reduce_fusion.15
  1922.0 5.7 add_reduce_fusion.15
  1927.8 1.0 copy.73
  1928.8 26.8 %reduce-scatter.11.cloned.1.call-done = f32[6,128]{0,1:T(8,128)} async-done(((f32[6,1024]{0,1:T(8,128)}), f32[6,128]{0,1:T(8,128)}) %reduce-scatter.11.cloned.1.call-update) | async-done | bytes 3088 | tf_op jit(solution)/shard_map/reduce_scatter | solution.py:132
  1955.6 368.3 %all_gather.23 = f32[6,16384]{0,1:T(8,128)} all-gather(f32[6,128]{0,1:T(8,128)} %reduce-scatter.11.cloned.1.call-done), channel_id=1, replica_groups=mesh['src'=16,'tgt'=8] {'src','tgt'}, dimensions={1}, use_global_device_ids=true | all-gather | bytes 396288 | tf_op jit(solution)/shard_map/all_gather | solution.py:133
  2323.9 6.2 gather_fusion.3
  2330.1 6.2 gather_fusion.2
  2336.7 1.2 subtract_maximum_fusion
  2338.0 0.7 copy.76
  (134 shorter events, 6.9 us)
Async XLA Ops:
  7.2 666.7 %reduce-scatter.5.cloned.1.call-start = ((), (), s32[]{:S(2)}) async-start(), calls=%async_computation.4 | async-start | bytes 8454144 | tf_op jit(solution)/shard_map/reduce_scatter | solution.py:116
  12.1 21.9 copy-start.4
  21.8 741.2 %copy-start.5 = (f32[2]{0:T(128)S(1)}, f32[2]{0:T(128)}, u32[]{:S(2)}) copy-start(f32[2]{0:T(128)} %param.17) | copy-start | bytes 28
  33.9 755.9 %reduce-scatter.7.cloned.1.call-start = ((), (), s32[]{:S(2)}) async-start(), calls=%async_computation.5 | async-start | bytes 589824 | tf_op jit(solution)/shard_map/reduce_scatter | solution.py:132
  713.8 456.8 %copy-start.1 = (f32[1024]{0:T(1024)S(1)}, f32[1024]{0:T(1024)}, u32[]{:S(2)}) copy-start(f32[1024]{0:T(1024)} %param.15) | copy-start | bytes 12292
  713.8 456.8 %copy-start.2 = (f32[1024]{0:T(1024)S(1)}, f32[1024]{0:T(1024)}, u32[]{:S(2)}) copy-start(f32[1024]{0:T(1024)} %param.16) | copy-start | bytes 12292
  713.8 456.8 %copy-start.3 = (f32[1024]{0:T(1024)S(1)}, f32[1024]{0:T(1024)}, u32[]{:S(2)}) copy-start(f32[1024]{0:T(1024)} %param.14) | copy-start | bytes 12292
  763.0 1076.5 %reduce-scatter.9.cloned.1.call-start = ((), (), s32[]{:S(2)}) async-start(), calls=%async_computation.6 | async-start | bytes 8454144 | tf_op jit(solution)/shard_map/reduce_scatter | solution.py:116
  1193.5 762.1 %reduce-scatter.11.cloned.1.call-start = ((), (), s32[]{:S(2)}) async-start(), calls=%async_computation.7 | async-start | bytes 589824 | tf_op jit(solution)/shard_map/reduce_scatter | solution.py:132
  1955.6 382.4 %copy-start = (f32[6,128]{0,1:T(8,128)S(1)}, f32[6,128]{0,1:T(8,128)}, u32[]{:S(2)}) copy-start(f32[6,128]{0,1:T(8,128)} %reduce-scatter.11.cloned.1.call-done) | copy-start | bytes 9220
Sparse Core Ops, SparseCore 0:
  34.0 639.8 reduce-scatter.4
  763.1 26.5 reduce-scatter.6
  1193.6 645.9 reduce-scatter.8
  1928.9 26.5 reduce-scatter.10
where the time goes:
time: 2360 us; the launch traced here: 2350 us
  waiting for transfers between devices  1290 us (55%)
  blocking collectives  866 us (37%)
  other arithmetic  142 us (6%)
  local copies, waits for them, and re-layouts  33.9 us (1%)
    reduce_scatter x2, waiting for transfers between devices, per_device(): lax.psum_scatter(forces, ('src', 'tgt'), scatter_dimension=1, tiled=True)  1240 us
    all_gather x2, blocking collectives, per_device(): gathered = lax.all_gather(own_velocity, ('src', 'tgt'), axis=1, tiled=True)  736 us
    reduce_sum x16, other arithmetic, pair_block(): jnp.sum(spin_z, 1)  91.4 us
    all_gather x2, blocking collectives, per_device(): shard_piece = lax.all_gather(mine, 'src', axis=1, tiled=True)  79.2 us
    reduce_scatter x2, waiting for transfers between devices, per_device(): lax.psum_scatter(partial_value, 'tgt', scatter_dimension=1, tiled=True)  52.4 us
  transfers between devices with their start and end apart: 4, of which 4 were waited for; matrix products, arithmetic and copies ran while one was open for 0% of the time, Pallas kernels for 0%

commit v1 on v0

v1 whole, which is shorter than its diff:
```python
import jax
import jax.numpy as jnp
from jax import lax
from jax.sharding import PartitionSpec as P

ITERS = 2
MOMENTUM = 0.4
AXES = ("src", "tgt")
SOURCE_BLOCK = 1024


def cross_product(first, second):
    return jnp.stack(
        [
            first[1] * second[2] - first[2] * second[1],
            first[2] * second[0] - first[0] * second[2],
            first[0] * second[1] - first[1] * second[0],
        ]
    )


def contact_rows(frame):
    normal = frame[0:3]
    lever_first = cross_product(frame[3:6], normal)
    lever_second = cross_product(frame[6:9], normal)
    return (jnp.concatenate([-normal, -lever_first]), jnp.concatenate([normal, lever_second]))


def pair_block(target_pos, target_ids, source_pos, source_ids, forces):
    delta_x = target_pos[0][None, :] - source_pos[0][:, None]
    delta_y = target_pos[1][None, :] - source_pos[1][:, None]
    delta_z = target_pos[2][None, :] - source_pos[2][:, None]
    coincide = target_ids[None, :] == source_ids[:, None]
    dist_sq = jnp.where(coincide, 1.0, delta_x * delta_x + delta_y * delta_y + delta_z * delta_z)
    inverse = jnp.where(coincide, 0.0, lax.rsqrt(dist_sq))
    self_term = jnp.where(coincide, 1.0, 0.0)
    unit_x = delta_x * inverse
    unit_y = delta_y * inverse
    unit_z = delta_z * inverse
    force_x, force_y, force_z = (forces[0][:, None], forces[1][:, None], forces[2][:, None])
    torque_x, torque_y, torque_z = (forces[3][:, None], forces[4][:, None], forces[5][:, None])
    inverse_sq = inverse * inverse
    c_one = 0.75 * inverse
    c_two = 0.75 * inverse_sq
    c_three = 0.375 * inverse_sq * inverse
    along_force = unit_x * force_x + unit_y * force_y + unit_z * force_z
    along_torque = unit_x * torque_x + unit_y * torque_y + unit_z * torque_z
    isotropic = c_one * (1.0 + inverse_sq * (2.0 / 3.0)) + self_term
    dyadic = c_one * (1.0 - 2.0 * inverse_sq) * along_force
    vel_x = isotropic * force_x + dyadic * unit_x + c_two * (torque_y * unit_z - torque_z * unit_y)
    vel_y = isotropic * force_y + dyadic * unit_y + c_two * (torque_z * unit_x - torque_x * unit_z)
    vel_z = isotropic * force_z + dyadic * unit_z + c_two * (torque_x * unit_y - torque_y * unit_x)
    spin_self = 0.75 * self_term - c_three
    spin_x = (
        c_two * (force_y * unit_z - force_z * unit_y)
        + c_three * 3.0 * unit_x * along_torque
        + spin_self * torque_x
    )
    spin_y = (
        c_two * (force_z * unit_x - force_x * unit_z)
        + c_three * 3.0 * unit_y * along_torque
        + spin_self * torque_y
    )
    spin_z = (
        c_two * (force_x * unit_y - force_y * unit_x)
        + c_three * 3.0 * unit_z * along_torque
        + spin_self * torque_z
    )
    return jnp.stack(
        [
            jnp.sum(vel_x, 0),
            jnp.sum(vel_y, 0),
            jnp.sum(vel_z, 0),
            jnp.sum(spin_x, 0),
            jnp.sum(spin_y, 0),
            jnp.sum(spin_z, 0),
        ]
    )


def gather_all(block, devices):
    rows, width = block.shape
    spread = jnp.broadcast_to(block[None], (devices, rows, width))
    spread = lax.all_to_all(spread, AXES, 0, 0, tiled=True)
    return spread.transpose(1, 0, 2).reshape(rows, devices * width)


def scatter_sum(full, devices):
    rows, length = full.shape
    width = length // devices
    pieces = full.reshape(rows, devices, width).transpose(1, 0, 2)
    pieces = lax.all_to_all(pieces, AXES, 0, 0, tiled=True)
    return jnp.sum(pieces, 0)


def per_device(
    positions, contact_bodies, contact_frame, gaps, impulse_now, impulse_prev, step_sizes
):
    devices = lax.axis_size("src") * lax.axis_size("tgt")
    me = lax.axis_index("src") * lax.axis_size("tgt") + lax.axis_index("tgt")
    own_rows = positions.shape[1]
    body_count = own_rows * devices
    all_pos = gather_all(positions, devices)
    target_ids = me * own_rows + jnp.arange(own_rows, dtype=jnp.int32)
    first_rows, second_rows = contact_rows(contact_frame)
    current = impulse_now
    shifted = impulse_now + MOMENTUM * (impulse_now - impulse_prev)
    own_velocity = jnp.zeros((6, own_rows), jnp.float32)
    block = min(SOURCE_BLOCK, body_count)
    blocks = body_count // block
    for k in range(ITERS):
        forces = jnp.zeros((6, body_count), jnp.float32)
        forces = forces.at[:, contact_bodies[0]].add(first_rows * shifted[None, :])
        forces = forces.at[:, contact_bodies[1]].add(second_rows * shifted[None, :])
        own_forces = scatter_sum(forces, devices)
        all_forces = gather_all(own_forces, devices)

        def one_block(block_index, running_sum):
            start = block_index * block
            force_block = lax.dynamic_slice_in_dim(all_forces, start, block, 1)
            place_block = lax.dynamic_slice_in_dim(all_pos, start, block, 1)
            ids_block = start + jnp.arange(block, dtype=jnp.int32)
            return running_sum + pair_block(
                positions, target_ids, place_block, ids_block, force_block
            )

        own_velocity = lax.fori_loop(
            0, blocks, one_block, jnp.zeros((6, own_rows), jnp.float32)
        )
        gathered = gather_all(own_velocity, devices)
        normal_rate = jnp.sum(first_rows * gathered[:, contact_bodies[0]], 0) + jnp.sum(
            second_rows * gathered[:, contact_bodies[1]], 0
        )
        updated = jnp.maximum(shifted - step_sizes[k] * (gaps + normal_rate), 0.0)
        shifted = updated + MOMENTUM * (updated - current)
        current = updated
    return (current, own_velocity)


def solution(mesh):
    placed = (
        P(None, AXES),
        P(None, AXES),
        P(None, AXES),
        P(AXES),
        P(AXES),
        P(AXES),
        P(),
    )
    return jax.shard_map(
        per_device,
        mesh=mesh,
        in_specs=placed,
        out_specs=(P(AXES), P(None, AXES)),
        check_vma=False,
    )
```

time: 2360 us -> 311 us (0.13)
  waiting for transfers between devices: 1290 us -> 48.5 us
  blocking collectives: 866 us -> 59.4 us
    reduce_scatter x4 -> x0, waiting for transfers between devices: 1290 us -> none  [the longest x2 1240 us: per_device(): lax.psum_scatter(forces, ('src', 'tgt'), scatter_dimension=1, tiled=True)]
    all_gather x6 -> x0, blocking collectives: 866 us -> none  [the longest x2 736 us: per_device(): gathered = lax.all_gather(own_velocity, ('src', 'tgt'), axis=1, tiled=True)]
    all_to_all x0 -> x3, blocking collectives: none -> 59.4 us  [the longest x2 41.8 us: scatter_sum(): pieces = lax.all_to_all(pieces, AXES, 0, 0, tiled=True)]
    all_to_all x0 -> x4, waiting for transfers between devices: none -> 48.5 us  [gather_all(): spread = lax.all_to_all(spread, AXES, 0, 0, tiled=True)]
    reduce_sum x16 -> x34, other arithmetic: 91.4 us -> 72.5 us  [the longest x32 72.2 us: pair_block(): jnp.sum(spin_z, 0)]
where the time goes in v1:
time: 311 us; the launch traced here: 310 us
  other arithmetic  124 us (40%)
  blocking collectives  59.4 us (19%)
  local copies, waits for them, and re-layouts  56 us (18%)
  waiting for transfers between devices  48.5 us (16%)
  starting transfers between devices  18.9 us (6%)
    reduce_sum x32, other arithmetic, pair_block(): jnp.sum(spin_z, 0)  72.2 us
    all_to_all x4, waiting for transfers between devices, gather_all(): spread = lax.all_to_all(spread, AXES, 0, 0, tiled=True)  48.5 us
    all_to_all x2, blocking collectives, scatter_sum(): pieces = lax.all_to_all(pieces, AXES, 0, 0, tiled=True)  41.8 us
    scatter-add x2, other arithmetic, per_device(): forces = forces.at[:, contact_bodies[1]].add(second_rows * shifted[None, :])  24 us
    scatter-add x2, other arithmetic, per_device(): forces = forces.at[:, contact_bodies[0]].add(first_rows * shifted[None, :])  19.5 us
    all_to_all x4, starting transfers between devices, gather_all(): spread = lax.all_to_all(spread, AXES, 0, 0, tiled=True)  18.9 us
    all_to_all x1, blocking collectives, gather_all(): spread = lax.all_to_all(spread, AXES, 0, 0, tiled=True)  17.6 us
    gather x2, local copies, waits for them, and re-layouts, per_device(): gathered[:, contact_bodies[0]]  12.4 us
  transfers between devices with their start and end apart: 4, of which 4 were waited for; matrix products, arithmetic and copies ran while one was open for 0% of the time, Pallas kernels for 0%

profile of v1, /device:TPU:1, one launch (start us, length us, event | category | flops | bytes accessed | tf_op | source)
XLA Modules:
  0.0 309.6 jit_solution(15478274172333831839)
XLA Ops:
  5.5 9.7 %scatter_custom_fusion = f32[6,16384]{0,1:T(8,128)} fusion(s32[1024]{0:T(1024)S(1)} %bitcast.189, f32[1024,6]{1,0:T(8,128)S(1)} %copy.61, f32[]{:T(128)} %constant.160.clone.1), kind=kCustom, calls=%fused_computation.80 | custom fusion | flops 6144 | bytes 393220 | tf_op jit(solution)/shard_map/scatter-add | solution.py:113
  15.2 12.0 %scatter_fusion = f32[6,16384]{0,1:T(8,128)} fusion(f32[6,16384]{0,1:T(8,128)} %scatter_custom_fusion, s32[1024]{0:T(1024)S(1)} %bitcast.186, f32[1024,6]{1,0:T(8,128)S(1)} %copy.62), kind=kCustom, calls=%fused_computation.5 | custom fusion | flops 6144 | bytes 77824 | tf_op jit(solution)/shard_map/scatter-add | solution.py:114
  27.3 5.5 %copy.63 = f32[6,128,128]{2,0,1:T(8,128)S(1)} copy(f32[6,128,128]{0,2,1:T(8,128)} %bitcast.156) | data formatting | bytes 786432 | tf_op jit(solution)/shard_map/reshape | solution.py:91
  32.8 24.2 %all_to_all.35 = f32[128,6,128]{2,1,0:T(8,128)S(1)} all-to-all(f32[128,6,128]{2,1,0:T(8,128)S(1)} %bitcast.162), channel_id=1, replica_groups=mesh['src'=16,'tgt'=8] {'src','tgt'}, dimensions={0} | all-to-all | bytes 786432 | tf_op jit(solution)/shard_map/all_to_all | solution.py:92
  57.7 4.9 %all-to-all-start = ((f32[128,3,128]{2,1,0:T(4,128)}), f32[128,3,128]{2,1,0:T(4,128)S(1)}, u32[]{:S(2)}, u32[]{:S(2)}) async-start(f32[128,3,128]{2,1,0:T(4,128)} %broadcast_in_dim.89), calls=%async_computation | async-start | bytes 524288 | tf_op jit(solution)/shard_map/all_to_all | solution.py:84
  62.8 10.8 %all-to-all-done = f32[128,3,128]{2,1,0:T(4,128)S(1)} async-done(((f32[128,3,128]{2,1,0:T(4,128)}), f32[128,3,128]{2,1,0:T(4,128)S(1)}, u32[]{:S(2)}, u32[]{:S(2)}) %all-to-all-start) | async-done | bytes 196640 | tf_op jit(solution)/shard_map/all_to_all | solution.py:84
  74.4 4.2 %all-to-all-start.2 = ((f32[128,6,128]{2,1,0:T(8,128)}), f32[128,6,128]{2,1,0:T(8,128)S(1)}, u32[]{:S(2)}, u32[]{:S(2)}) async-start(f32[128,6,128]{2,1,0:T(8,128)} %broadcast_in_dim.90), calls=%async_computation.2 | async-start | bytes 1048576 | tf_op jit(solution)/shard_map/all_to_all | solution.py:84
  78.6 13.0 %all-to-all-done.2 = f32[128,6,128]{2,1,0:T(8,128)S(1)} async-done(((f32[128,6,128]{2,1,0:T(8,128)}), f32[128,6,128]{2,1,0:T(8,128)S(1)}, u32[]{:S(2)}, u32[]{:S(2)}) %all-to-all-start.2) | async-done | bytes 393248 | tf_op jit(solution)/shard_map/all_to_all | solution.py:84
  91.7 40.0 %while.28 = (s32[]{:T(128)}, f32[6,128]{1,0:T(8,128)S(1)}, f32[3,128]{1,0:T(4,128)S(1)}, f32[3,16384]{1,0:T(4,128)S(1)}, f32[6,16384]{1,0:T(8,128)S(1)}, /*index...) while((s32[]{:T(128)}, f32[6,128]{1,0:T(8,128)S(1)}, ...), condition=%wide.region_10.11_spmd.clone, body=%wide.region_3.10_spmd.clone.sunk | while | flops 12846988 | bytes 143137 | solution.py:127
  91.8 2.2 add_reduce_fusion.14
  94.3 2.2 add_reduce_fusion.14
  101.8 2.2 add_reduce_fusion.14
  111.8 2.2 add_reduce_fusion.14
  119.4 2.2 add_reduce_fusion.14
  121.9 2.2 add_reduce_fusion.14
  129.4 2.2 add_reduce_fusion.14
  132.5 4.9 %all-to-all-start.3 = ((f32[128,6,128]{2,1,0:T(8,128)}), f32[128,6,128]{2,1,0:T(8,128)S(1)}, u32[]{:S(2)}, u32[]{:S(2)}) async-start(f32[128,6,128]{2,1,0:T(8,128)} %broadcast_in_dim.91), calls=%async_computation.3 | async-start | bytes 1048576 | tf_op jit(solution)/shard_map/all_to_all | solution.py:84
  138.5 11.9 %all-to-all-done.3 = f32[128,6,128]{2,1,0:T(8,128)S(1)} async-done(((f32[128,6,128]{2,1,0:T(8,128)}), f32[128,6,128]{2,1,0:T(8,128)S(1)}, u32[]{:S(2)}, u32[]{:S(2)}) %all-to-all-start.3) | async-done | bytes 393248 | tf_op jit(solution)/shard_map/all_to_all | solution.py:84
  150.3 4.9 %copy.66 = f32[6,128,128]{0,2,1:T(8,128)} copy(f32[6,128,128]{2,0,1:T(8,128)S(1)} %bitcast.161) | data formatting | bytes 786432 | tf_op jit(solution)/shard_map/transpose | solution.py:85
  155.2 6.2 %gather_fusion.1 = f32[1024,6]{1,0:T(8,128)S(1)} fusion(f32[6,16384]{0,1:T(8,128)} %bitcast.159, s32[1024]{0:T(1024)S(1)} %broadcast_clamp_fusion), kind=kCustom, calls=%fused_computation.1 | custom fusion | bytes 53248 | tf_op jit(solution)/shard_map/gather | solution.py:132
  161.4 6.2 %gather_fusion = f32[1024,6]{1,0:T(8,128)S(1)} fusion(f32[6,16384]{0,1:T(8,128)} %bitcast.160, s32[1024]{0:T(1024)S(1)} %broadcast_clamp_fusion.1), kind=kCustom, calls=%fused_computation | custom fusion | bytes 53248 | tf_op jit(solution)/shard_map/gather | solution.py:131
  168.9 9.7 %scatter_custom_fusion.2 = f32[6,16384]{0,1:T(8,128)} fusion(s32[1024]{0:T(1024)S(1)} %bitcast.191, f32[1024,6]{1,0:T(8,128)S(1)} %copy.69, f32[]{:T(128)} %constant.160.clone.1), kind=kCustom, calls=%fused_computation.78 | custom fusion | flops 6144 | bytes 393220 | tf_op jit(solution)/shard_map/scatter-add | solution.py:113
  178.9 12.0 %scatter_fusion.1 = f32[6,16384]{0,1:T(8,128)} fusion(f32[6,16384]{0,1:T(8,128)} %scatter_custom_fusion.2, s32[1024]{0:T(1024)S(1)} %bitcast.188, f32[1024,6]{1,0:T(8,128)S(1)} %copy.70), kind=kCustom, calls=%fused_computation.7 | custom fusion | flops 6144 | bytes 77824 | tf_op jit(solution)/shard_map/scatter-add | solution.py:114
  190.9 5.5 %copy.71 = f32[6,128,128]{2,0,1:T(8,128)S(1)} copy(f32[6,128,128]{0,2,1:T(8,128)} %bitcast.155) | data formatting | bytes 786432 | tf_op jit(solution)/shard_map/reshape | solution.py:91
  196.4 17.6 %all_to_all.36 = f32[128,6,128]{2,1,0:T(8,128)S(1)} all-to-all(f32[128,6,128]{2,1,0:T(8,128)S(1)} %bitcast.163), channel_id=1, replica_groups=mesh['src'=16,'tgt'=8] {'src','tgt'}, dimensions={0} | all-to-all | bytes 786432 | tf_op jit(solution)/shard_map/all_to_all | solution.py:92
  215.0 4.9 %all-to-all-start.5 = ((f32[128,6,128]{2,1,0:T(8,128)}), f32[128,6,128]{2,1,0:T(8,128)S(1)}, u32[]{:S(2)}, u32[]{:S(2)}) async-start(f32[128,6,128]{2,1,0:T(8,128)} %broadcast_in_dim.92), calls=%async_computation.5 | async-start | bytes 1048576 | tf_op jit(solution)/shard_map/all_to_all | solution.py:84
  219.9 12.9 %all-to-all-done.5 = f32[128,6,128]{2,1,0:T(8,128)S(1)} async-done(((f32[128,6,128]{2,1,0:T(8,128)}), f32[128,6,128]{2,1,0:T(8,128)S(1)}, u32[]{:S(2)}, u32[]{:S(2)}) %all-to-all-start.5) | async-done | bytes 393248 | tf_op jit(solution)/shard_map/all_to_all | solution.py:84
  232.8 40.3 %while.29 = (s32[]{:T(128)}, f32[6,128]{1,0:T(8,128)S(1)}, f32[3,128]{1,0:T(4,128)S(1)}, f32[3,16384]{1,0:T(4,128)S(1)}, f32[6,16384]{1,0:T(8,128)S(1)}, /*index...) while((s32[]{:T(128)}, f32[6,128]{1,0:T(8,128)S(1)}, ...), condition=%wide.region_23.24_spmd.clone, body=%wide.region_16.23_spmd.clone.sunk | while | flops 12846988 | bytes 143137 | solution.py:127
  233.0 2.3 add_reduce_fusion.15
  235.5 2.3 add_reduce_fusion.15
  238.0 2.3 add_reduce_fusion.15
  240.5 2.3 add_reduce_fusion.15
  243.1 2.3 add_reduce_fusion.15
  245.6 2.3 add_reduce_fusion.15
  248.1 2.3 add_reduce_fusion.15
  250.6 2.3 add_reduce_fusion.15
  253.1 2.3 add_reduce_fusion.15
  255.6 2.3 add_reduce_fusion.15
  258.2 2.3 add_reduce_fusion.15
  260.7 2.3 add_reduce_fusion.15
  263.2 2.3 add_reduce_fusion.15
  265.7 2.3 add_reduce_fusion.15
  268.2 2.3 add_reduce_fusion.15
  270.7 2.3 add_reduce_fusion.15
  273.1 17.6 %all_to_all.37 = f32[128,6,128]{2,1,0:T(8,128)S(1)} all-to-all(f32[128,6,128]{2,1,0:T(8,128)S(1)} %broadcast_in_dim.93), channel_id=1, replica_groups=mesh['src'=16,'tgt'=8] {'src','tgt'}, dimensions={0} | all-to-all | bytes 786432 | tf_op jit(solution)/shard_map/all_to_all | solution.py:84
  290.7 4.9 %copy.74 = f32[6,128,128]{0,2,1:T(8,128)} copy(f32[6,128,128]{2,0,1:T(8,128)S(1)} %bitcast.164) | data formatting | bytes 786432 | tf_op jit(solution)/shard_map/transpose | solution.py:85
  295.6 6.2 %gather_fusion.3 = f32[1024,6]{1,0:T(8,128)S(1)} fusion(f32[6,16384]{0,1:T(8,128)} %bitcast.157, s32[1024]{0:T(1024)S(1)} %broadcast_clamp_fusion), kind=kCustom, calls=%fused_computation.3 | custom fusion | bytes 53248 | tf_op jit(solution)/shard_map/gather | solution.py:132
  301.8 6.2 %gather_fusion.2 = f32[1024,6]{1,0:T(8,128)S(1)} fusion(f32[6,16384]{0,1:T(8,128)} %bitcast.158, s32[1024]{0:T(1024)S(1)} %broadcast_clamp_fusion.1), kind=kCustom, calls=%fused_computation.2 | custom fusion | bytes 53248 | tf_op jit(solution)/shard_map/gather | solution.py:131
  (244 shorter events, 38.7 us)
Async XLA Ops:
  5.5 51.5 %copy-start = (f32[3,128]{1,0:T(4,128)S(1)}, f32[3,128]{1,0:T(4,128)}, u32[]{:S(2)}) copy-start(f32[3,128]{1,0:T(4,128)} %param.11) | copy-start | bytes 4612
  27.3 110.6 %copy-start.5 = (f32[2]{0:T(128)S(1)}, f32[2]{0:T(128)}, u32[]{:S(2)}) copy-start(f32[2]{0:T(128)} %param.17) | copy-start | bytes 28
  57.7 15.8 %all-to-all-start = ((f32[128,3,128]{2,1,0:T(4,128)}), f32[128,3,128]{2,1,0:T(4,128)S(1)}, u32[]{:S(2)}, u32[]{:S(2)}) async-start(f32[128,3,128]{2,1,0:T(4,128)} %broadcast_in_dim.89), calls=%async_computation | async-start | bytes 524288 | tf_op jit(solution)/shard_map/all_to_all | solution.py:84
  74.4 17.3 %all-to-all-start.2 = ((f32[128,6,128]{2,1,0:T(8,128)}), f32[128,6,128]{2,1,0:T(8,128)S(1)}, u32[]{:S(2)}, u32[]{:S(2)}) async-start(f32[128,6,128]{2,1,0:T(8,128)} %broadcast_in_dim.90), calls=%async_computation.2 | async-start | bytes 1048576 | tf_op jit(solution)/shard_map/all_to_all | solution.py:84
  91.6 76.3 %copy-start.2 = (f32[1024]{0:T(1024)S(1)}, f32[1024]{0:T(1024)}, u32[]{:S(2)}) copy-start(f32[1024]{0:T(1024)} %param.15) | copy-start | bytes 12292
  91.7 76.3 %copy-start.3 = (f32[1024]{0:T(1024)S(1)}, f32[1024]{0:T(1024)}, u32[]{:S(2)}) copy-start(f32[1024]{0:T(1024)} %param.16) | copy-start | bytes 12292
  91.7 76.4 %copy-start.4 = (f32[1024]{0:T(1024)S(1)}, f32[1024]{0:T(1024)}, u32[]{:S(2)}) copy-start(f32[1024]{0:T(1024)} %param.14) | copy-start | bytes 12292
  132.5 17.8 %all-to-all-start.3 = ((f32[128,6,128]{2,1,0:T(8,128)}), f32[128,6,128]{2,1,0:T(8,128)S(1)}, u32[]{:S(2)}, u32[]{:S(2)}) async-start(f32[128,6,128]{2,1,0:T(8,128)} %broadcast_in_dim.91), calls=%async_computation.3 | async-start | bytes 1048576 | tf_op jit(solution)/shard_map/all_to_all | solution.py:84
  215.0 17.8 %all-to-all-start.5 = ((f32[128,6,128]{2,1,0:T(8,128)}), f32[128,6,128]{2,1,0:T(8,128)S(1)}, u32[]{:S(2)}, u32[]{:S(2)}) async-start(f32[128,6,128]{2,1,0:T(8,128)} %broadcast_in_dim.92), calls=%async_computation.5 | async-start | bytes 1048576 | tf_op jit(solution)/shard_map/all_to_all | solution.py:84
  273.1 36.5 %copy-start.1 = (f32[6,128]{1,0:T(8,128)}, f32[6,128]{1,0:T(8,128)S(1)}, u32[]{:S(2)}) copy-start(f32[6,128]{1,0:T(8,128)S(1)} %get-tuple-element.219) | copy-start | bytes 9220

commit v2 on v1

--- a/solution.py
+++ b/solution.py
@@ -103,16 +103,27 @@
     all_pos = gather_all(positions, devices)
     target_ids = me * own_rows + jnp.arange(own_rows, dtype=jnp.int32)
     first_rows, second_rows = contact_rows(contact_frame)
+    contacts = contact_bodies.shape[1]
+    end_bodies = jnp.concatenate([contact_bodies[0], contact_bodies[1]])
+    end_rows = jnp.concatenate([first_rows, second_rows], axis=1).T
+    owner_hot = (
+        (end_bodies // own_rows)[:, None] == jnp.arange(devices, dtype=jnp.int32)[None, :]
+    ).astype(jnp.float32)
+    slot_hot = (
+        (end_bodies % own_rows)[:, None] == jnp.arange(own_rows, dtype=jnp.int32)[None, :]
+    ).astype(jnp.float32)
+    exact = lax.Precision.HIGHEST
     current = impulse_now
     shifted = impulse_now + MOMENTUM * (impulse_now - impulse_prev)
     own_velocity = jnp.zeros((6, own_rows), jnp.float32)
     block = min(SOURCE_BLOCK, body_count)
     blocks = body_count // block
     for k in range(ITERS):
-        forces = jnp.zeros((6, body_count), jnp.float32)
-        forces = forces.at[:, contact_bodies[0]].add(first_rows * shifted[None, :])
-        forces = forces.at[:, contact_bodies[1]].add(second_rows * shifted[None, :])
-        own_forces = scatter_sum(forces, devices)
+        end_force = end_rows * jnp.concatenate([shifted, shifted])[:, None]
+        spread = (owner_hot[:, :, None] * end_force[:, None, :]).reshape(2 * contacts, devices * 6)
+        pieces = jnp.dot(spread.T, slot_hot, precision=exact).reshape(devices, 6, own_rows)
+        pieces = lax.all_to_all(pieces, AXES, 0, 0, tiled=True)
+        own_forces = jnp.sum(pieces, 0)
         all_forces = gather_all(own_forces, devices)
 
         def one_block(block_index, running_sum):
@@ -127,10 +138,12 @@
         own_velocity = lax.fori_loop(
             0, blocks, one_block, jnp.zeros((6, own_rows), jnp.float32)
         )
-        gathered = gather_all(own_velocity, devices)
-        normal_rate = jnp.sum(first_rows * gathered[:, contact_bodies[0]], 0) + jnp.sum(
-            second_rows * gathered[:, contact_bodies[1]], 0
-        )
+        every = jnp.broadcast_to(own_velocity[None], (devices, 6, own_rows))
+        every = lax.all_to_all(every, AXES, 0, 0, tiled=True).reshape(devices, 6 * own_rows)
+        picked = jnp.dot(owner_hot, every, precision=exact).reshape(2 * contacts, 6, own_rows)
+        end_velocity = jnp.sum(picked * slot_hot[:, None, :], 2)
+        end_rate = jnp.sum(end_rows * end_velocity, 1)
+        normal_rate = end_rate[:contacts] + end_rate[contacts:]
         updated = jnp.maximum(shifted - step_sizes[k] * (gaps + normal_rate), 0.0)
         shifted = updated + MOMENTUM * (updated - current)
         current = updated

time: 311 us -> 291 us (0.936)
  other arithmetic: 124 us -> 88.1 us
  matrix products: 0 us -> 27.2 us
  local copies, waits for them, and re-layouts: 56 us -> 44.8 us
    scatter-add x4 -> x0, other arithmetic: 43.5 us -> none  [the longest x2 24 us: per_device(): forces = forces.at[:, contact_bodies[1]].add(second_rows * shifted[None, :])]
    dot_general x0 -> x4, matrix products: none -> 27.2 us  [the longest x2 19.7 us: per_device(): jnp.dot(spread.T, slot_hot, precision=exact).reshape(devices, 6, own_rows)]
    gather x4 -> x0, local copies, waits for them, and re-layouts: 24.8 us -> none  [the longest x2 12.4 us: per_device(): gathered[:, contact_bodies[0]]]
    dot_general x0 -> x4, local copies, waits for them, and re-layouts: none -> 16.2 us  [per_device(): jnp.dot(spread.T, slot_hot, precision=exact).reshape(devices, 6, own_rows)]
    mul x4 -> x2, local copies, waits for them, and re-layouts: 0.88 us -> 16.5 us  [per_device(): owner_hot[:, :, None] * end_force[:, None, :]]
    all_to_all x4 -> x3, waiting for transfers between devices: 48.5 us -> 36.8 us  [gather_all(): spread = lax.all_to_all(spread, AXES, 0, 0, tiled=True)]
    reshape x2 -> x0, local copies, waits for them, and re-layouts: 11 us -> none  [scatter_sum(): pieces = full.reshape(rows, devices, width).transpose(1, 0, 2)]
    all_to_all x0 -> x1, waiting for transfers between devices: none -> 10.8 us  [per_device(): lax.all_to_all(every, AXES, 0, 0, tiled=True).reshape(devices, 6 * own_rows)]
  transfers between devices with their start and end apart: 4 -> 4, of which waited for: 4 -> 4; matrix products, arithmetic and copies ran while one was open for 0% -> 1% of each run, Pallas kernels for 0% -> 0%
where the time goes in v2:
time: 291 us; the launch traced here: 289 us
  other arithmetic  88.1 us (30%)
  blocking collectives  59.4 us (20%)
  waiting for transfers between devices  47.6 us (16%)
  local copies, waits for them, and re-layouts  44.8 us (15%)
  matrix products  27.2 us (9%)
  starting transfers between devices  19 us (7%)
    reduce_sum x32, other arithmetic, pair_block(): jnp.sum(spin_z, 0)  72.5 us
    all_to_all x2, blocking collectives, per_device(): pieces = lax.all_to_all(pieces, AXES, 0, 0, tiled=True)  41.8 us
    all_to_all x3, waiting for transfers between devices, gather_all(): spread = lax.all_to_all(spread, AXES, 0, 0, tiled=True)  36.8 us
    dot_general x2, matrix products, per_device(): jnp.dot(spread.T, slot_hot, precision=exact).reshape(devices, 6, own_rows)  19.7 us
    all_to_all x1, blocking collectives, per_device(): lax.all_to_all(every, AXES, 0, 0, tiled=True).reshape(devices, 6 * own_rows)  17.6 us
    mul x2, local copies, waits for them, and re-layouts, per_device(): owner_hot[:, :, None] * end_force[:, None, :]  16.5 us
    dot_general x4, local copies, waits for them, and re-layouts, per_device(): jnp.dot(spread.T, slot_hot, precision=exact).reshape(devices, 6, own_rows)  16.2 us
    all_to_all x3, starting transfers between devices, gather_all(): spread = lax.all_to_all(spread, AXES, 0, 0, tiled=True)  14.1 us
  transfers between devices with their start and end apart: 4, of which 4 were waited for; matrix products, arithmetic and copies ran while one was open for 1% of the time, Pallas kernels for 0%

profile of v2, /device:TPU:1, one launch (start us, length us, event | category | flops | bytes accessed | tf_op | source)
XLA Modules:
  0.0 289.2 jit_solution(15515256464023259207)
XLA Ops:
  5.7 4.3 %broadcast_multiply_fusion.1 = f32[2048,128,6]{0,2,1:T(8,128)} fusion(f32[2048,6]{0,1:T(8,128)S(1)} %broadcast_multiply_fusion.3, f32[2048,128]{0,1:T(8,128)S(1)} %copy.32), kind=kLoop, calls=%fused_computation.77 | loop fusion | flops 1572864 | bytes 7389184 | tf_op jit(solution)/shard_map/mul | solution.py:123
  10.0 8.3 %mul.1289 = f32[2048,768]{0,1:T(8,128)} reshape(f32[2048,128,6]{0,2,1:T(8,128)} %broadcast_multiply_fusion.1) | data formatting | bytes 12582912 | tf_op jit(solution)/shard_map/mul | solution.py:123
  18.2 7.9 %dot_general.29 = f32[128,6,2048]{2,1,0:T(8,128)} reshape(f32[768,2048]{1,0:T(8,128)} %bitcast.157) | data formatting | bytes 12582912 | tf_op jit(solution)/shard_map/dot_general | solution.py:124
  26.1 9.8 %fusion.18 = f32[128,6,128]{2,0,1:T(8,128)S(1)} fusion(f32[128,6,2048]{2,1,0:T(8,128)} %dot_general.29, s32[2048]{0:T(1024)S(1)} %get-tuple-element.351), kind=kOutput, calls=%fused_computation.72 | convolution fusion | flops 2416181248 | bytes 6692864 | tf_op jit(solution)/shard_map/dot_general | solution.py:124
  36.2 24.2 %all_to_all.35 = f32[128,6,128]{2,1,0:T(8,128)S(1)} all-to-all(f32[128,6,128]{2,1,0:T(8,128)S(1)} %copy.34), channel_id=1, replica_groups=mesh['src'=16,'tgt'=8] {'src','tgt'}, dimensions={0} | all-to-all | bytes 786432 | tf_op jit(solution)/shard_map/all_to_all | solution.py:125
  61.1 4.9 %all-to-all-start = ((f32[128,3,128]{2,1,0:T(4,128)}), f32[128,3,128]{2,1,0:T(4,128)S(1)}, u32[]{:S(2)}, u32[]{:S(2)}) async-start(f32[128,3,128]{2,1,0:T(4,128)} %broadcast_in_dim.89), calls=%async_computation | async-start | bytes 524288 | tf_op jit(solution)/shard_map/all_to_all | solution.py:84
  66.2 10.8 %all-to-all-done = f32[128,3,128]{2,1,0:T(4,128)S(1)} async-done(((f32[128,3,128]{2,1,0:T(4,128)}), f32[128,3,128]{2,1,0:T(4,128)S(1)}, u32[]{:S(2)}, u32[]{:S(2)}) %all-to-all-start) | async-done | bytes 196640 | tf_op jit(solution)/shard_map/all_to_all | solution.py:84
  77.8 4.2 %all-to-all-start.2 = ((f32[128,6,128]{2,1,0:T(8,128)}), f32[128,6,128]{2,1,0:T(8,128)S(1)}, u32[]{:S(2)}, u32[]{:S(2)}) async-start(f32[128,6,128]{2,1,0:T(8,128)} %broadcast_in_dim.90), calls=%async_computation.2 | async-start | bytes 1048576 | tf_op jit(solution)/shard_map/all_to_all | solution.py:84
  82.0 13.0 %all-to-all-done.2 = f32[128,6,128]{2,1,0:T(8,128)S(1)} async-done(((f32[128,6,128]{2,1,0:T(8,128)}), f32[128,6,128]{2,1,0:T(8,128)S(1)}, u32[]{:S(2)}, u32[]{:S(2)}) %all-to-all-start.2) | async-done | bytes 393248 | tf_op jit(solution)/shard_map/all_to_all | solution.py:84
  95.1 40.3 %while.28 = (s32[]{:T(128)}, f32[6,128]{1,0:T(8,128)S(1)}, f32[3,128]{1,0:T(4,128)S(1)}, f32[3,16384]{1,0:T(4,128)S(1)}, f32[6,16384]{1,0:T(8,128)S(1)}, /*index...) while((s32[]{:T(128)}, f32[6,128]{1,0:T(8,128)S(1)}, ...), condition=%wide.region_8.9_spmd.clone, body=%wide.region_1.8_spmd.clone.sunk | while | flops 12846988 | bytes 143137 | solution.py:138
  95.2 2.3 add_reduce_fusion.14
  97.8 2.3 add_reduce_fusion.14
  100.3 2.3 add_reduce_fusion.14
  102.8 2.3 add_reduce_fusion.14
  105.3 2.3 add_reduce_fusion.14
  107.8 2.3 add_reduce_fusion.14
  110.4 2.3 add_reduce_fusion.14
  112.9 2.3 add_reduce_fusion.14
  115.4 2.3 add_reduce_fusion.14
  117.9 2.3 add_reduce_fusion.14
  120.4 2.3 add_reduce_fusion.14
  122.9 2.3 add_reduce_fusion.14
  125.5 2.3 add_reduce_fusion.14
  128.0 2.3 add_reduce_fusion.14
  130.5 2.3 add_reduce_fusion.14
  133.0 2.3 add_reduce_fusion.14
  136.2 4.9 %all-to-all-start.3 = ((f32[128,6,128]{2,1,0:T(8,128)}), f32[128,6,128]{2,1,0:T(8,128)S(1)}, u32[]{:S(2)}, u32[]{:S(2)}) async-start(f32[128,6,128]{2,1,0:T(8,128)} %broadcast_in_dim.91), calls=%async_computation.3 | async-start | bytes 1048576 | tf_op jit(solution)/shard_map/all_to_all | solution.py:142
  143.4 10.8 %all-to-all-done.3 = f32[128,6,128]{2,1,0:T(8,128)S(1)} async-done(((f32[128,6,128]{2,1,0:T(8,128)}), f32[128,6,128]{2,1,0:T(8,128)S(1)}, u32[]{:S(2)}, u32[]{:S(2)}) %all-to-all-start.3) | async-done | bytes 393248 | tf_op jit(solution)/shard_map/all_to_all | solution.py:142
  154.3 4.3 %multiply_reduce_fusion.1 = f32[2048,6]{0,1:T(8,128)S(1)} fusion(f32[2048,128]{0,1:T(8,128)} %copy.36, s32[2048]{0:T(1024)S(1)} %get-tuple-element.350, f32[128,6,128]{0,2,1:T(8,128)S(1)} %copy.35), kind=kOutput, calls=%fused_computation.75 | convolution fusion | flops 2419314688 | bytes 1499136 | tf_op jit(solution)/shard_map/dot_general | solution.py:143
  159.4 4.3 %broadcast_multiply_fusion = f32[2048,128,6]{0,2,1:T(8,128)} fusion(f32[2048,6]{0,1:T(8,128)S(1)} %broadcast_multiply_fusion.2, f32[2048,128]{0,1:T(8,128)S(1)} %copy.32), kind=kLoop, calls=%fused_computation.76 | loop fusion | flops 1572864 | bytes 7389184 | tf_op jit(solution)/shard_map/mul | solution.py:123
  163.7 8.3 %mul.1300 = f32[2048,768]{0,1:T(8,128)} reshape(f32[2048,128,6]{0,2,1:T(8,128)} %broadcast_multiply_fusion) | data formatting | bytes 12582912 | tf_op jit(solution)/shard_map/mul | solution.py:123
  171.9 7.8 %dot_general.35 = f32[128,6,2048]{2,1,0:T(8,128)} reshape(f32[768,2048]{1,0:T(8,128)} %bitcast.158) | data formatting | bytes 12582912 | tf_op jit(solution)/shard_map/dot_general | solution.py:124
  179.8 9.9 %fusion.16 = f32[128,6,128]{2,0,1:T(8,128)S(1)} fusion(f32[128,6,2048]{2,1,0:T(8,128)} %dot_general.35, s32[2048]{0:T(1024)S(1)} %get-tuple-element.351), kind=kOutput, calls=%fused_computation.70 | convolution fusion | flops 2416181248 | bytes 6692864 | tf_op jit(solution)/shard_map/dot_general | solution.py:124
  189.9 17.6 %all_to_all.36 = f32[128,6,128]{2,1,0:T(8,128)S(1)} all-to-all(f32[128,6,128]{2,1,0:T(8,128)S(1)} %copy.38), channel_id=1, replica_groups=mesh['src'=16,'tgt'=8] {'src','tgt'}, dimensions={0} | all-to-all | bytes 786432 | tf_op jit(solution)/shard_map/all_to_all | solution.py:125
  208.5 5.0 %all-to-all-start.5 = ((f32[128,6,128]{2,1,0:T(8,128)}), f32[128,6,128]{2,1,0:T(8,128)S(1)}, u32[]{:S(2)}, u32[]{:S(2)}) async-start(f32[128,6,128]{2,1,0:T(8,128)} %broadcast_in_dim.92), calls=%async_computation.5 | async-start | bytes 1048576 | tf_op jit(solution)/shard_map/all_to_all | solution.py:84
  213.5 13.0 %all-to-all-done.5 = f32[128,6,128]{2,1,0:T(8,128)S(1)} async-done(((f32[128,6,128]{2,1,0:T(8,128)}), f32[128,6,128]{2,1,0:T(8,128)S(1)}, u32[]{:S(2)}, u32[]{:S(2)}) %all-to-all-start.5) | async-done | bytes 393248 | tf_op jit(solution)/shard_map/all_to_all | solution.py:84
  226.5 40.2 %while.29 = (s32[]{:T(128)}, f32[6,128]{1,0:T(8,128)S(1)}, f32[3,128]{1,0:T(4,128)S(1)}, f32[3,16384]{1,0:T(4,128)S(1)}, f32[6,16384]{1,0:T(8,128)S(1)}, /*index...) while((s32[]{:T(128)}, f32[6,128]{1,0:T(8,128)S(1)}, ...), condition=%wide.region_19.20_spmd.clone, body=%wide.region_12.19_spmd.clone.sunk | while | flops 12846988 | bytes 143137 | solution.py:138
  226.7 2.3 add_reduce_fusion.15
  229.2 2.3 add_reduce_fusion.15
  231.7 2.3 add_reduce_fusion.15
  234.3 2.3 add_reduce_fusion.15
  236.8 2.3 add_reduce_fusion.15
  239.3 2.3 add_reduce_fusion.15
  241.8 2.3 add_reduce_fusion.15
  249.4 2.3 add_reduce_fusion.15
  251.9 2.3 add_reduce_fusion.15
  266.8 17.6 %all_to_all.37 = f32[128,6,128]{2,1,0:T(8,128)S(1)} all-to-all(f32[128,6,128]{2,1,0:T(8,128)S(1)} %broadcast_in_dim.93), channel_id=1, replica_groups=mesh['src'=16,'tgt'=8] {'src','tgt'}, dimensions={0} | all-to-all | bytes 786432 | tf_op jit(solution)/shard_map/all_to_all | solution.py:142
  284.7 3.2 %multiply_reduce_fusion = f32[2048,6]{0,1:T(8,128)S(1)} fusion(f32[2048,128]{0,1:T(8,128)S(1)} %copy-done, s32[2048]{0:T(1024)S(1)} %get-tuple-element.350, f32[128,6,128]{0,2,1:T(8,128)S(1)} %copy.39), kind=kOutput, calls=%fused_computation.74 | convolution fusion | flops 2419314688 | bytes 1499136 | tf_op jit(solution)/shard_map/dot_general | solution.py:143
  (245 shorter events, 35.5 us)
Async XLA Ops:
  18.2 42.1 %copy-start.1 = (f32[3,128]{1,0:T(4,128)S(1)}, f32[3,128]{1,0:T(4,128)}, u32[]{:S(2)}) copy-start(f32[3,128]{1,0:T(4,128)} %param.11) | copy-start | bytes 4612
  26.1 116.7 %copy-start.6 = (f32[2]{0:T(128)S(1)}, f32[2]{0:T(128)}, u32[]{:S(2)}) copy-start(f32[2]{0:T(128)} %param.17) | copy-start | bytes 28
  60.4 98.3 %copy-start.3 = (f32[1024]{0:T(1024)S(1)}, f32[1024]{0:T(1024)}, u32[]{:S(2)}) copy-start(f32[1024]{0:T(1024)} %param.15) | copy-start | bytes 12292
  60.4 98.3 %copy-start.4 = (f32[1024]{0:T(1024)S(1)}, f32[1024]{0:T(1024)}, u32[]{:S(2)}) copy-start(f32[1024]{0:T(1024)} %param.16) | copy-start | bytes 12292
  60.4 98.3 %copy-start.5 = (f32[1024]{0:T(1024)S(1)}, f32[1024]{0:T(1024)}, u32[]{:S(2)}) copy-start(f32[1024]{0:T(1024)} %param.14) | copy-start | bytes 12292
  61.1 15.8 %all-to-all-start = ((f32[128,3,128]{2,1,0:T(4,128)}), f32[128,3,128]{2,1,0:T(4,128)S(1)}, u32[]{:S(2)}, u32[]{:S(2)}) async-start(f32[128,3,128]{2,1,0:T(4,128)} %broadcast_in_dim.89), calls=%async_computation | async-start | bytes 524288 | tf_op jit(solution)/shard_map/all_to_all | solution.py:84
  77.8 17.3 %all-to-all-start.2 = ((f32[128,6,128]{2,1,0:T(8,128)}), f32[128,6,128]{2,1,0:T(8,128)S(1)}, u32[]{:S(2)}, u32[]{:S(2)}) async-start(f32[128,6,128]{2,1,0:T(8,128)} %broadcast_in_dim.90), calls=%async_computation.2 | async-start | bytes 1048576 | tf_op jit(solution)/shard_map/all_to_all | solution.py:84
  136.2 18.0 %all-to-all-start.3 = ((f32[128,6,128]{2,1,0:T(8,128)}), f32[128,6,128]{2,1,0:T(8,128)S(1)}, u32[]{:S(2)}, u32[]{:S(2)}) async-start(f32[128,6,128]{2,1,0:T(8,128)} %broadcast_in_dim.91), calls=%async_computation.3 | async-start | bytes 1048576 | tf_op jit(solution)/shard_map/all_to_all | solution.py:142
  179.8 104.9 %copy-start = (f32[2048,128]{0,1:T(8,128)S(1)}, f32[2048,128]{0,1:T(8,128)}, u32[]{:S(2)}) copy-start(f32[2048,128]{0,1:T(8,128)} %copy.36) | copy-start | bytes 3145732
  208.5 18.0 %all-to-all-start.5 = ((f32[128,6,128]{2,1,0:T(8,128)}), f32[128,6,128]{2,1,0:T(8,128)S(1)}, u32[]{:S(2)}, u32[]{:S(2)}) async-start(f32[128,6,128]{2,1,0:T(8,128)} %broadcast_in_dim.92), calls=%async_computation.5 | async-start | bytes 1048576 | tf_op jit(solution)/shard_map/all_to_all | solution.py:84
  266.8 22.4 %copy-start.2 = (f32[6,128]{1,0:T(8,128)}, f32[6,128]{1,0:T(8,128)S(1)}, u32[]{:S(2)}) copy-start(f32[6,128]{1,0:T(8,128)S(1)} %get-tuple-element.219) | copy-start | bytes 9220

commit v3 on v1

--- a/solution.py
+++ b/solution.py
@@ -1,6 +1,7 @@
 import jax
 import jax.numpy as jnp
 from jax import lax
+from jax.experimental import pallas as pl
 from jax.sharding import PartitionSpec as P
 
 ITERS = 2
@@ -78,6 +79,67 @@
     )
 
 
+def split_three(value):
+    high = lax.reduce_precision(value, exponent_bits=8, mantissa_bits=7)
+    rest = value - high
+    middle = lax.reduce_precision(rest, exponent_bits=8, mantissa_bits=7)
+    low = rest - middle
+    return jnp.stack([high, middle, low]).astype(jnp.bfloat16)
+
+
+def scatter_kernel(owner_ref, slot_ref, parts_ref, out_ref):
+    slots = slot_ref.shape[0]
+    owner = owner_ref[...]
+    slot = slot_ref[...]
+    for k in range(6):
+        total = None
+        for p in range(3):
+            weighted = slot * parts_ref[p, k : k + 1, :]
+            term = lax.dot_general(
+                owner, weighted, (((1,), (1,)), ((), ())), preferred_element_type=jnp.float32
+            )
+            total = term if total is None else total + term
+        out_ref[:, k * slots : (k + 1) * slots] = total
+
+
+def gather_kernel(owner_ref, slot_ref, parts_ref, out_ref):
+    slots = slot_ref.shape[0]
+    owner = owner_ref[...]
+    slot = slot_ref[...].astype(jnp.float32)
+    for k in range(6):
+        picked = None
+        for p in range(3):
+            part = parts_ref[p, k * slots : (k + 1) * slots, :]
+            term = jnp.dot(part, owner, preferred_element_type=jnp.float32)
+            picked = term if picked is None else picked + term
+        out_ref[k : k + 1, :] = jnp.sum(picked * slot, axis=0, keepdims=True)
+
+
+def scatter_forces(owner_t, slot_t, end_force):
+    owners, ends = owner_t.shape
+    slots = slot_t.shape[0]
+    parts = split_three(end_force)
+    return pl.pallas_call(
+        scatter_kernel,
+        out_shape=jax.ShapeDtypeStruct((owners, 6 * slots), jnp.float32),
+        cost_estimate=pl.CostEstimate(
+            flops=2 * 18 * owners * slots * ends, transcendentals=0, bytes_accessed=4 * ends * 300
+        ),
+    )(owner_t, slot_t, parts)
+
+
+def gather_velocity(owner_t, slot_t, table):
+    owners, ends = owner_t.shape
+    slots = slot_t.shape[0]
+    return pl.pallas_call(
+        gather_kernel,
+        out_shape=jax.ShapeDtypeStruct((6, ends), jnp.float32),
+        cost_estimate=pl.CostEstimate(
+            flops=2 * 18 * owners * slots * ends, transcendentals=0, bytes_accessed=4 * ends * 300
+        ),
+    )(owner_t, slot_t, split_three(table))
+
+
 def gather_all(block, devices):
     rows, width = block.shape
     spread = jnp.broadcast_to(block[None], (devices, rows, width))
@@ -103,16 +165,25 @@
     all_pos = gather_all(positions, devices)
     target_ids = me * own_rows + jnp.arange(own_rows, dtype=jnp.int32)
     first_rows, second_rows = contact_rows(contact_frame)
+    contacts = contact_bodies.shape[1]
+    end_bodies = jnp.concatenate([contact_bodies[0], contact_bodies[1]])
+    end_rows = jnp.concatenate([first_rows, second_rows], axis=1)
+    owner_t = (
+        jnp.arange(devices, dtype=jnp.int32)[:, None] == (end_bodies // own_rows)[None, :]
+    ).astype(jnp.bfloat16)
+    slot_t = (
+        jnp.arange(own_rows, dtype=jnp.int32)[:, None] == (end_bodies % own_rows)[None, :]
+    ).astype(jnp.bfloat16)
     current = impulse_now
     shifted = impulse_now + MOMENTUM * (impulse_now - impulse_prev)
     own_velocity = jnp.zeros((6, own_rows), jnp.float32)
     block = min(SOURCE_BLOCK, body_count)
     blocks = body_count // block
     for k in range(ITERS):
-        forces = jnp.zeros((6, body_count), jnp.float32)
-        forces = forces.at[:, contact_bodies[0]].add(first_rows * shifted[None, :])
-        forces = forces.at[:, contact_bodies[1]].add(second_rows * shifted[None, :])
-        own_forces = scatter_sum(forces, devices)
+        end_force = end_rows * jnp.concatenate([shifted, shifted])[None, :]
+        pieces = scatter_forces(owner_t, slot_t, end_force)
+        pieces = lax.all_to_all(pieces, AXES, 0, 0, tiled=True)
+        own_forces = jnp.sum(pieces, 0).reshape(6, own_rows)
         all_forces = gather_all(own_forces, devices)
 
         def one_block(block_index, running_sum):
@@ -127,10 +198,11 @@
         own_velocity = lax.fori_loop(
             0, blocks, one_block, jnp.zeros((6, own_rows), jnp.float32)
         )
-        gathered = gather_all(own_velocity, devices)
-        normal_rate = jnp.sum(first_rows * gathered[:, contact_bodies[0]], 0) + jnp.sum(
-            second_rows * gathered[:, contact_bodies[1]], 0
-        )
+        every = jnp.broadcast_to(own_velocity.reshape(1, 6 * own_rows), (devices, 6 * own_rows))
+        every = lax.all_to_all(every, AXES, 0, 0, tiled=True)
+        end_velocity = gather_velocity(owner_t, slot_t, every.T)
+        end_rate = jnp.sum(end_rows * end_velocity, 0)
+        normal_rate = end_rate[:contacts] + end_rate[contacts:]
         updated = jnp.maximum(shifted - step_sizes[k] * (gaps + normal_rate), 0.0)
         shifted = updated + MOMENTUM * (updated - current)
         current = updated

time: 311 us -> 243 us (0.78)
  local copies, waits for them, and re-layouts: 56 us -> 14.2 us
  other arithmetic: 124 us -> 84.4 us
  Pallas kernels: 0 us -> 18.3 us
  blocking collectives: 59.4 us -> 56.1 us
    scatter-add x4 -> x0, other arithmetic: 43.5 us -> none  [the longest x2 24 us: per_device(): forces = forces.at[:, contact_bodies[1]].add(second_rows * shifted[None, :])]
    gather x4 -> x0, local copies, waits for them, and re-layouts: 24.8 us -> none  [the longest x2 12.4 us: per_device(): gathered[:, contact_bodies[0]]]
    pallas_call x0 -> x4, Pallas kernels: none -> 18.3 us  [the longest x2 9.22 us: gather_velocity(): pl.pallas_call(gather_kernel, out_shape=jax.ShapeDtypeStruct((6, ends), j...]
    all_to_all x4 -> x3, waiting for transfers between devices: 48.5 us -> 36.8 us  [gather_all(): spread = lax.all_to_all(spread, AXES, 0, 0, tiled=True)]
    all_to_all x0 -> x1, waiting for transfers between devices: none -> 11.4 us  [per_device(): every = lax.all_to_all(every, AXES, 0, 0, tiled=True)]
    reshape x2 -> x0, local copies, waits for them, and re-layouts: 11 us -> none  [scatter_sum(): pieces = full.reshape(rows, devices, width).transpose(1, 0, 2)]
    transpose x2 -> x0, local copies, waits for them, and re-layouts: 9.7 us -> none  [gather_all(): return spread.transpose(1, 0, 2).reshape(rows, devices * width)]
    all_to_all x4 -> x3, starting transfers between devices: 18.9 us -> 13.3 us  [gather_all(): spread = lax.all_to_all(spread, AXES, 0, 0, tiled=True)]
where the time goes in v3:
time: 243 us; the launch traced here: 242 us
  other arithmetic  84.4 us (35%)
  blocking collectives  56.1 us (23%)
  waiting for transfers between devices  48.2 us (20%)
  Pallas kernels  18.3 us (8%)
  starting transfers between devices  18.2 us (7%)
  local copies, waits for them, and re-layouts  14.2 us (6%)
    reduce_sum x32, other arithmetic, pair_block(): jnp.sum(spin_z, 0)  72.2 us
    all_to_all x2, blocking collectives, per_device(): pieces = lax.all_to_all(pieces, AXES, 0, 0, tiled=True)  39.4 us
    all_to_all x3, waiting for transfers between devices, gather_all(): spread = lax.all_to_all(spread, AXES, 0, 0, tiled=True)  36.8 us
    all_to_all x1, blocking collectives, per_device(): every = lax.all_to_all(every, AXES, 0, 0, tiled=True)  16.6 us
    all_to_all x3, starting transfers between devices, gather_all(): spread = lax.all_to_all(spread, AXES, 0, 0, tiled=True)  13.3 us
    all_to_all x1, waiting for transfers between devices, per_device(): every = lax.all_to_all(every, AXES, 0, 0, tiled=True)  11.4 us
    pallas_call x2, Pallas kernels, gather_velocity(): pl.pallas_call(gather_kernel, out_shape=jax.ShapeDtypeStruct((6, ends), j...  9.22 us
    pallas_call x2, Pallas kernels, scatter_forces(): pl.pallas_call(scatter_kernel, out_shape=jax.ShapeDtypeStruct((owners, 6...  9.09 us
  transfers between devices with their start and end apart: 4, of which 4 were waited for; matrix products, arithmetic and copies ran while one was open for 0% of the time, Pallas kernels for 0%

profile of v3, /device:TPU:1, one launch (start us, length us, event | category | flops | bytes accessed | tf_op | source)
XLA Modules:
  0.0 242.4 jit_solution(10213472207062376516)
XLA Ops:
  6.2 4.5 %shard_map.86 = f32[128,768]{1,0:T(8,128)} custom-call(bf16[128,2048]{1,0:T(8,128)(2,1)} %get-tuple-element.368.owner_ref, bf16[128,2048]{1,0:T(8,128)(2,1)} %get-tuple-element.369.slot_ref, bf16[3,6,2048]{2,1,0:T(8,128)(2,1)} %pad_maximum_fusion.2.parts_ref), custom_call_target="tpu_custom_call" | custom-call | flops 1207959552 | bytes 2457600 | tf_op jit(solution)/shard_map/pallas_call | solution.py:122
  12.1 23.2 %all_to_all.51 = f32[128,1,768]{2,1,0:T(1,128)S(1)} all-to-all(f32[128,1,768]{2,1,0:T(1,128)S(1)} %copy.13), channel_id=1, replica_groups=mesh['src'=16,'tgt'=8] {'src','tgt'}, dimensions={0} | all-to-all | bytes 786432 | tf_op jit(solution)/shard_map/all_to_all | solution.py:185
  36.1 4.5 %all-to-all-start = ((f32[128,3,128]{2,1,0:T(4,128)}), f32[128,3,128]{2,1,0:T(4,128)S(1)}, u32[]{:S(2)}, u32[]{:S(2)}) async-start(f32[128,3,128]{2,1,0:T(4,128)} %broadcast_in_dim.87), calls=%async_computation | async-start | bytes 524288 | tf_op jit(solution)/shard_map/all_to_all | solution.py:146
  40.9 10.8 %all-to-all-done = f32[128,3,128]{2,1,0:T(4,128)S(1)} async-done(((f32[128,3,128]{2,1,0:T(4,128)}), f32[128,3,128]{2,1,0:T(4,128)S(1)}, u32[]{:S(2)}, u32[]{:S(2)}) %all-to-all-start) | async-done | bytes 196640 | tf_op jit(solution)/shard_map/all_to_all | solution.py:146
  52.5 4.2 %all-to-all-start.2 = ((f32[128,6,128]{2,1,0:T(8,128)}), f32[128,6,128]{2,1,0:T(8,128)S(1)}, u32[]{:S(2)}, u32[]{:S(2)}) async-start(f32[128,6,128]{2,1,0:T(8,128)} %broadcast_in_dim.89), calls=%async_computation.2 | async-start | bytes 1048576 | tf_op jit(solution)/shard_map/all_to_all | solution.py:146
  56.7 13.0 %all-to-all-done.2 = f32[128,6,128]{2,1,0:T(8,128)S(1)} async-done(((f32[128,6,128]{2,1,0:T(8,128)}), f32[128,6,128]{2,1,0:T(8,128)S(1)}, u32[]{:S(2)}, u32[]{:S(2)}) %all-to-all-start.2) | async-done | bytes 393248 | tf_op jit(solution)/shard_map/all_to_all | solution.py:146
  69.8 40.1 %while.28 = (s32[]{:T(128)}, f32[6,128]{1,0:T(8,128)S(1)}, f32[3,128]{1,0:T(4,128)S(1)}, f32[3,16384]{1,0:T(4,128)S(1)}, f32[6,16384]{1,0:T(8,128)S(1)}, /*index...) while((s32[]{:T(128)}, f32[6,128]{1,0:T(8,128)S(1)}, ...), condition=%wide.region_8.9_spmd.clone, body=%wide.region_1.8_spmd.clone.sunk | while | flops 12846988 | bytes 143137 | solution.py:198
  69.9 2.3 add_reduce_fusion.14
  72.5 2.3 add_reduce_fusion.14
  75.0 2.3 add_reduce_fusion.14
  77.5 2.3 add_reduce_fusion.14
  80.0 2.3 add_reduce_fusion.14
  82.5 2.3 add_reduce_fusion.14
  85.0 2.3 add_reduce_fusion.14
  87.5 2.3 add_reduce_fusion.14
  90.0 2.3 add_reduce_fusion.14
  92.5 2.3 add_reduce_fusion.14
  95.1 2.3 add_reduce_fusion.14
  97.6 2.3 add_reduce_fusion.14
  100.1 2.3 add_reduce_fusion.14
  102.6 2.3 add_reduce_fusion.14
  105.1 2.3 add_reduce_fusion.14
  107.6 2.3 add_reduce_fusion.14
  110.9 4.9 %all-to-all-start.3 = ((f32[128,1,768]{2,1,0:T(1,128)}), f32[128,1,768]{2,1,0:T(1,128)S(1)}, u32[]{:S(2)}, u32[]{:S(2)}) async-start(f32[128,1,768]{2,1,0:T(1,128)} %broadcast_in_dim.91), calls=%async_computation.3 | async-start | bytes 786432 | tf_op jit(solution)/shard_map/all_to_all | solution.py:202
  116.4 11.4 %all-to-all-done.3 = f32[128,1,768]{2,1,0:T(1,128)S(1)} async-done(((f32[128,1,768]{2,1,0:T(1,128)}), f32[128,1,768]{2,1,0:T(1,128)S(1)}, u32[]{:S(2)}, u32[]{:S(2)}) %all-to-all-start.3) | async-done | bytes 393248 | tf_op jit(solution)/shard_map/all_to_all | solution.py:202
  129.2 4.6 %shard_map.87 = f32[6,2048]{1,0:T(8,128)} custom-call(bf16[128,2048]{1,0:T(8,128)(2,1)} %get-tuple-element.368.owner_ref, bf16[128,2048]{1,0:T(8,128)(2,1)} %get-tuple-element.369.slot_ref, bf16[3,768,128]{2,1,0:T(8,128)(2,1)} %pad_maximum_fusion.parts_ref), custom_call_target="tpu_custom_call" | custom-call | flops 1207959552 | bytes 2457600 | tf_op jit(solution)/shard_map/pallas_call | solution.py:134
  136.1 4.5 %shard_map.88 = f32[128,768]{1,0:T(8,128)} custom-call(bf16[128,2048]{1,0:T(8,128)(2,1)} %get-tuple-element.368.owner_ref, bf16[128,2048]{1,0:T(8,128)(2,1)} %get-tuple-element.369.slot_ref, bf16[3,6,2048]{2,1,0:T(8,128)(2,1)} %pad_maximum_fusion.3.parts_ref), custom_call_target="tpu_custom_call" | custom-call | flops 1207959552 | bytes 2457600 | tf_op jit(solution)/shard_map/pallas_call | solution.py:122
  142.0 16.2 %all_to_all.52 = f32[128,1,768]{2,1,0:T(1,128)S(1)} all-to-all(f32[128,1,768]{2,1,0:T(1,128)S(1)} %copy.15), channel_id=1, replica_groups=mesh['src'=16,'tgt'=8] {'src','tgt'}, dimensions={0} | all-to-all | bytes 786432 | tf_op jit(solution)/shard_map/all_to_all | solution.py:185
  159.4 4.5 %all-to-all-start.5 = ((f32[128,6,128]{2,1,0:T(8,128)}), f32[128,6,128]{2,1,0:T(8,128)S(1)}, u32[]{:S(2)}, u32[]{:S(2)}) async-start(f32[128,6,128]{2,1,0:T(8,128)} %broadcast_in_dim.93), calls=%async_computation.5 | async-start | bytes 1048576 | tf_op jit(solution)/shard_map/all_to_all | solution.py:146
  163.9 13.0 %all-to-all-done.5 = f32[128,6,128]{2,1,0:T(8,128)S(1)} async-done(((f32[128,6,128]{2,1,0:T(8,128)}), f32[128,6,128]{2,1,0:T(8,128)S(1)}, u32[]{:S(2)}, u32[]{:S(2)}) %all-to-all-start.5) | async-done | bytes 393248 | tf_op jit(solution)/shard_map/all_to_all | solution.py:146
  176.9 40.1 %while.29 = (s32[]{:T(128)}, f32[6,128]{1,0:T(8,128)S(1)}, f32[3,128]{1,0:T(4,128)S(1)}, f32[3,16384]{1,0:T(4,128)S(1)}, f32[6,16384]{1,0:T(8,128)S(1)}, /*index...) while((s32[]{:T(128)}, f32[6,128]{1,0:T(8,128)S(1)}, ...), condition=%wide.region_18.19_spmd.clone, body=%wide.region_11.18_spmd.clone.sunk | while | flops 12846988 | bytes 143137 | solution.py:198
  177.1 2.3 add_reduce_fusion.15
  179.6 2.3 add_reduce_fusion.15
  182.1 2.3 add_reduce_fusion.15
  184.6 2.3 add_reduce_fusion.15
  187.1 2.3 add_reduce_fusion.15
  189.6 2.3 add_reduce_fusion.15
  192.1 2.3 add_reduce_fusion.15
  194.7 2.3 add_reduce_fusion.15
  197.2 2.3 add_reduce_fusion.15
  199.7 2.3 add_reduce_fusion.15
  202.2 2.3 add_reduce_fusion.15
  204.7 2.3 add_reduce_fusion.15
  207.2 2.3 add_reduce_fusion.15
  209.7 2.3 add_reduce_fusion.15
  212.2 2.3 add_reduce_fusion.15
  217.6 16.6 %all_to_all.53 = f32[128,1,768]{2,1,0:T(1,128)S(1)} all-to-all(f32[128,1,768]{2,1,0:T(1,128)S(1)} %broadcast_in_dim.95), channel_id=1, replica_groups=mesh['src'=16,'tgt'=8] {'src','tgt'}, dimensions={0} | all-to-all | bytes 786432 | tf_op jit(solution)/shard_map/all_to_all | solution.py:202
  235.6 4.6 %shard_map.89 = f32[6,2048]{1,0:T(8,128)} custom-call(bf16[128,2048]{1,0:T(8,128)(2,1)} %get-tuple-element.368.owner_ref, bf16[128,2048]{1,0:T(8,128)(2,1)} %get-tuple-element.369.slot_ref, bf16[3,768,128]{2,1,0:T(8,128)(2,1)} %pad_maximum_fusion.1.parts_ref), custom_call_target="tpu_custom_call" | custom-call | flops 1207959552 | bytes 2457600 | tf_op jit(solution)/shard_map/pallas_call | solution.py:134
  (244 shorter events, 28.7 us)
Async XLA Ops:
  2.5 1.0 copy-start.2
  2.5 1.0 copy-start.3
  3.5 0.7 copy-start.5
  12.1 23.2 %copy-start = (f32[3,128]{1,0:T(4,128)S(1)}, f32[3,128]{1,0:T(4,128)}, u32[]{:S(2)}) copy-start(f32[3,128]{1,0:T(4,128)} %param.11) | copy-start | bytes 4612
  36.1 15.6 %all-to-all-start = ((f32[128,3,128]{2,1,0:T(4,128)}), f32[128,3,128]{2,1,0:T(4,128)S(1)}, u32[]{:S(2)}, u32[]{:S(2)}) async-start(f32[128,3,128]{2,1,0:T(4,128)} %broadcast_in_dim.87), calls=%async_computation | async-start | bytes 524288 | tf_op jit(solution)/shard_map/all_to_all | solution.py:146
  52.5 17.3 %all-to-all-start.2 = ((f32[128,6,128]{2,1,0:T(8,128)}), f32[128,6,128]{2,1,0:T(8,128)S(1)}, u32[]{:S(2)}, u32[]{:S(2)}) async-start(f32[128,6,128]{2,1,0:T(8,128)} %broadcast_in_dim.89), calls=%async_computation.2 | async-start | bytes 1048576 | tf_op jit(solution)/shard_map/all_to_all | solution.py:146
  110.9 4.9 %copy-start.6 = (f32[2]{0:T(128)S(1)}, f32[2]{0:T(128)}, u32[]{:S(2)}) copy-start(f32[2]{0:T(128)} %param.17) | copy-start | bytes 28
  110.9 17.0 %all-to-all-start.3 = ((f32[128,1,768]{2,1,0:T(1,128)}), f32[128,1,768]{2,1,0:T(1,128)S(1)}, u32[]{:S(2)}, u32[]{:S(2)}) async-start(f32[128,1,768]{2,1,0:T(1,128)} %broadcast_in_dim.91), calls=%async_computation.3 | async-start | bytes 786432 | tf_op jit(solution)/shard_map/all_to_all | solution.py:202
  133.8 0.9 copy-start.4
  159.4 17.6 %all-to-all-start.5 = ((f32[128,6,128]{2,1,0:T(8,128)}), f32[128,6,128]{2,1,0:T(8,128)S(1)}, u32[]{:S(2)}, u32[]{:S(2)}) async-start(f32[128,6,128]{2,1,0:T(8,128)} %broadcast_in_dim.93), calls=%async_computation.5 | async-start | bytes 1048576 | tf_op jit(solution)/shard_map/all_to_all | solution.py:146
  217.0 0.6 copy-start.1

commit v4 on v3

--- a/solution.py
+++ b/solution.py
@@ -162,7 +162,6 @@
     me = lax.axis_index("src") * lax.axis_size("tgt") + lax.axis_index("tgt")
     own_rows = positions.shape[1]
     body_count = own_rows * devices
-    all_pos = gather_all(positions, devices)
     target_ids = me * own_rows + jnp.arange(own_rows, dtype=jnp.int32)
     first_rows, second_rows = contact_rows(contact_frame)
     contacts = contact_bodies.shape[1]
@@ -184,7 +183,11 @@
         pieces = scatter_forces(owner_t, slot_t, end_force)
         pieces = lax.all_to_all(pieces, AXES, 0, 0, tiled=True)
         own_forces = jnp.sum(pieces, 0).reshape(6, own_rows)
-        all_forces = gather_all(own_forces, devices)
+        if k == 0:
+            both = gather_all(jnp.concatenate([own_forces, positions]), devices)
+            all_forces, all_pos = both[:6], both[6:]
+        else:
+            all_forces = gather_all(own_forces, devices)
 
         def one_block(block_index, running_sum):
             start = block_index * block

time: 243 us -> 234 us (0.963)
  waiting for transfers between devices: 48.2 us -> 43 us
  starting transfers between devices: 18.2 us -> 14 us
    all_to_all x3 -> x2, waiting for transfers between devices: 36.8 us -> 31.6 us  [gather_all(): spread = lax.all_to_all(spread, AXES, 0, 0, tiled=True)]
    all_to_all x3 -> x2, starting transfers between devices: 13.3 us -> 9.03 us  [gather_all(): spread = lax.all_to_all(spread, AXES, 0, 0, tiled=True)]
  transfers between devices with their start and end apart: 4 -> 3, of which waited for: 4 -> 3; matrix products, arithmetic and copies ran while one was open for 0% -> 0% of each run, Pallas kernels for 0% -> 0%
where the time goes in v4:
time: 234 us; the launch traced here: 233 us
  other arithmetic  84.5 us (36%)
  blocking collectives  56.1 us (24%)
  waiting for transfers between devices  43 us (18%)
  Pallas kernels  18.3 us (8%)
  local copies, waits for them, and re-layouts  14.2 us (6%)
  starting transfers between devices  14 us (6%)
    reduce_sum x32, other arithmetic, pair_block(): jnp.sum(spin_z, 0)  72.2 us
    all_to_all x2, blocking collectives, per_device(): pieces = lax.all_to_all(pieces, AXES, 0, 0, tiled=True)  39.4 us
    all_to_all x2, waiting for transfers between devices, gather_all(): spread = lax.all_to_all(spread, AXES, 0, 0, tiled=True)  31.6 us
    all_to_all x1, blocking collectives, per_device(): every = lax.all_to_all(every, AXES, 0, 0, tiled=True)  16.6 us
    all_to_all x1, waiting for transfers between devices, per_device(): every = lax.all_to_all(every, AXES, 0, 0, tiled=True)  11.4 us
    pallas_call x2, Pallas kernels, gather_velocity(): pl.pallas_call(gather_kernel, out_shape=jax.ShapeDtypeStruct((6, ends), j...  9.21 us
    pallas_call x2, Pallas kernels, scatter_forces(): pl.pallas_call(scatter_kernel, out_shape=jax.ShapeDtypeStruct((owners, 6...  9.09 us
    all_to_all x2, starting transfers between devices, gather_all(): spread = lax.all_to_all(spread, AXES, 0, 0, tiled=True)  9.03 us
  transfers between devices with their start and end apart: 3, of which 3 were waited for; matrix products, arithmetic and copies ran while one was open for 0% of the time, Pallas kernels for 0%

profile of v4, /device:TPU:1, one launch (start us, length us, event | category | flops | bytes accessed | tf_op | source)
XLA Modules:
  0.0 233.1 jit_solution(15376670912359873269)
XLA Ops:
  6.2 4.5 %shard_map.86 = f32[128,768]{1,0:T(8,128)} custom-call(bf16[128,2048]{1,0:T(8,128)(2,1)} %get-tuple-element.368.owner_ref, bf16[128,2048]{1,0:T(8,128)(2,1)} %get-tuple-element.369.slot_ref, bf16[3,6,2048]{2,1,0:T(8,128)(2,1)} %pad_maximum_fusion.2.parts_ref), custom_call_target="tpu_custom_call" | custom-call | flops 1207959552 | bytes 2457600 | tf_op jit(solution)/shard_map/pallas_call | solution.py:122
  10.8 1.4 copy.13
  12.2 23.2 %all_to_all.46 = f32[128,1,768]{2,1,0:T(1,128)S(1)} all-to-all(f32[128,1,768]{2,1,0:T(1,128)S(1)} %copy.13), channel_id=1, replica_groups=mesh['src'=16,'tgt'=8] {'src','tgt'}, dimensions={0} | all-to-all | bytes 786432 | tf_op jit(solution)/shard_map/all_to_all | solution.py:184
  37.1 4.5 %all-to-all-start.1 = ((f32[128,9,128]{2,1,0:T(8,128)}), f32[128,9,128]{2,1,0:T(8,128)S(1)}, u32[]{:S(2)}, u32[]{:S(2)}) async-start(f32[128,9,128]{2,1,0:T(8,128)} %broadcast_in_dim.80), calls=%async_computation.1 | async-start | bytes 2097152 | tf_op jit(solution)/shard_map/all_to_all | solution.py:146
  41.7 18.5 %all-to-all-done.1 = f32[128,9,128]{2,1,0:T(8,128)S(1)} async-done(((f32[128,9,128]{2,1,0:T(8,128)}), f32[128,9,128]{2,1,0:T(8,128)S(1)}, u32[]{:S(2)}, u32[]{:S(2)}) %all-to-all-start.1) | async-done | bytes 589856 | tf_op jit(solution)/shard_map/all_to_all | solution.py:146
  60.3 40.2 %while.28 = (s32[]{:T(128)}, f32[6,128]{1,0:T(8,128)S(1)}, f32[3,128]{1,0:T(4,128)S(1)}, f32[3,16384]{1,0:T(4,128)S(1)}, f32[6,16384]{1,0:T(8,128)S(1)}, /*index...) while((s32[]{:T(128)}, f32[6,128]{1,0:T(8,128)S(1)}, ...), condition=%wide.region_8.9_spmd.clone, body=%wide.region_1.8_spmd.clone.sunk | while | flops 12846988 | bytes 143137 | solution.py:201
  60.5 2.3 add_reduce_fusion.14
  63.0 2.3 add_reduce_fusion.14
  65.6 2.3 add_reduce_fusion.14
  68.1 2.3 add_reduce_fusion.14
  70.6 2.3 add_reduce_fusion.14
  73.1 2.3 add_reduce_fusion.14
  75.6 2.3 add_reduce_fusion.14
  78.1 2.3 add_reduce_fusion.14
  80.6 2.3 add_reduce_fusion.14
  83.1 2.3 add_reduce_fusion.14
  85.6 2.3 add_reduce_fusion.14
  88.2 2.3 add_reduce_fusion.14
  90.7 2.3 add_reduce_fusion.14
  93.2 2.3 add_reduce_fusion.14
  95.7 2.3 add_reduce_fusion.14
  98.2 2.3 add_reduce_fusion.14
  101.5 5.0 %all-to-all-start.2 = ((f32[128,1,768]{2,1,0:T(1,128)}), f32[128,1,768]{2,1,0:T(1,128)S(1)}, u32[]{:S(2)}, u32[]{:S(2)}) async-start(f32[128,1,768]{2,1,0:T(1,128)} %broadcast_in_dim.82), calls=%async_computation.2 | async-start | bytes 786432 | tf_op jit(solution)/shard_map/all_to_all | solution.py:205
  107.1 11.4 %all-to-all-done.2 = f32[128,1,768]{2,1,0:T(1,128)S(1)} async-done(((f32[128,1,768]{2,1,0:T(1,128)}), f32[128,1,768]{2,1,0:T(1,128)S(1)}, u32[]{:S(2)}, u32[]{:S(2)}) %all-to-all-start.2) | async-done | bytes 393248 | tf_op jit(solution)/shard_map/all_to_all | solution.py:205
  119.9 4.6 %shard_map.87 = f32[6,2048]{1,0:T(8,128)} custom-call(bf16[128,2048]{1,0:T(8,128)(2,1)} %get-tuple-element.368.owner_ref, bf16[128,2048]{1,0:T(8,128)(2,1)} %get-tuple-element.369.slot_ref, bf16[3,768,128]{2,1,0:T(8,128)(2,1)} %pad_maximum_fusion.parts_ref), custom_call_target="tpu_custom_call" | custom-call | flops 1207959552 | bytes 2457600 | tf_op jit(solution)/shard_map/pallas_call | solution.py:134
  126.8 4.5 %shard_map.88 = f32[128,768]{1,0:T(8,128)} custom-call(bf16[128,2048]{1,0:T(8,128)(2,1)} %get-tuple-element.368.owner_ref, bf16[128,2048]{1,0:T(8,128)(2,1)} %get-tuple-element.369.slot_ref, bf16[3,6,2048]{2,1,0:T(8,128)(2,1)} %pad_maximum_fusion.3.parts_ref), custom_call_target="tpu_custom_call" | custom-call | flops 1207959552 | bytes 2457600 | tf_op jit(solution)/shard_map/pallas_call | solution.py:122
  132.7 16.2 %all_to_all.47 = f32[128,1,768]{2,1,0:T(1,128)S(1)} all-to-all(f32[128,1,768]{2,1,0:T(1,128)S(1)} %copy.15), channel_id=1, replica_groups=mesh['src'=16,'tgt'=8] {'src','tgt'}, dimensions={0} | all-to-all | bytes 786432 | tf_op jit(solution)/shard_map/all_to_all | solution.py:184
  150.0 4.5 %all-to-all-start.4 = ((f32[128,6,128]{2,1,0:T(8,128)}), f32[128,6,128]{2,1,0:T(8,128)S(1)}, u32[]{:S(2)}, u32[]{:S(2)}) async-start(f32[128,6,128]{2,1,0:T(8,128)} %broadcast_in_dim.84), calls=%async_computation.4 | async-start | bytes 1048576 | tf_op jit(solution)/shard_map/all_to_all | solution.py:146
  154.6 13.0 %all-to-all-done.4 = f32[128,6,128]{2,1,0:T(8,128)S(1)} async-done(((f32[128,6,128]{2,1,0:T(8,128)}), f32[128,6,128]{2,1,0:T(8,128)S(1)}, u32[]{:S(2)}, u32[]{:S(2)}) %all-to-all-start.4) | async-done | bytes 393248 | tf_op jit(solution)/shard_map/all_to_all | solution.py:146
  167.6 40.2 %while.29 = (s32[]{:T(128)}, f32[6,128]{1,0:T(8,128)S(1)}, f32[3,128]{1,0:T(4,128)S(1)}, f32[3,16384]{1,0:T(4,128)S(1)}, f32[6,16384]{1,0:T(8,128)S(1)}, /*index...) while((s32[]{:T(128)}, f32[6,128]{1,0:T(8,128)S(1)}, ...), condition=%wide.region_18.19_spmd.clone, body=%wide.region_11.18_spmd.clone.sunk | while | flops 12846988 | bytes 143137 | solution.py:201
  167.8 2.3 add_reduce_fusion.15
  170.3 2.3 add_reduce_fusion.15
  172.8 2.3 add_reduce_fusion.15
  175.3 2.3 add_reduce_fusion.15
  177.8 2.3 add_reduce_fusion.15
  180.3 2.3 add_reduce_fusion.15
  182.8 2.3 add_reduce_fusion.15
  185.4 2.3 add_reduce_fusion.15
  187.9 2.3 add_reduce_fusion.15
  190.4 2.3 add_reduce_fusion.15
  192.9 2.3 add_reduce_fusion.15
  195.4 2.3 add_reduce_fusion.15
  197.9 2.3 add_reduce_fusion.15
  200.4 2.3 add_reduce_fusion.15
  202.9 2.3 add_reduce_fusion.15
  205.4 2.3 add_reduce_fusion.15
  208.4 16.6 %all_to_all.48 = f32[128,1,768]{2,1,0:T(1,128)S(1)} all-to-all(f32[128,1,768]{2,1,0:T(1,128)S(1)} %broadcast_in_dim.86), channel_id=1, replica_groups=mesh['src'=16,'tgt'=8] {'src','tgt'}, dimensions={0} | all-to-all | bytes 786432 | tf_op jit(solution)/shard_map/all_to_all | solution.py:205
  226.4 4.6 %shard_map.89 = f32[6,2048]{1,0:T(8,128)} custom-call(bf16[128,2048]{1,0:T(8,128)(2,1)} %get-tuple-element.368.owner_ref, bf16[128,2048]{1,0:T(8,128)(2,1)} %get-tuple-element.369.slot_ref, bf16[3,768,128]{2,1,0:T(8,128)(2,1)} %pad_maximum_fusion.1.parts_ref), custom_call_target="tpu_custom_call" | custom-call | flops 1207959552 | bytes 2457600 | tf_op jit(solution)/shard_map/pallas_call | solution.py:134
  (244 shorter events, 25.1 us)
Async XLA Ops:
  2.5 1.0 copy-start.2
  2.5 1.0 copy-start.3
  3.5 0.7 copy-start.5
  35.4 0.7 copy-start
  37.1 23.1 %all-to-all-start.1 = ((f32[128,9,128]{2,1,0:T(8,128)}), f32[128,9,128]{2,1,0:T(8,128)S(1)}, u32[]{:S(2)}, u32[]{:S(2)}) async-start(f32[128,9,128]{2,1,0:T(8,128)} %broadcast_in_dim.80), calls=%async_computation.1 | async-start | bytes 2097152 | tf_op jit(solution)/shard_map/all_to_all | solution.py:146
  101.5 5.0 %copy-start.6 = (f32[2]{0:T(128)S(1)}, f32[2]{0:T(128)}, u32[]{:S(2)}) copy-start(f32[2]{0:T(128)} %param.17) | copy-start | bytes 28
  101.5 17.1 %all-to-all-start.2 = ((f32[128,1,768]{2,1,0:T(1,128)}), f32[128,1,768]{2,1,0:T(1,128)S(1)}, u32[]{:S(2)}, u32[]{:S(2)}) async-start(f32[128,1,768]{2,1,0:T(1,128)} %broadcast_in_dim.82), calls=%async_computation.2 | async-start | bytes 786432 | tf_op jit(solution)/shard_map/all_to_all | solution.py:205
  124.5 0.9 copy-start.4
  150.0 17.6 %all-to-all-start.4 = ((f32[128,6,128]{2,1,0:T(8,128)}), f32[128,6,128]{2,1,0:T(8,128)S(1)}, u32[]{:S(2)}, u32[]{:S(2)}) async-start(f32[128,6,128]{2,1,0:T(8,128)} %broadcast_in_dim.84), calls=%async_computation.4 | async-start | bytes 1048576 | tf_op jit(solution)/shard_map/all_to_all | solution.py:146
  207.8 0.6 copy-start.1

commit v5 on v4

--- a/solution.py
+++ b/solution.py
@@ -140,6 +140,75 @@
     )(owner_t, slot_t, split_three(table))
 
 
+def pair_kernel(target_ref, place_ref, force_ref, out_ref):
+    targets = target_ref.shape[1]
+    chunks = place_ref.shape[1] // 128
+
+    def group(g, carry):
+        rows = pl.ds(pl.multiple_of(g * 8, 8), 8)
+        target_x = target_ref[0, rows, :]
+        target_y = target_ref[1, rows, :]
+        target_z = target_ref[2, rows, :]
+
+        def chunk(j, sums):
+            lanes = pl.ds(pl.multiple_of(j * 128, 128), 128)
+            place = place_ref[:, lanes]
+            force = force_ref[:, lanes]
+            r_x = target_x - place[0:1]
+            r_y = target_y - place[1:2]
+            r_z = target_z - place[2:3]
+            f_x, f_y, f_z = force[0:1], force[1:2], force[2:3]
+            t_x, t_y, t_z = force[3:4], force[4:5], force[5:6]
+            dist_sq = r_x * r_x + r_y * r_y + r_z * r_z
+            inverse = jnp.where(dist_sq > 0.0, lax.rsqrt(dist_sq), 0.0)
+            inverse_sq = inverse * inverse
+            inverse_cube = inverse_sq * inverse
+            inverse_fifth = inverse_cube * inverse_sq
+            c_cross = 0.75 * inverse_cube
+            c_iso = 0.75 * inverse + 0.5 * inverse_cube
+            c_dyad = c_cross - 1.5 * inverse_fifth
+            c_spin = 1.125 * inverse_fifth
+            c_self = 0.375 * inverse_cube
+            dyad = c_dyad * (r_x * f_x + r_y * f_y + r_z * f_z)
+            spin = c_spin * (r_x * t_x + r_y * t_y + r_z * t_z)
+            s_x = c_cross * r_x
+            s_y = c_cross * r_y
+            s_z = c_cross * r_z
+            return (
+                sums[0] + (c_iso * f_x + dyad * r_x + (t_y * s_z - t_z * s_y)),
+                sums[1] + (c_iso * f_y + dyad * r_y + (t_z * s_x - t_x * s_z)),
+                sums[2] + (c_iso * f_z + dyad * r_z + (t_x * s_y - t_y * s_x)),
+                sums[3] + ((f_y * s_z - f_z * s_y) + spin * r_x - c_self * t_x),
+                sums[4] + ((f_z * s_x - f_x * s_z) + spin * r_y - c_self * t_y),
+                sums[5] + ((f_x * s_y - f_y * s_x) + spin * r_z - c_self * t_z),
+            )
+
+        zero = jnp.zeros((8, 128), jnp.float32)
+        sums = lax.fori_loop(0, chunks, chunk, (zero,) * 6, unroll=2)
+        for k in range(6):
+            out_ref[k, rows, :] = sums[k]
+        return carry
+
+    lax.fori_loop(0, targets // 8, group, 0)
+
+
+def mobility_own(positions, all_pos, all_forces, own_forces):
+    own_rows = positions.shape[1]
+    sources = all_pos.shape[1]
+    spread = jnp.broadcast_to(positions[:, :, None], (3, own_rows, 128))
+    partial = pl.pallas_call(
+        pair_kernel,
+        out_shape=jax.ShapeDtypeStruct((6, own_rows, 128), jnp.float32),
+        cost_estimate=pl.CostEstimate(
+            flops=90 * own_rows * sources,
+            transcendentals=own_rows * sources,
+            bytes_accessed=4 * (9 * sources + 9 * own_rows * 128),
+        ),
+    )(spread, all_pos, all_forces)
+    self_scale = jnp.array([1.0, 1.0, 1.0, 0.75, 0.75, 0.75], jnp.float32)[:, None]
+    return jnp.sum(partial, 2) + self_scale * own_forces
+
+
 def gather_all(block, devices):
     rows, width = block.shape
     spread = jnp.broadcast_to(block[None], (devices, rows, width))
@@ -162,7 +231,6 @@
     me = lax.axis_index("src") * lax.axis_size("tgt") + lax.axis_index("tgt")
     own_rows = positions.shape[1]
     body_count = own_rows * devices
-    target_ids = me * own_rows + jnp.arange(own_rows, dtype=jnp.int32)
     first_rows, second_rows = contact_rows(contact_frame)
     contacts = contact_bodies.shape[1]
     end_bodies = jnp.concatenate([contact_bodies[0], contact_bodies[1]])
@@ -176,8 +244,6 @@
     current = impulse_now
     shifted = impulse_now + MOMENTUM * (impulse_now - impulse_prev)
     own_velocity = jnp.zeros((6, own_rows), jnp.float32)
-    block = min(SOURCE_BLOCK, body_count)
-    blocks = body_count // block
     for k in range(ITERS):
         end_force = end_rows * jnp.concatenate([shifted, shifted])[None, :]
         pieces = scatter_forces(owner_t, slot_t, end_force)
@@ -189,18 +255,7 @@
         else:
             all_forces = gather_all(own_forces, devices)
 
-        def one_block(block_index, running_sum):
-            start = block_index * block
-            force_block = lax.dynamic_slice_in_dim(all_forces, start, block, 1)
-            place_block = lax.dynamic_slice_in_dim(all_pos, start, block, 1)
-            ids_block = start + jnp.arange(block, dtype=jnp.int32)
-            return running_sum + pair_block(
-                positions, target_ids, place_block, ids_block, force_block
-            )
-
-        own_velocity = lax.fori_loop(
-            0, blocks, one_block, jnp.zeros((6, own_rows), jnp.float32)
-        )
+        own_velocity = mobility_own(positions, all_pos, all_forces, own_forces)
         every = jnp.broadcast_to(own_velocity.reshape(1, 6 * own_rows), (devices, 6 * own_rows))
         every = lax.all_to_all(every, AXES, 0, 0, tiled=True)
         end_velocity = gather_velocity(owner_t, slot_t, every.T)

time: 234 us -> 231 us (0.987)
  Pallas kernels: 18.3 us -> 92.5 us
  other arithmetic: 84.5 us -> 14.9 us
  blocking collectives: 56.1 us -> 79.7 us
  waiting for transfers between devices: 43 us -> 22.6 us
  local copies, waits for them, and re-layouts: 14.2 us -> 9.76 us
  starting transfers between devices: 14 us -> 9.9 us
    pallas_call x0 -> x2, Pallas kernels: none -> 74.1 us  [mobility_own(): pl.pallas_call(pair_kernel, out_shape=jax.ShapeDtypeStruct((6, own_rows,...]
    reduce_sum x32 -> x2, other arithmetic: 72.2 us -> 2.35 us  [mobility_own(): return jnp.sum(partial, 2) + self_scale * own_forces]
    all_to_all x2 -> x0, waiting for transfers between devices: 31.6 us -> none  [gather_all(): spread = lax.all_to_all(spread, AXES, 0, 0, tiled=True)]
    all_to_all x1 -> x2, blocking collectives: 16.6 us -> 40.3 us  [gather_all(): spread = lax.all_to_all(spread, AXES, 0, 0, tiled=True)]
    all_to_all x1 -> x2, waiting for transfers between devices: 11.4 us -> 22.6 us  [per_device(): every = lax.all_to_all(every, AXES, 0, 0, tiled=True)]
    all_to_all x2 -> x0, starting transfers between devices: 9.03 us -> none  [gather_all(): spread = lax.all_to_all(spread, AXES, 0, 0, tiled=True)]
    all_to_all x1 -> x2, starting transfers between devices: 5.01 us -> 9.9 us  [per_device(): every = lax.all_to_all(every, AXES, 0, 0, tiled=True)]
    slice x32 -> x0, local copies, waits for them, and re-layouts: 4.49 us -> none  [pair_block(): delta_x = target_pos[0][None, :] - source_pos[0][:, None]]
  transfers between devices with their start and end apart: 3 -> 2, of which waited for: 3 -> 2; matrix products, arithmetic and copies ran while one was open for 0% -> 1% of each run, Pallas kernels for 0% -> 0%
where the time goes in v5:
time: 231 us; the launch traced here: 230 us
  Pallas kernels  92.5 us (40%)
  blocking collectives  79.7 us (35%)
  waiting for transfers between devices  22.6 us (10%)
  other arithmetic  14.9 us (6%)
  starting transfers between devices  9.9 us (4%)
  local copies, waits for them, and re-layouts  9.76 us (4%)
    pallas_call x2, Pallas kernels, mobility_own(): pl.pallas_call(pair_kernel, out_shape=jax.ShapeDtypeStruct((6, own_rows,...  74.1 us
    all_to_all x2, blocking collectives, gather_all(): spread = lax.all_to_all(spread, AXES, 0, 0, tiled=True)  40.3 us
    all_to_all x2, blocking collectives, per_device(): pieces = lax.all_to_all(pieces, AXES, 0, 0, tiled=True)  39.4 us
    all_to_all x2, waiting for transfers between devices, per_device(): every = lax.all_to_all(every, AXES, 0, 0, tiled=True)  22.6 us
    all_to_all x2, starting transfers between devices, per_device(): every = lax.all_to_all(every, AXES, 0, 0, tiled=True)  9.9 us
    pallas_call x2, Pallas kernels, gather_velocity(): pl.pallas_call(gather_kernel, out_shape=jax.ShapeDtypeStruct((6, ends), j...  9.22 us
    pallas_call x2, Pallas kernels, scatter_forces(): pl.pallas_call(scatter_kernel, out_shape=jax.ShapeDtypeStruct((owners, 6...  9.14 us
  transfers between devices with their start and end apart: 2, of which 2 were waited for; matrix products, arithmetic and copies ran while one was open for 1% of the time, Pallas kernels for 0%

profile of v5, /device:TPU:1, one launch (start us, length us, event | category | flops | bytes accessed | tf_op | source)
XLA Modules:
  0.0 230.2 jit_solution(15376360806917891916)
XLA Ops:
  0.6 1.1 multiply_subtract_fusion.5
  1.7 0.8 slice_negate_fusion
  2.5 1.0 multiply_subtract_fusion.2
  3.5 0.7 copy-done.4
  4.2 1.2 fusion
  5.5 0.7 pad_maximum_fusion.2.parts_ref
  6.2 4.6 %shard_map.104 = f32[128,768]{1,0:T(8,128)} custom-call(bf16[128,2048]{1,0:T(8,128)(2,1)} %get-tuple-element.28.owner_ref, bf16[128,2048]{1,0:T(8,128)(2,1)} %get-tuple-element.29.slot_ref, bf16[3,6,2048]{2,1,0:T(8,128)(2,1)} %pad_maximum_fusion.2.parts_ref), custom_call_target="tpu_custom_call" | custom-call | flops 1207959552 | bytes 2457600 | tf_op jit(solution)/shard_map/pallas_call | solution.py:122
  10.7 1.4 copy.11
  12.1 23.2 %all_to_all.46 = f32[128,1,768]{2,1,0:T(1,128)S(1)} all-to-all(f32[128,1,768]{2,1,0:T(1,128)S(1)} %copy.11), channel_id=1, replica_groups=mesh['src'=16,'tgt'=8] {'src','tgt'}, dimensions={0} | all-to-all | bytes 786432 | tf_op jit(solution)/shard_map/all_to_all | solution.py:250
  35.4 0.3 reduce_sum.58
  35.6 0.4 copy-done.3
  36.1 0.1 broadcast_in_dim.13
  36.1 22.7 %all_to_all.47 = f32[128,9,128]{2,1,0:T(8,128)S(1)} all-to-all(f32[128,9,128]{2,1,0:T(8,128)S(1)} %broadcast_in_dim.13), channel_id=1, replica_groups=mesh['src'=16,'tgt'=8] {'src','tgt'}, dimensions={0} | all-to-all | bytes 1179648 | tf_op jit(solution)/shard_map/all_to_all | solution.py:215
  58.8 0.8 slice_bitcast_fusion.force_ref
  59.7 0.8 slice_bitcast_fusion.1.place_ref
  60.4 0.8 broadcast_in_dim.12.target_ref
  61.2 37.1 %shard_map.105 = f32[6,128,128]{2,1,0:T(8,128)} custom-call(f32[3,128,128]{2,1,0:T(8,128)} %broadcast_in_dim.12.target_ref, f32[3,16384]{1,0:T(4,128)} %slice_bitcast_fusion.1.place_ref, f32[6,16384]{1,0:T(8,128)} %slice_bitcast_fusion.force_ref), custom_call_target="tpu_custom_call" | custom-call | flops 188743680 | bytes 1179648 | tf_op jit(solution)/shard_map/pallas_call | solution.py:199
  98.3 1.2 reduce_sum.59
  99.5 0.1 fusion.13
  99.6 1.0 broadcast_in_dim.14
  100.5 5.0 %all-to-all-start.2 = ((f32[128,1,768]{2,1,0:T(1,128)}), f32[128,1,768]{2,1,0:T(1,128)S(1)}, u32[]{:S(2)}, u32[]{:S(2)}) async-start(f32[128,1,768]{2,1,0:T(1,128)} %broadcast_in_dim.14), calls=%async_computation.2 | async-start | bytes 786432 | tf_op jit(solution)/shard_map/all_to_all | solution.py:260
  105.5 0.6 fusion.24
  106.2 11.4 %all-to-all-done.2 = f32[128,1,768]{2,1,0:T(1,128)S(1)} async-done(((f32[128,1,768]{2,1,0:T(1,128)}), f32[128,1,768]{2,1,0:T(1,128)S(1)}, u32[]{:S(2)}, u32[]{:S(2)}) %all-to-all-start.2) | async-done | bytes 393248 | tf_op jit(solution)/shard_map/all_to_all | solution.py:260
  117.6 0.4 copy.12
  118.0 0.1 fusion.6
  118.1 0.9 pad_maximum_fusion.parts_ref
  119.0 4.6 %shard_map.106 = f32[6,2048]{1,0:T(8,128)} custom-call(bf16[128,2048]{1,0:T(8,128)(2,1)} %get-tuple-element.28.owner_ref, bf16[128,2048]{1,0:T(8,128)(2,1)} %get-tuple-element.29.slot_ref, bf16[3,768,128]{2,1,0:T(8,128)(2,1)} %pad_maximum_fusion.parts_ref), custom_call_target="tpu_custom_call" | custom-call | flops 1207959552 | bytes 2457600 | tf_op jit(solution)/shard_map/pallas_call | solution.py:134
  123.6 0.9 multiply_reduce_fusion.1
  124.5 0.7 multiply_add_fusion.1
  125.2 0.7 pad_maximum_fusion.3.parts_ref
  125.9 4.6 %shard_map.107 = f32[128,768]{1,0:T(8,128)} custom-call(bf16[128,2048]{1,0:T(8,128)(2,1)} %get-tuple-element.28.owner_ref, bf16[128,2048]{1,0:T(8,128)(2,1)} %get-tuple-element.29.slot_ref, bf16[3,6,2048]{2,1,0:T(8,128)(2,1)} %pad_maximum_fusion.3.parts_ref), custom_call_target="tpu_custom_call" | custom-call | flops 1207959552 | bytes 2457600 | tf_op jit(solution)/shard_map/pallas_call | solution.py:122
  130.4 1.4 copy.13
  131.8 16.2 %all_to_all.48 = f32[128,1,768]{2,1,0:T(1,128)S(1)} all-to-all(f32[128,1,768]{2,1,0:T(1,128)S(1)} %copy.13), channel_id=1, replica_groups=mesh['src'=16,'tgt'=8] {'src','tgt'}, dimensions={0} | all-to-all | bytes 786432 | tf_op jit(solution)/shard_map/all_to_all | solution.py:250
  148.1 0.3 reduce_sum.62
  148.4 17.6 %all_to_all.49 = f32[128,6,128]{2,1,0:T(8,128)} all-to-all(f32[128,6,128]{2,1,0:T(8,128)S(1)} %broadcast_in_dim.16), channel_id=1, replica_groups=mesh['src'=16,'tgt'=8] {'src','tgt'}, dimensions={0} | all-to-all | bytes 786432 | tf_op jit(solution)/shard_map/all_to_all | solution.py:215
  166.0 37.1 %shard_map.108 = f32[6,128,128]{2,1,0:T(8,128)} custom-call(f32[3,128,128]{2,1,0:T(8,128)} %broadcast_in_dim.12.target_ref, f32[3,16384]{1,0:T(4,128)} %slice_bitcast_fusion.1.place_ref, f32[6,16384]{1,0:T(8,128)} %bitcast.76), custom_call_target="tpu_custom_call" | custom-call | flops 188743680 | bytes 1179648 | tf_op jit(solution)/shard_map/pallas_call | solution.py:199
  203.0 1.2 reduce_sum.63
  204.2 0.1 fusion.14
  204.3 1.0 broadcast_in_dim.17
  205.3 4.9 %all-to-all-start.5 = ((f32[128,1,768]{2,1,0:T(1,128)}), f32[128,1,768]{2,1,0:T(1,128)S(1)}, u32[]{:S(2)}, u32[]{:S(2)}) async-start(f32[128,1,768]{2,1,0:T(1,128)} %broadcast_in_dim.17), calls=%async_computation.5 | async-start | bytes 786432 | tf_op jit(solution)/shard_map/all_to_all | solution.py:260
  210.2 0.7 multiply_add_fusion
  210.8 11.3 %all-to-all-done.5 = f32[128,1,768]{2,1,0:T(1,128)S(1)} async-done(((f32[128,1,768]{2,1,0:T(1,128)}), f32[128,1,768]{2,1,0:T(1,128)S(1)}, u32[]{:S(2)}, u32[]{:S(2)}) %all-to-all-start.5) | async-done | bytes 393248 | tf_op jit(solution)/shard_map/all_to_all | solution.py:260
  222.1 0.4 copy.14
  222.5 0.1 fusion.8
  222.6 0.9 pad_maximum_fusion.1.parts_ref
  223.5 4.6 %shard_map.109 = f32[6,2048]{1,0:T(8,128)} custom-call(bf16[128,2048]{1,0:T(8,128)(2,1)} %get-tuple-element.28.owner_ref, bf16[128,2048]{1,0:T(8,128)(2,1)} %get-tuple-element.29.slot_ref, bf16[3,768,128]{2,1,0:T(8,128)(2,1)} %pad_maximum_fusion.1.parts_ref), custom_call_target="tpu_custom_call" | custom-call | flops 1207959552 | bytes 2457600 | tf_op jit(solution)/shard_map/pallas_call | solution.py:134
  228.1 0.9 multiply_reduce_fusion
  229.0 1.2 fusion.18
  (23 shorter events, 0.2 us)
Async XLA Ops:
  2.5 1.0 copy-start
  2.5 1.0 copy-start.1
  3.5 0.7 copy-start.4
  35.4 0.7 copy-start.3
  98.3 1.2 copy-start.5
  100.5 5.0 %copy-start.6 = (f32[2]{0:T(128)S(1)}, f32[2]{0:T(128)}, u32[]{:S(2)}) copy-start(f32[2]{0:T(128)} %param.15) | copy-start | bytes 28
  100.5 17.0 %all-to-all-start.2 = ((f32[128,1,768]{2,1,0:T(1,128)}), f32[128,1,768]{2,1,0:T(1,128)S(1)}, u32[]{:S(2)}, u32[]{:S(2)}) async-start(f32[128,1,768]{2,1,0:T(1,128)} %broadcast_in_dim.14), calls=%async_computation.2 | async-start | bytes 786432 | tf_op jit(solution)/shard_map/all_to_all | solution.py:260
  123.6 0.9 copy-start.2
  205.3 16.8 %all-to-all-start.5 = ((f32[128,1,768]{2,1,0:T(1,128)}), f32[128,1,768]{2,1,0:T(1,128)S(1)}, u32[]{:S(2)}, u32[]{:S(2)}) async-start(f32[128,1,768]{2,1,0:T(1,128)} %broadcast_in_dim.17), calls=%async_computation.5 | async-start | bytes 786432 | tf_op jit(solution)/shard_map/all_to_all | solution.py:260

commit v6 on v5

--- a/solution.py
+++ b/solution.py
@@ -184,7 +184,7 @@
             )
 
         zero = jnp.zeros((8, 128), jnp.float32)
-        sums = lax.fori_loop(0, chunks, chunk, (zero,) * 6, unroll=2)
+        sums = lax.fori_loop(0, chunks, chunk, (zero,) * 6, unroll=32)
         for k in range(6):
             out_ref[k, rows, :] = sums[k]
         return carry

time: 231 us -> 209 us (0.905)
  Pallas kernels: 92.5 us -> 70.3 us
    pallas_call x2, Pallas kernels: 74.1 us -> 51.9 us  [mobility_own(): pl.pallas_call(pair_kernel, out_shape=jax.ShapeDtypeStruct((6, own_rows,...]
where the time goes in v6:
time: 209 us; the launch traced here: 208 us
  blocking collectives  79.7 us (38%)
  Pallas kernels  70.3 us (34%)
  waiting for transfers between devices  22.6 us (11%)
  other arithmetic  14.9 us (7%)
  starting transfers between devices  9.9 us (5%)
  local copies, waits for them, and re-layouts  9.76 us (5%)
    pallas_call x2, Pallas kernels, mobility_own(): pl.pallas_call(pair_kernel, out_shape=jax.ShapeDtypeStruct((6, own_rows,...  51.9 us
    all_to_all x2, blocking collectives, gather_all(): spread = lax.all_to_all(spread, AXES, 0, 0, tiled=True)  40.3 us
    all_to_all x2, blocking collectives, per_device(): pieces = lax.all_to_all(pieces, AXES, 0, 0, tiled=True)  39.4 us
    all_to_all x2, waiting for transfers between devices, per_device(): every = lax.all_to_all(every, AXES, 0, 0, tiled=True)  22.6 us
    all_to_all x2, starting transfers between devices, per_device(): every = lax.all_to_all(every, AXES, 0, 0, tiled=True)  9.9 us
    pallas_call x2, Pallas kernels, gather_velocity(): pl.pallas_call(gather_kernel, out_shape=jax.ShapeDtypeStruct((6, ends), j...  9.22 us
    pallas_call x2, Pallas kernels, scatter_forces(): pl.pallas_call(scatter_kernel, out_shape=jax.ShapeDtypeStruct((owners, 6...  9.14 us
  transfers between devices with their start and end apart: 2, of which 2 were waited for; matrix products, arithmetic and copies ran while one was open for 1% of the time, Pallas kernels for 0%

profile of v6, /device:TPU:1, one launch (start us, length us, event | category | flops | bytes accessed | tf_op | source)
XLA Modules:
  0.0 208.0 jit_solution(14931564118225726036)
XLA Ops:
  0.6 1.1 multiply_subtract_fusion.5
  1.7 0.8 slice_negate_fusion
  2.5 1.0 multiply_subtract_fusion.2
  3.5 0.7 copy-done.4
  4.2 1.2 fusion
  5.5 0.7 pad_maximum_fusion.2.parts_ref
  6.2 4.6 %shard_map.104 = f32[128,768]{1,0:T(8,128)} custom-call(bf16[128,2048]{1,0:T(8,128)(2,1)} %get-tuple-element.28.owner_ref, bf16[128,2048]{1,0:T(8,128)(2,1)} %get-tuple-element.29.slot_ref, bf16[3,6,2048]{2,1,0:T(8,128)(2,1)} %pad_maximum_fusion.2.parts_ref), custom_call_target="tpu_custom_call" | custom-call | flops 1207959552 | bytes 2457600 | tf_op jit(solution)/shard_map/pallas_call | solution.py:122
  10.7 1.4 copy.11
  12.1 23.2 %all_to_all.46 = f32[128,1,768]{2,1,0:T(1,128)S(1)} all-to-all(f32[128,1,768]{2,1,0:T(1,128)S(1)} %copy.11), channel_id=1, replica_groups=mesh['src'=16,'tgt'=8] {'src','tgt'}, dimensions={0} | all-to-all | bytes 786432 | tf_op jit(solution)/shard_map/all_to_all | solution.py:250
  35.4 0.3 reduce_sum.58
  35.6 0.4 copy-done.3
  36.1 0.1 broadcast_in_dim.13
  36.1 22.7 %all_to_all.47 = f32[128,9,128]{2,1,0:T(8,128)S(1)} all-to-all(f32[128,9,128]{2,1,0:T(8,128)S(1)} %broadcast_in_dim.13), channel_id=1, replica_groups=mesh['src'=16,'tgt'=8] {'src','tgt'}, dimensions={0} | all-to-all | bytes 1179648 | tf_op jit(solution)/shard_map/all_to_all | solution.py:215
  58.8 0.8 slice_bitcast_fusion.force_ref
  59.7 0.8 slice_bitcast_fusion.1.place_ref
  60.4 0.8 broadcast_in_dim.12.target_ref
  61.2 26.0 %shard_map.105 = f32[6,128,128]{2,1,0:T(8,128)} custom-call(f32[3,128,128]{2,1,0:T(8,128)} %broadcast_in_dim.12.target_ref, f32[3,16384]{1,0:T(4,128)} %slice_bitcast_fusion.1.place_ref, f32[6,16384]{1,0:T(8,128)} %slice_bitcast_fusion.force_ref), custom_call_target="tpu_custom_call" | custom-call | flops 188743680 | bytes 1179648 | tf_op jit(solution)/shard_map/pallas_call | solution.py:199
  87.2 1.2 reduce_sum.59
  88.4 0.1 fusion.13
  88.5 1.0 broadcast_in_dim.14
  89.4 5.0 %all-to-all-start.2 = ((f32[128,1,768]{2,1,0:T(1,128)}), f32[128,1,768]{2,1,0:T(1,128)S(1)}, u32[]{:S(2)}, u32[]{:S(2)}) async-start(f32[128,1,768]{2,1,0:T(1,128)} %broadcast_in_dim.14), calls=%async_computation.2 | async-start | bytes 786432 | tf_op jit(solution)/shard_map/all_to_all | solution.py:260
  94.4 0.6 fusion.24
  95.1 11.4 %all-to-all-done.2 = f32[128,1,768]{2,1,0:T(1,128)S(1)} async-done(((f32[128,1,768]{2,1,0:T(1,128)}), f32[128,1,768]{2,1,0:T(1,128)S(1)}, u32[]{:S(2)}, u32[]{:S(2)}) %all-to-all-start.2) | async-done | bytes 393248 | tf_op jit(solution)/shard_map/all_to_all | solution.py:260
  106.5 0.4 copy.12
  106.9 0.1 fusion.6
  107.0 0.9 pad_maximum_fusion.parts_ref
  107.9 4.6 %shard_map.106 = f32[6,2048]{1,0:T(8,128)} custom-call(bf16[128,2048]{1,0:T(8,128)(2,1)} %get-tuple-element.28.owner_ref, bf16[128,2048]{1,0:T(8,128)(2,1)} %get-tuple-element.29.slot_ref, bf16[3,768,128]{2,1,0:T(8,128)(2,1)} %pad_maximum_fusion.parts_ref), custom_call_target="tpu_custom_call" | custom-call | flops 1207959552 | bytes 2457600 | tf_op jit(solution)/shard_map/pallas_call | solution.py:134
  112.5 0.9 multiply_reduce_fusion.1
  113.4 0.7 multiply_add_fusion.1
  114.1 0.7 pad_maximum_fusion.3.parts_ref
  114.8 4.6 %shard_map.107 = f32[128,768]{1,0:T(8,128)} custom-call(bf16[128,2048]{1,0:T(8,128)(2,1)} %get-tuple-element.28.owner_ref, bf16[128,2048]{1,0:T(8,128)(2,1)} %get-tuple-element.29.slot_ref, bf16[3,6,2048]{2,1,0:T(8,128)(2,1)} %pad_maximum_fusion.3.parts_ref), custom_call_target="tpu_custom_call" | custom-call | flops 1207959552 | bytes 2457600 | tf_op jit(solution)/shard_map/pallas_call | solution.py:122
  119.3 1.4 copy.13
  120.7 16.2 %all_to_all.48 = f32[128,1,768]{2,1,0:T(1,128)S(1)} all-to-all(f32[128,1,768]{2,1,0:T(1,128)S(1)} %copy.13), channel_id=1, replica_groups=mesh['src'=16,'tgt'=8] {'src','tgt'}, dimensions={0} | all-to-all | bytes 786432 | tf_op jit(solution)/shard_map/all_to_all | solution.py:250
  137.0 0.3 reduce_sum.62
  137.3 17.6 %all_to_all.49 = f32[128,6,128]{2,1,0:T(8,128)} all-to-all(f32[128,6,128]{2,1,0:T(8,128)S(1)} %broadcast_in_dim.16), channel_id=1, replica_groups=mesh['src'=16,'tgt'=8] {'src','tgt'}, dimensions={0} | all-to-all | bytes 786432 | tf_op jit(solution)/shard_map/all_to_all | solution.py:215
  154.9 26.0 %shard_map.108 = f32[6,128,128]{2,1,0:T(8,128)} custom-call(f32[3,128,128]{2,1,0:T(8,128)} %broadcast_in_dim.12.target_ref, f32[3,16384]{1,0:T(4,128)} %slice_bitcast_fusion.1.place_ref, f32[6,16384]{1,0:T(8,128)} %bitcast.76), custom_call_target="tpu_custom_call" | custom-call | flops 188743680 | bytes 1179648 | tf_op jit(solution)/shard_map/pallas_call | solution.py:199
  180.8 1.2 reduce_sum.63
  182.0 0.1 fusion.14
  182.1 1.0 broadcast_in_dim.17
  183.1 4.9 %all-to-all-start.5 = ((f32[128,1,768]{2,1,0:T(1,128)}), f32[128,1,768]{2,1,0:T(1,128)S(1)}, u32[]{:S(2)}, u32[]{:S(2)}) async-start(f32[128,1,768]{2,1,0:T(1,128)} %broadcast_in_dim.17), calls=%async_computation.5 | async-start | bytes 786432 | tf_op jit(solution)/shard_map/all_to_all | solution.py:260
  188.0 0.7 multiply_add_fusion
  188.6 11.3 %all-to-all-done.5 = f32[128,1,768]{2,1,0:T(1,128)S(1)} async-done(((f32[128,1,768]{2,1,0:T(1,128)}), f32[128,1,768]{2,1,0:T(1,128)S(1)}, u32[]{:S(2)}, u32[]{:S(2)}) %all-to-all-start.5) | async-done | bytes 393248 | tf_op jit(solution)/shard_map/all_to_all | solution.py:260
  199.9 0.4 copy.14
  200.3 0.1 fusion.8
  200.4 0.9 pad_maximum_fusion.1.parts_ref
  201.3 4.6 %shard_map.109 = f32[6,2048]{1,0:T(8,128)} custom-call(bf16[128,2048]{1,0:T(8,128)(2,1)} %get-tuple-element.28.owner_ref, bf16[128,2048]{1,0:T(8,128)(2,1)} %get-tuple-element.29.slot_ref, bf16[3,768,128]{2,1,0:T(8,128)(2,1)} %pad_maximum_fusion.1.parts_ref), custom_call_target="tpu_custom_call" | custom-call | flops 1207959552 | bytes 2457600 | tf_op jit(solution)/shard_map/pallas_call | solution.py:134
  205.9 0.9 multiply_reduce_fusion
  206.8 1.2 fusion.18
  (23 shorter events, 0.2 us)
Async XLA Ops:
  2.5 1.0 copy-start
  2.5 1.0 copy-start.1
  3.5 0.7 copy-start.4
  35.4 0.7 copy-start.3
  87.2 1.2 copy-start.5
  89.4 5.0 %copy-start.6 = (f32[2]{0:T(128)S(1)}, f32[2]{0:T(128)}, u32[]{:S(2)}) copy-start(f32[2]{0:T(128)} %param.15) | copy-start | bytes 28
  89.4 17.0 %all-to-all-start.2 = ((f32[128,1,768]{2,1,0:T(1,128)}), f32[128,1,768]{2,1,0:T(1,128)S(1)}, u32[]{:S(2)}, u32[]{:S(2)}) async-start(f32[128,1,768]{2,1,0:T(1,128)} %broadcast_in_dim.14), calls=%async_computation.2 | async-start | bytes 786432 | tf_op jit(solution)/shard_map/all_to_all | solution.py:260
  112.5 0.9 copy-start.2
  183.1 16.8 %all-to-all-start.5 = ((f32[128,1,768]{2,1,0:T(1,128)}), f32[128,1,768]{2,1,0:T(1,128)S(1)}, u32[]{:S(2)}, u32[]{:S(2)}) async-start(f32[128,1,768]{2,1,0:T(1,128)} %broadcast_in_dim.17), calls=%async_computation.5 | async-start | bytes 786432 | tf_op jit(solution)/shard_map/all_to_all | solution.py:260

commit v7 on v6

--- a/solution.py
+++ b/solution.py
@@ -79,12 +79,10 @@
     )
 
 
-def split_three(value):
+def split_two(value):
     high = lax.reduce_precision(value, exponent_bits=8, mantissa_bits=7)
-    rest = value - high
-    middle = lax.reduce_precision(rest, exponent_bits=8, mantissa_bits=7)
-    low = rest - middle
-    return jnp.stack([high, middle, low]).astype(jnp.bfloat16)
+    low = value - high
+    return jnp.stack([high, low]).astype(jnp.bfloat16)
 
 
 def scatter_kernel(owner_ref, slot_ref, parts_ref, out_ref):
@@ -93,7 +91,7 @@
     slot = slot_ref[...]
     for k in range(6):
         total = None
-        for p in range(3):
+        for p in range(2):
             weighted = slot * parts_ref[p, k : k + 1, :]
             term = lax.dot_general(
                 owner, weighted, (((1,), (1,)), ((), ())), preferred_element_type=jnp.float32
@@ -108,7 +106,7 @@
     slot = slot_ref[...].astype(jnp.float32)
     for k in range(6):
         picked = None
-        for p in range(3):
+        for p in range(2):
             part = parts_ref[p, k * slots : (k + 1) * slots, :]
             term = jnp.dot(part, owner, preferred_element_type=jnp.float32)
             picked = term if picked is None else picked + term
@@ -118,12 +116,12 @@
 def scatter_forces(owner_t, slot_t, end_force):
     owners, ends = owner_t.shape
     slots = slot_t.shape[0]
-    parts = split_three(end_force)
+    parts = split_two(end_force)
     return pl.pallas_call(
         scatter_kernel,
         out_shape=jax.ShapeDtypeStruct((owners, 6 * slots), jnp.float32),
         cost_estimate=pl.CostEstimate(
-            flops=2 * 18 * owners * slots * ends, transcendentals=0, bytes_accessed=4 * ends * 300
+            flops=2 * 12 * owners * slots * ends, transcendentals=0, bytes_accessed=4 * ends * 300
         ),
     )(owner_t, slot_t, parts)
 
@@ -135,9 +133,9 @@
         gather_kernel,
         out_shape=jax.ShapeDtypeStruct((6, ends), jnp.float32),
         cost_estimate=pl.CostEstimate(
-            flops=2 * 18 * owners * slots * ends, transcendentals=0, bytes_accessed=4 * ends * 300
+            flops=2 * 12 * owners * slots * ends, transcendentals=0, bytes_accessed=4 * ends * 300
         ),
-    )(owner_t, slot_t, split_three(table))
+    )(owner_t, slot_t, split_two(table))
 
 
 def pair_kernel(target_ref, place_ref, force_ref, out_ref):

time: 209 us -> 205 us (0.981)
  Pallas kernels: 70.3 us -> 66.9 us
where the time goes in v7:
time: 205 us; the launch traced here: 204 us
  blocking collectives  79.7 us (39%)
  Pallas kernels  66.9 us (33%)
  waiting for transfers between devices  22.7 us (11%)
  other arithmetic  14.5 us (7%)
  starting transfers between devices  9.9 us (5%)
  local copies, waits for them, and re-layouts  9.74 us (5%)
    pallas_call x2, Pallas kernels, mobility_own(): pl.pallas_call(pair_kernel, out_shape=jax.ShapeDtypeStruct((6, own_rows,...  51.9 us
    all_to_all x2, blocking collectives, gather_all(): spread = lax.all_to_all(spread, AXES, 0, 0, tiled=True)  40.3 us
    all_to_all x2, blocking collectives, per_device(): pieces = lax.all_to_all(pieces, AXES, 0, 0, tiled=True)  39.4 us
    all_to_all x2, waiting for transfers between devices, per_device(): every = lax.all_to_all(every, AXES, 0, 0, tiled=True)  22.7 us
    all_to_all x2, starting transfers between devices, per_device(): every = lax.all_to_all(every, AXES, 0, 0, tiled=True)  9.9 us
    pallas_call x2, Pallas kernels, scatter_forces(): pl.pallas_call(scatter_kernel, out_shape=jax.ShapeDtypeStruct((owners, 6...  7.51 us
    pallas_call x2, Pallas kernels, gather_velocity(): pl.pallas_call(gather_kernel, out_shape=jax.ShapeDtypeStruct((6, ends), j...  7.46 us
  transfers between devices with their start and end apart: 2, of which 2 were waited for; matrix products, arithmetic and copies ran while one was open for 1% of the time, Pallas kernels for 0%

profile of v7, /device:TPU:1, one launch (start us, length us, event | category | flops | bytes accessed | tf_op | source)
XLA Modules:
  0.0 204.3 jit_solution(3923006696055286237)
XLA Ops:
  0.6 1.1 multiply_subtract_fusion.5
  1.7 0.8 slice_negate_fusion
  2.5 1.0 multiply_subtract_fusion.2
  3.5 0.7 copy-done.4
  4.3 0.6 pad_maximum_fusion.3.parts_ref
  4.9 1.2 fusion
  6.1 3.8 %shard_map.104 = f32[128,768]{1,0:T(8,128)} custom-call(bf16[128,2048]{1,0:T(8,128)(2,1)} %get-tuple-element.24.owner_ref, bf16[128,2048]{1,0:T(8,128)(2,1)} %get-tuple-element.25.slot_ref, bf16[2,6,2048]{2,1,0:T(8,128)(2,1)} %pad_maximum_fusion.3.parts_ref), custom_call_target="tpu_custom_call" | custom-call | flops 805306368 | bytes 2457600 | tf_op jit(solution)/shard_map/pallas_call | solution.py:120
  9.9 1.4 copy.11
  11.3 23.2 %all_to_all.46 = f32[128,1,768]{2,1,0:T(1,128)S(1)} all-to-all(f32[128,1,768]{2,1,0:T(1,128)S(1)} %copy.11), channel_id=1, replica_groups=mesh['src'=16,'tgt'=8] {'src','tgt'}, dimensions={0} | all-to-all | bytes 786432 | tf_op jit(solution)/shard_map/all_to_all | solution.py:248
  34.5 0.3 reduce_sum.58
  34.8 0.4 copy-done.3
  35.2 0.1 broadcast_in_dim.13
  35.3 22.7 %all_to_all.47 = f32[128,9,128]{2,1,0:T(8,128)S(1)} all-to-all(f32[128,9,128]{2,1,0:T(8,128)S(1)} %broadcast_in_dim.13), channel_id=1, replica_groups=mesh['src'=16,'tgt'=8] {'src','tgt'}, dimensions={0} | all-to-all | bytes 1179648 | tf_op jit(solution)/shard_map/all_to_all | solution.py:213
  58.0 0.8 slice_bitcast_fusion.force_ref
  58.8 0.8 slice_bitcast_fusion.1.place_ref
  59.6 0.8 broadcast_in_dim.12.target_ref
  60.4 26.0 %shard_map.105 = f32[6,128,128]{2,1,0:T(8,128)} custom-call(f32[3,128,128]{2,1,0:T(8,128)} %broadcast_in_dim.12.target_ref, f32[3,16384]{1,0:T(4,128)} %slice_bitcast_fusion.1.place_ref, f32[6,16384]{1,0:T(8,128)} %slice_bitcast_fusion.force_ref), custom_call_target="tpu_custom_call" | custom-call | flops 188743680 | bytes 1179648 | tf_op jit(solution)/shard_map/pallas_call | solution.py:197
  86.3 1.2 reduce_sum.59
  87.5 0.1 fusion.11
  87.6 1.0 broadcast_in_dim.14
  88.6 5.0 %all-to-all-start.2 = ((f32[128,1,768]{2,1,0:T(1,128)}), f32[128,1,768]{2,1,0:T(1,128)S(1)}, u32[]{:S(2)}, u32[]{:S(2)}) async-start(f32[128,1,768]{2,1,0:T(1,128)} %broadcast_in_dim.14), calls=%async_computation.2 | async-start | bytes 786432 | tf_op jit(solution)/shard_map/all_to_all | solution.py:258
  93.6 0.6 fusion.22
  94.2 11.4 %all-to-all-done.2 = f32[128,1,768]{2,1,0:T(1,128)S(1)} async-done(((f32[128,1,768]{2,1,0:T(1,128)}), f32[128,1,768]{2,1,0:T(1,128)S(1)}, u32[]{:S(2)}, u32[]{:S(2)}) %all-to-all-start.2) | async-done | bytes 393248 | tf_op jit(solution)/shard_map/all_to_all | solution.py:258
  105.6 0.4 copy.12
  106.0 0.1 fusion.6
  106.1 0.8 pad_maximum_fusion.parts_ref
  106.9 3.7 %shard_map.106 = f32[6,2048]{1,0:T(8,128)} custom-call(bf16[128,2048]{1,0:T(8,128)(2,1)} %get-tuple-element.24.owner_ref, bf16[128,2048]{1,0:T(8,128)(2,1)} %get-tuple-element.25.slot_ref, bf16[2,768,128]{2,1,0:T(8,128)(2,1)} %pad_maximum_fusion.parts_ref), custom_call_target="tpu_custom_call" | custom-call | flops 805306368 | bytes 2457600 | tf_op jit(solution)/shard_map/pallas_call | solution.py:132
  110.6 0.9 multiply_reduce_fusion.1
  111.5 0.7 multiply_add_fusion.1
  112.2 0.6 pad_maximum_fusion.4.parts_ref
  112.9 3.8 %shard_map.107 = f32[128,768]{1,0:T(8,128)} custom-call(bf16[128,2048]{1,0:T(8,128)(2,1)} %get-tuple-element.24.owner_ref, bf16[128,2048]{1,0:T(8,128)(2,1)} %get-tuple-element.25.slot_ref, bf16[2,6,2048]{2,1,0:T(8,128)(2,1)} %pad_maximum_fusion.4.parts_ref), custom_call_target="tpu_custom_call" | custom-call | flops 805306368 | bytes 2457600 | tf_op jit(solution)/shard_map/pallas_call | solution.py:120
  116.6 1.4 copy.13
  118.0 16.2 %all_to_all.48 = f32[128,1,768]{2,1,0:T(1,128)S(1)} all-to-all(f32[128,1,768]{2,1,0:T(1,128)S(1)} %copy.13), channel_id=1, replica_groups=mesh['src'=16,'tgt'=8] {'src','tgt'}, dimensions={0} | all-to-all | bytes 786432 | tf_op jit(solution)/shard_map/all_to_all | solution.py:248
  134.2 0.3 reduce_sum.62
  134.6 17.6 %all_to_all.49 = f32[128,6,128]{2,1,0:T(8,128)} all-to-all(f32[128,6,128]{2,1,0:T(8,128)S(1)} %broadcast_in_dim.16), channel_id=1, replica_groups=mesh['src'=16,'tgt'=8] {'src','tgt'}, dimensions={0} | all-to-all | bytes 786432 | tf_op jit(solution)/shard_map/all_to_all | solution.py:213
  152.2 26.0 %shard_map.108 = f32[6,128,128]{2,1,0:T(8,128)} custom-call(f32[3,128,128]{2,1,0:T(8,128)} %broadcast_in_dim.12.target_ref, f32[3,16384]{1,0:T(4,128)} %slice_bitcast_fusion.1.place_ref, f32[6,16384]{1,0:T(8,128)} %bitcast.60), custom_call_target="tpu_custom_call" | custom-call | flops 188743680 | bytes 1179648 | tf_op jit(solution)/shard_map/pallas_call | solution.py:197
  178.1 1.2 reduce_sum.63
  179.3 0.1 fusion.12
  179.4 1.0 broadcast_in_dim.17
  180.3 4.9 %all-to-all-start.5 = ((f32[128,1,768]{2,1,0:T(1,128)}), f32[128,1,768]{2,1,0:T(1,128)S(1)}, u32[]{:S(2)}, u32[]{:S(2)}) async-start(f32[128,1,768]{2,1,0:T(1,128)} %broadcast_in_dim.17), calls=%async_computation.5 | async-start | bytes 786432 | tf_op jit(solution)/shard_map/all_to_all | solution.py:258
  185.3 0.7 multiply_add_fusion
  185.9 11.3 %all-to-all-done.5 = f32[128,1,768]{2,1,0:T(1,128)S(1)} async-done(((f32[128,1,768]{2,1,0:T(1,128)}), f32[128,1,768]{2,1,0:T(1,128)S(1)}, u32[]{:S(2)}, u32[]{:S(2)}) %all-to-all-start.5) | async-done | bytes 393248 | tf_op jit(solution)/shard_map/all_to_all | solution.py:258
  197.2 0.4 copy.14
  197.6 0.1 fusion.7
  197.6 0.8 pad_maximum_fusion.1.parts_ref
  198.4 3.7 %shard_map.109 = f32[6,2048]{1,0:T(8,128)} custom-call(bf16[128,2048]{1,0:T(8,128)(2,1)} %get-tuple-element.24.owner_ref, bf16[128,2048]{1,0:T(8,128)(2,1)} %get-tuple-element.25.slot_ref, bf16[2,768,128]{2,1,0:T(8,128)(2,1)} %pad_maximum_fusion.1.parts_ref), custom_call_target="tpu_custom_call" | custom-call | flops 805306368 | bytes 2457600 | tf_op jit(solution)/shard_map/pallas_call | solution.py:132
  202.2 0.9 multiply_reduce_fusion
  203.1 1.2 fusion.16
  (23 shorter events, 0.2 us)
Async XLA Ops:
  2.5 1.0 copy-start
  2.5 1.0 copy-start.1
  3.5 0.7 copy-start.4
  34.5 0.7 copy-start.3
  86.3 1.2 copy-start.5
  88.6 5.0 %copy-start.6 = (f32[2]{0:T(128)S(1)}, f32[2]{0:T(128)}, u32[]{:S(2)}) copy-start(f32[2]{0:T(128)} %param.15) | copy-start | bytes 28
  88.6 17.0 %all-to-all-start.2 = ((f32[128,1,768]{2,1,0:T(1,128)}), f32[128,1,768]{2,1,0:T(1,128)S(1)}, u32[]{:S(2)}, u32[]{:S(2)}) async-start(f32[128,1,768]{2,1,0:T(1,128)} %broadcast_in_dim.14), calls=%async_computation.2 | async-start | bytes 786432 | tf_op jit(solution)/shard_map/all_to_all | solution.py:258
  110.6 0.9 copy-start.2
  180.3 16.8 %all-to-all-start.5 = ((f32[128,1,768]{2,1,0:T(1,128)}), f32[128,1,768]{2,1,0:T(1,128)S(1)}, u32[]{:S(2)}, u32[]{:S(2)}) async-start(f32[128,1,768]{2,1,0:T(1,128)} %broadcast_in_dim.17), calls=%async_computation.5 | async-start | bytes 786432 | tf_op jit(solution)/shard_map/all_to_all | solution.py:258

commit v8 on v7

--- a/solution.py
+++ b/solution.py
@@ -2,6 +2,7 @@
 import jax.numpy as jnp
 from jax import lax
 from jax.experimental import pallas as pl
+from jax.experimental.pallas import tpu as pltpu
 from jax.sharding import PartitionSpec as P
 
 ITERS = 2
@@ -138,9 +139,10 @@
     )(owner_t, slot_t, split_two(table))
 
 
-def pair_kernel(target_ref, place_ref, force_ref, out_ref):
+def pair_kernel(target_ref, place_ref, force_ref, own_ref, out_ref, sums_ref):
     targets = target_ref.shape[1]
-    chunks = place_ref.shape[1] // 128
+    chunks = place_ref.shape[0]
+    first_place = place_ref.shape[1] - 3
 
     def group(g, carry):
         rows = pl.ds(pl.multiple_of(g * 8, 8), 8)
@@ -149,9 +151,8 @@
         target_z = target_ref[2, rows, :]
 
         def chunk(j, sums):
-            lanes = pl.ds(pl.multiple_of(j * 128, 128), 128)
-            place = place_ref[:, lanes]
-            force = force_ref[:, lanes]
+            place = place_ref[j, first_place : first_place + 3, :]
+            force = force_ref[j, 0:6, :]
             r_x = target_x - place[0:1]
             r_y = target_y - place[1:2]
             r_z = target_z - place[2:3]
@@ -184,28 +185,40 @@
         zero = jnp.zeros((8, 128), jnp.float32)
         sums = lax.fori_loop(0, chunks, chunk, (zero,) * 6, unroll=32)
         for k in range(6):
-            out_ref[k, rows, :] = sums[k]
+            sums_ref[k, rows, :] = sums[k]
         return carry
 
     lax.fori_loop(0, targets // 8, group, 0)
-
-
-def mobility_own(positions, all_pos, all_forces, own_forces):
-    own_rows = positions.shape[1]
-    sources = all_pos.shape[1]
-    spread = jnp.broadcast_to(positions[:, :, None], (3, own_rows, 128))
-    partial = pl.pallas_call(
+    ones = jnp.ones((8, 128), jnp.bfloat16)
+    for k in range(6):
+        value = sums_ref[k]
+        high = value.astype(jnp.bfloat16)
+        rest = value - high.astype(jnp.float32)
+        middle = rest.astype(jnp.bfloat16)
+        low = (rest - middle.astype(jnp.float32)).astype(jnp.bfloat16)
+        total = None
+        for part in (high, middle, low):
+            term = lax.dot_general(
+                ones, part, (((1,), (1,)), ((), ())), preferred_element_type=jnp.float32
+            )
+            total = term if total is None else total + term
+        scale = 1.0 if k < 3 else 0.75
+        out_ref[k : k + 1, :] = total[0:1, :] + scale * own_ref[k : k + 1, :]
+
+
+def mobility_own(spread, places, forces, own_forces):
+    own_rows = own_forces.shape[1]
+    sources = places.shape[0] * places.shape[2]
+    return pl.pallas_call(
         pair_kernel,
-        out_shape=jax.ShapeDtypeStruct((6, own_rows, 128), jnp.float32),
+        out_shape=jax.ShapeDtypeStruct((6, own_rows), jnp.float32),
+        scratch_shapes=[pltpu.VMEM((6, own_rows, 128), jnp.float32)],
         cost_estimate=pl.CostEstimate(
             flops=90 * own_rows * sources,
             transcendentals=own_rows * sources,
-            bytes_accessed=4 * (9 * sources + 9 * own_rows * 128),
+            bytes_accessed=4 * (9 * sources + 3 * own_rows * 128),
         ),
-    )(spread, all_pos, all_forces)
-    self_scale = jnp.array([1.0, 1.0, 1.0, 0.75, 0.75, 0.75], jnp.float32)[:, None]
-    return jnp.sum(partial, 2) + self_scale * own_forces
-
+    )(spread, places, forces, own_forces)
 
 def gather_all(block, devices):
     rows, width = block.shape
@@ -239,6 +252,7 @@
     slot_t = (
         jnp.arange(own_rows, dtype=jnp.int32)[:, None] == (end_bodies % own_rows)[None, :]
     ).astype(jnp.bfloat16)
+    spread = jnp.broadcast_to(positions[:, :, None], (3, own_rows, 128))
     current = impulse_now
     shifted = impulse_now + MOMENTUM * (impulse_now - impulse_prev)
     own_velocity = jnp.zeros((6, own_rows), jnp.float32)
@@ -248,12 +262,16 @@
         pieces = lax.all_to_all(pieces, AXES, 0, 0, tiled=True)
         own_forces = jnp.sum(pieces, 0).reshape(6, own_rows)
         if k == 0:
-            both = gather_all(jnp.concatenate([own_forces, positions]), devices)
-            all_forces, all_pos = both[:6], both[6:]
+            places = lax.all_to_all(
+                jnp.broadcast_to(jnp.concatenate([own_forces, positions])[None], (devices, 9, own_rows)),
+                AXES, 0, 0, tiled=True,
+            )
+            forces = places
         else:
-            all_forces = gather_all(own_forces, devices)
-
-        own_velocity = mobility_own(positions, all_pos, all_forces, own_forces)
+            forces = lax.all_to_all(
+                jnp.broadcast_to(own_forces[None], (devices, 6, own_rows)), AXES, 0, 0, tiled=True
+            )
+        own_velocity = mobility_own(spread, places, forces, own_forces)
         every = jnp.broadcast_to(own_velocity.reshape(1, 6 * own_rows), (devices, 6 * own_rows))
         every = lax.all_to_all(every, AXES, 0, 0, tiled=True)
         end_velocity = gather_velocity(owner_t, slot_t, every.T)

time: 205 us -> 204 us (level)
  blocking collectives: 79.7 us -> 96.8 us
  waiting for transfers between devices: 22.7 us -> 11.4 us
  starting transfers between devices: 9.9 us -> 5.01 us
  other arithmetic: 14.5 us -> 11.4 us
    all_to_all x2 -> x3, blocking collectives: 40.3 us -> 57.3 us  [the longest x1 23.1 us: per_device(): lax.all_to_all(jnp.broadcast_to(jnp.concatenate([own_forces, positions])[...]
    all_to_all x2 -> x1, waiting for transfers between devices: 22.7 us -> 11.4 us  [per_device(): every = lax.all_to_all(every, AXES, 0, 0, tiled=True)]
    all_to_all x2 -> x1, starting transfers between devices: 9.9 us -> 5.01 us  [per_device(): every = lax.all_to_all(every, AXES, 0, 0, tiled=True)]
    reduce_sum x2 -> x0, other arithmetic: 2.35 us -> none  [mobility_own(): return jnp.sum(partial, 2) + self_scale * own_forces]
  transfers between devices with their start and end apart: 2 -> 1, of which waited for: 2 -> 1; matrix products, arithmetic and copies ran while one was open for 1% -> 0% of each run, Pallas kernels for 0% -> 0%
where the time goes in v8:
time: 204 us; the launch traced here: 203 us
  blocking collectives  96.8 us (47%)
  Pallas kernels  68.3 us (33%)
  other arithmetic  11.4 us (6%)
  waiting for transfers between devices  11.4 us (6%)
  local copies, waits for them, and re-layouts  9.41 us (5%)
  starting transfers between devices  5.01 us (2%)
    pallas_call x2, Pallas kernels, mobility_own(): pl.pallas_call(pair_kernel, out_shape=jax.ShapeDtypeStruct((6, own_rows),...  53.3 us
    all_to_all x2, blocking collectives, per_device(): pieces = lax.all_to_all(pieces, AXES, 0, 0, tiled=True)  39.4 us
    all_to_all x1, blocking collectives, per_device(): lax.all_to_all(jnp.broadcast_to(jnp.concatenate([own_forces, positions])[...  23.1 us
    all_to_all x1, blocking collectives, per_device(): lax.all_to_all(jnp.broadcast_to(own_forces[None], (devices, 6, own_rows))...  17.6 us
    all_to_all x1, blocking collectives, per_device(): every = lax.all_to_all(every, AXES, 0, 0, tiled=True)  16.6 us
    all_to_all x1, waiting for transfers between devices, per_device(): every = lax.all_to_all(every, AXES, 0, 0, tiled=True)  11.4 us
    pallas_call x2, Pallas kernels, scatter_forces(): pl.pallas_call(scatter_kernel, out_shape=jax.ShapeDtypeStruct((owners, 6...  7.48 us
    pallas_call x2, Pallas kernels, gather_velocity(): pl.pallas_call(gather_kernel, out_shape=jax.ShapeDtypeStruct((6, ends), j...  7.47 us
  transfers between devices with their start and end apart: 1, of which 1 were waited for; matrix products, arithmetic and copies ran while one was open for 0% of the time, Pallas kernels for 0%

profile of v8, /device:TPU:1, one launch (start us, length us, event | category | flops | bytes accessed | tf_op | source)
XLA Modules:
  0.0 203.1 jit_solution(10305735716861511646)
XLA Ops:
  0.6 1.1 multiply_subtract_fusion.5
  1.7 0.8 slice_negate_fusion
  2.5 0.0 copy-start.2
  2.5 1.0 multiply_subtract_fusion.2
  3.5 0.0 copy-done.2
  3.5 0.0 copy-done.3
  3.5 0.0 copy-start.6
  3.5 0.7 copy-done.6
  4.3 0.6 pad_maximum_fusion.3.parts_ref
  4.9 1.2 fusion
  6.2 3.7 %shard_map.86 = f32[128,768]{1,0:T(8,128)} custom-call(bf16[128,2048]{1,0:T(8,128)(2,1)} %get-tuple-element.24.owner_ref, bf16[128,2048]{1,0:T(8,128)(2,1)} %get-tuple-element.25.slot_ref, bf16[2,6,2048]{2,1,0:T(8,128)(2,1)} %pad_maximum_fusion.3.parts_ref), custom_call_target="tpu_custom_call" | custom-call | flops 805306368 | bytes 2457600 | tf_op jit(solution)/shard_map/pallas_call | solution.py:121
  9.9 1.4 copy.9
  11.3 23.2 %all_to_all.46 = f32[128,1,768]{2,1,0:T(1,128)S(1)} all-to-all(f32[128,1,768]{2,1,0:T(1,128)S(1)} %copy.9), channel_id=1, replica_groups=mesh['src'=16,'tgt'=8] {'src','tgt'}, dimensions={0} | all-to-all | bytes 786432 | tf_op jit(solution)/shard_map/all_to_all | solution.py:262
  34.5 0.3 reduce_sum.36
  34.8 0.4 copy-done.5
  35.2 0.2 copy-done.1
  35.4 0.1 broadcast_in_dim.17
  35.5 23.1 %all_to_all.47.place_ref.force_ref = f32[128,9,128]{2,1,0:T(8,128)} all-to-all(f32[128,9,128]{2,1,0:T(8,128)S(1)} %broadcast_in_dim.17), channel_id=1, replica_groups=mesh['src'=16,'tgt'=8] {'src','tgt'}, dimensions={0} | all-to-all | bytes 1179648 | tf_op jit(solution)/shard_map/all_to_all | solution.py:265
  58.6 0.8 broadcast_in_dim.16.target_ref
  59.4 26.8 %shard_map.87 = f32[6,128]{1,0:T(8,128)} custom-call(f32[3,128,128]{2,1,0:T(8,128)} %broadcast_in_dim.16.target_ref, f32[128,9,128]{2,1,0:T(8,128)} %all_to_all.47.place_ref.force_ref, f32[128,9,128]{2,1,0:T(8,128)} %all_to_all.47.place_ref.force_ref, f32[6,128]{1,0:T(8,128)} %bitcast.45), custom_call_target="tpu_custom_call" | custom-call | flops 188743680 | bytes 786432 | tf_op jit(solution)/shard_map/pallas_call | solution.py:212
  86.2 1.6 broadcast_in_dim.19
  87.8 5.0 %all-to-all-start.2 = ((f32[128,1,768]{2,1,0:T(1,128)}), f32[128,1,768]{2,1,0:T(1,128)S(1)}, u32[]{:S(2)}, u32[]{:S(2)}) async-start(f32[128,1,768]{2,1,0:T(1,128)} %broadcast_in_dim.19), calls=%async_computation.2 | async-start | bytes 786432 | tf_op jit(solution)/shard_map/all_to_all | solution.py:276
  92.8 0.0 copy-done.7
  92.8 0.6 fusion.20
  93.4 11.4 %all-to-all-done.2 = f32[128,1,768]{2,1,0:T(1,128)S(1)} async-done(((f32[128,1,768]{2,1,0:T(1,128)}), f32[128,1,768]{2,1,0:T(1,128)S(1)}, u32[]{:S(2)}, u32[]{:S(2)}) %all-to-all-start.2) | async-done | bytes 393248 | tf_op jit(solution)/shard_map/all_to_all | solution.py:276
  104.9 0.4 copy.10
  105.3 0.1 fusion.6
  105.3 0.8 pad_maximum_fusion.parts_ref
  106.1 3.7 %shard_map.88 = f32[6,2048]{1,0:T(8,128)} custom-call(bf16[128,2048]{1,0:T(8,128)(2,1)} %get-tuple-element.24.owner_ref, bf16[128,2048]{1,0:T(8,128)(2,1)} %get-tuple-element.25.slot_ref, bf16[2,768,128]{2,1,0:T(8,128)(2,1)} %pad_maximum_fusion.parts_ref), custom_call_target="tpu_custom_call" | custom-call | flops 805306368 | bytes 2457600 | tf_op jit(solution)/shard_map/pallas_call | solution.py:133
  109.9 0.9 multiply_reduce_fusion.1
  110.8 0.0 copy-done.4
  110.8 0.7 multiply_add_fusion
  111.5 0.6 pad_maximum_fusion.4.parts_ref
  112.1 3.7 %shard_map.89 = f32[128,768]{1,0:T(8,128)} custom-call(bf16[128,2048]{1,0:T(8,128)(2,1)} %get-tuple-element.24.owner_ref, bf16[128,2048]{1,0:T(8,128)(2,1)} %get-tuple-element.25.slot_ref, bf16[2,6,2048]{2,1,0:T(8,128)(2,1)} %pad_maximum_fusion.4.parts_ref), custom_call_target="tpu_custom_call" | custom-call | flops 805306368 | bytes 2457600 | tf_op jit(solution)/shard_map/pallas_call | solution.py:121
  115.9 1.4 copy.11
  117.3 16.2 %all_to_all.48 = f32[128,1,768]{2,1,0:T(1,128)S(1)} all-to-all(f32[128,1,768]{2,1,0:T(1,128)S(1)} %copy.11), channel_id=1, replica_groups=mesh['src'=16,'tgt'=8] {'src','tgt'}, dimensions={0} | all-to-all | bytes 786432 | tf_op jit(solution)/shard_map/all_to_all | solution.py:262
  133.5 0.3 reduce_sum.38
  133.8 0.5 copy-done
  134.3 17.6 %all_to_all.49.force_ref = f32[128,6,128]{2,1,0:T(8,128)} all-to-all(f32[128,6,128]{2,1,0:T(8,128)S(1)} %broadcast_in_dim.21), channel_id=1, replica_groups=mesh['src'=16,'tgt'=8] {'src','tgt'}, dimensions={0} | all-to-all | bytes 786432 | tf_op jit(solution)/shard_map/all_to_all | solution.py:271
  151.9 26.5 %shard_map.90 = f32[6,128]{1,0:T(8,128)} custom-call(f32[3,128,128]{2,1,0:T(8,128)} %broadcast_in_dim.16.target_ref, f32[128,9,128]{2,1,0:T(8,128)} %all_to_all.47.place_ref.force_ref, f32[128,6,128]{2,1,0:T(8,128)} %all_to_all.49.force_ref, f32[6,128]{1,0:T(8,128)} %bitcast.43), custom_call_target="tpu_custom_call" | custom-call | flops 188743680 | bytes 786432 | tf_op jit(solution)/shard_map/pallas_call | solution.py:212
  178.5 0.9 broadcast_in_dim.46
  179.4 16.6 %all_to_all.50 = f32[128,1,768]{2,1,0:T(1,128)S(1)} all-to-all(f32[128,1,768]{2,1,0:T(1,128)S(1)} %broadcast_in_dim.46), channel_id=1, replica_groups=mesh['src'=16,'tgt'=8] {'src','tgt'}, dimensions={0} | all-to-all | bytes 786432 | tf_op jit(solution)/shard_map/all_to_all | solution.py:276
  196.0 0.4 copy.12
  196.4 0.1 fusion.7
  196.4 0.8 pad_maximum_fusion.1.parts_ref
  197.2 3.7 %shard_map.91 = f32[6,2048]{1,0:T(8,128)} custom-call(bf16[128,2048]{1,0:T(8,128)(2,1)} %get-tuple-element.24.owner_ref, bf16[128,2048]{1,0:T(8,128)(2,1)} %get-tuple-element.25.slot_ref, bf16[2,768,128]{2,1,0:T(8,128)(2,1)} %pad_maximum_fusion.1.parts_ref), custom_call_target="tpu_custom_call" | custom-call | flops 805306368 | bytes 2457600 | tf_op jit(solution)/shard_map/pallas_call | solution.py:133
  201.0 0.9 multiply_reduce_fusion
  201.8 1.2 fusion.14
  (17 shorter events, 0.2 us)
Async XLA Ops:
  2.5 1.0 copy-start.2
  2.5 1.0 copy-start.3
  3.5 0.7 copy-start.6
  34.5 0.7 copy-start.5
  34.8 0.6 copy-start.1
  87.8 5.0 %copy-start.7 = (f32[2]{0:T(128)S(1)}, f32[2]{0:T(128)}, u32[]{:S(2)}) copy-start(f32[2]{0:T(128)} %param.13) | copy-start | bytes 28
  87.8 17.0 %all-to-all-start.2 = ((f32[128,1,768]{2,1,0:T(1,128)}), f32[128,1,768]{2,1,0:T(1,128)S(1)}, u32[]{:S(2)}, u32[]{:S(2)}) async-start(f32[128,1,768]{2,1,0:T(1,128)} %broadcast_in_dim.19), calls=%async_computation.2 | async-start | bytes 786432 | tf_op jit(solution)/shard_map/all_to_all | solution.py:276
  109.9 0.9 copy-start.4
  133.8 0.6 copy-start

commit v9 on v8

--- a/solution.py
+++ b/solution.py
@@ -98,7 +98,7 @@
                 owner, weighted, (((1,), (1,)), ((), ())), preferred_element_type=jnp.float32
             )
             total = term if total is None else total + term
-        out_ref[:, k * slots : (k + 1) * slots] = total
+        out_ref[:, 0, k * slots : (k + 1) * slots] = total
 
 
 def gather_kernel(owner_ref, slot_ref, parts_ref, out_ref):
@@ -120,7 +120,7 @@
     parts = split_two(end_force)
     return pl.pallas_call(
         scatter_kernel,
-        out_shape=jax.ShapeDtypeStruct((owners, 6 * slots), jnp.float32),
+        out_shape=jax.ShapeDtypeStruct((owners, 1, 6 * slots), jnp.float32),
         cost_estimate=pl.CostEstimate(
             flops=2 * 12 * owners * slots * ends, transcendentals=0, bytes_accessed=4 * ends * 300
         ),
@@ -142,7 +142,7 @@
 def pair_kernel(target_ref, place_ref, force_ref, own_ref, out_ref, sums_ref):
     targets = target_ref.shape[1]
     chunks = place_ref.shape[0]
-    first_place = place_ref.shape[1] - 3
+    first_place = place_ref.shape[2] // 128 - 3
 
     def group(g, carry):
         rows = pl.ds(pl.multiple_of(g * 8, 8), 8)
@@ -151,13 +151,17 @@
         target_z = target_ref[2, rows, :]
 
         def chunk(j, sums):
-            place = place_ref[j, first_place : first_place + 3, :]
-            force = force_ref[j, 0:6, :]
-            r_x = target_x - place[0:1]
-            r_y = target_y - place[1:2]
-            r_z = target_z - place[2:3]
-            f_x, f_y, f_z = force[0:1], force[1:2], force[2:3]
-            t_x, t_y, t_z = force[3:4], force[4:5], force[5:6]
+            place = place_ref[j]
+            force = force_ref[j]
+
+            def lane_row(block, row):
+                return block[:, row * 128 : (row + 1) * 128]
+
+            r_x = target_x - lane_row(place, first_place)
+            r_y = target_y - lane_row(place, first_place + 1)
+            r_z = target_z - lane_row(place, first_place + 2)
+            f_x, f_y, f_z = (lane_row(force, 0), lane_row(force, 1), lane_row(force, 2))
+            t_x, t_y, t_z = (lane_row(force, 3), lane_row(force, 4), lane_row(force, 5))
             dist_sq = r_x * r_x + r_y * r_y + r_z * r_z
             inverse = jnp.where(dist_sq > 0.0, lax.rsqrt(dist_sq), 0.0)
             inverse_sq = inverse * inverse
@@ -208,7 +212,7 @@
 
 def mobility_own(spread, places, forces, own_forces):
     own_rows = own_forces.shape[1]
-    sources = places.shape[0] * places.shape[2]
+    sources = places.shape[0] * 128
     return pl.pallas_call(
         pair_kernel,
         out_shape=jax.ShapeDtypeStruct((6, own_rows), jnp.float32),
@@ -262,14 +266,15 @@
         pieces = lax.all_to_all(pieces, AXES, 0, 0, tiled=True)
         own_forces = jnp.sum(pieces, 0).reshape(6, own_rows)
         if k == 0:
+            block = jnp.concatenate([own_forces, positions]).reshape(1, 1, 9 * own_rows)
             places = lax.all_to_all(
-                jnp.broadcast_to(jnp.concatenate([own_forces, positions])[None], (devices, 9, own_rows)),
-                AXES, 0, 0, tiled=True,
+                jnp.broadcast_to(block, (devices, 1, 9 * own_rows)), AXES, 0, 0, tiled=True
             )
             forces = places
         else:
+            block = own_forces.reshape(1, 1, 6 * own_rows)
             forces = lax.all_to_all(
-                jnp.broadcast_to(own_forces[None], (devices, 6, own_rows)), AXES, 0, 0, tiled=True
+                jnp.broadcast_to(block, (devices, 1, 6 * own_rows)), AXES, 0, 0, tiled=True
             )
         own_velocity = mobility_own(spread, places, forces, own_forces)
         every = jnp.broadcast_to(own_velocity.reshape(1, 6 * own_rows), (devices, 6 * own_rows))

time: 204 us -> 195 us (0.956)
  blocking collectives: 96.8 us -> 91.5 us
  local copies, waits for them, and re-layouts: 9.41 us -> 6.84 us
    all_to_all x2, blocking collectives: 40.7 us -> 35.1 us  [the longest x1 18.5 us: per_device(): lax.all_to_all(jnp.broadcast_to(block, (devices, 1, 9 * own_rows)), AXES,...]
    all_to_all x2 -> x0, local copies, waits for them, and re-layouts: 2.8 us -> none  [per_device(): pieces = lax.all_to_all(pieces, AXES, 0, 0, tiled=True)]
where the time goes in v9:
time: 195 us; the launch traced here: 194 us
  blocking collectives  91.5 us (47%)
  Pallas kernels  67.5 us (35%)
  other arithmetic  11.4 us (6%)
  waiting for transfers between devices  11.4 us (6%)
  local copies, waits for them, and re-layouts  6.84 us (4%)
  starting transfers between devices  4.75 us (2%)
    pallas_call x2, Pallas kernels, mobility_own(): pl.pallas_call(pair_kernel, out_shape=jax.ShapeDtypeStruct((6, own_rows),...  52.4 us
    all_to_all x2, blocking collectives, per_device(): pieces = lax.all_to_all(pieces, AXES, 0, 0, tiled=True)  40.2 us
    all_to_all x1, blocking collectives, per_device(): lax.all_to_all(jnp.broadcast_to(block, (devices, 1, 9 * own_rows)), AXES,...  18.5 us
    all_to_all x1, blocking collectives, per_device(): lax.all_to_all(jnp.broadcast_to(block, (devices, 1, 6 * own_rows)), AXES,...  16.6 us
    all_to_all x1, blocking collectives, per_device(): every = lax.all_to_all(every, AXES, 0, 0, tiled=True)  16.2 us
    all_to_all x1, waiting for transfers between devices, per_device(): every = lax.all_to_all(every, AXES, 0, 0, tiled=True)  11.4 us
    pallas_call x2, Pallas kernels, scatter_forces(): pl.pallas_call(scatter_kernel, out_shape=jax.ShapeDtypeStruct((owners, 1,...  7.65 us
    pallas_call x2, Pallas kernels, gather_velocity(): pl.pallas_call(gather_kernel, out_shape=jax.ShapeDtypeStruct((6, ends), j...  7.47 us
  transfers between devices with their start and end apart: 1, of which 1 were waited for; matrix products, arithmetic and copies ran while one was open for 0% of the time, Pallas kernels for 0%

profile of v9, /device:TPU:1, one launch (start us, length us, event | category | flops | bytes accessed | tf_op | source)
XLA Modules:
  0.0 194.2 jit_solution(15833974192654102139)
XLA Ops:
  0.6 1.1 multiply_subtract_fusion.5
  1.7 0.8 slice_negate_fusion
  2.5 0.0 copy-start.2
  2.5 0.0 copy-start.3
  2.5 1.0 multiply_subtract_fusion.2
  3.5 0.0 copy-done.2
  3.5 0.0 copy-done.3
  3.5 0.0 copy-start.6
  3.5 0.7 copy-done.6
  4.3 0.6 pad_maximum_fusion.3.parts_ref
  4.9 1.2 fusion
  6.2 3.8 %shard_map.86 = f32[128,1,768]{2,1,0:T(1,128)} custom-call(bf16[128,2048]{1,0:T(8,128)(2,1)} %get-tuple-element.24.owner_ref, bf16[128,2048]{1,0:T(8,128)(2,1)} %get-tuple-element.25.slot_ref, bf16[2,6,2048]{2,1,0:T(8,128)(2,1)} %pad_maximum_fusion.3.parts_ref), custom_call_target="tpu_custom_call" | custom-call | flops 805306368 | bytes 2457600 | tf_op jit(solution)/shard_map/pallas_call | solution.py:121
  10.0 23.4 %all_to_all.38 = f32[128,1,768]{2,1,0:T(1,128)S(1)} all-to-all(f32[128,1,768]{2,1,0:T(1,128)} %shard_map.86), channel_id=1, replica_groups=mesh['src'=16,'tgt'=8] {'src','tgt'}, dimensions={0} | all-to-all | bytes 786432 | tf_op jit(solution)/shard_map/all_to_all | solution.py:266
  33.4 0.3 reduce_sum.36
  33.7 0.4 copy-done.5
  34.1 0.2 copy-done.1
  34.3 0.3 broadcast_in_dim.18
  34.6 18.5 %all_to_all.39.place_ref.force_ref = f32[128,1,1152]{2,1,0:T(1,128)} all-to-all(f32[128,1,1152]{2,1,0:T(1,128)S(1)} %broadcast_in_dim.18), channel_id=1, replica_groups=mesh['src'=16,'tgt'=8] {'src','tgt'}, dimensions={0} | all-to-all | bytes 1179648 | tf_op jit(solution)/shard_map/all_to_all | solution.py:270
  53.1 0.8 broadcast_in_dim.16.target_ref
  53.8 26.2 %shard_map.87 = f32[6,128]{1,0:T(8,128)} custom-call(f32[3,128,128]{2,1,0:T(8,128)} %broadcast_in_dim.16.target_ref, f32[128,1,1152]{2,1,0:T(1,128)} %all_to_all.39.place_ref.force_ref, f32[128,1,1152]{2,1,0:T(1,128)} %all_to_all.39.place_ref.force_ref, f32[6,128]{1,0:T(8,128)} %bitcast.42), custom_call_target="tpu_custom_call" | custom-call | flops 188743680 | bytes 786432 | tf_op jit(solution)/shard_map/pallas_call | solution.py:216
  80.1 1.6 broadcast_in_dim.20
  81.7 4.7 %all-to-all-start.2 = ((f32[128,1,768]{2,1,0:T(1,128)}), f32[128,1,768]{2,1,0:T(1,128)S(1)}, u32[]{:S(2)}, u32[]{:S(2)}) async-start(f32[128,1,768]{2,1,0:T(1,128)} %broadcast_in_dim.20), calls=%async_computation.2 | async-start | bytes 786432 | tf_op jit(solution)/shard_map/all_to_all | solution.py:281
  86.5 0.0 copy-done.7
  86.5 0.6 fusion.20
  87.1 11.4 %all-to-all-done.2 = f32[128,1,768]{2,1,0:T(1,128)S(1)} async-done(((f32[128,1,768]{2,1,0:T(1,128)}), f32[128,1,768]{2,1,0:T(1,128)S(1)}, u32[]{:S(2)}, u32[]{:S(2)}) %all-to-all-start.2) | async-done | bytes 393248 | tf_op jit(solution)/shard_map/all_to_all | solution.py:281
  98.4 0.4 copy.9
  98.8 0.1 fusion.6
  98.9 0.8 pad_maximum_fusion.parts_ref
  99.7 3.7 %shard_map.88 = f32[6,2048]{1,0:T(8,128)} custom-call(bf16[128,2048]{1,0:T(8,128)(2,1)} %get-tuple-element.24.owner_ref, bf16[128,2048]{1,0:T(8,128)(2,1)} %get-tuple-element.25.slot_ref, bf16[2,768,128]{2,1,0:T(8,128)(2,1)} %pad_maximum_fusion.parts_ref), custom_call_target="tpu_custom_call" | custom-call | flops 805306368 | bytes 2457600 | tf_op jit(solution)/shard_map/pallas_call | solution.py:133
  103.4 0.9 multiply_reduce_fusion.1
  104.3 0.0 copy-done.4
  104.3 0.7 multiply_add_fusion
  105.0 0.6 pad_maximum_fusion.4.parts_ref
  105.7 3.8 %shard_map.89 = f32[128,1,768]{2,1,0:T(1,128)} custom-call(bf16[128,2048]{1,0:T(8,128)(2,1)} %get-tuple-element.24.owner_ref, bf16[128,2048]{1,0:T(8,128)(2,1)} %get-tuple-element.25.slot_ref, bf16[2,6,2048]{2,1,0:T(8,128)(2,1)} %pad_maximum_fusion.4.parts_ref), custom_call_target="tpu_custom_call" | custom-call | flops 805306368 | bytes 2457600 | tf_op jit(solution)/shard_map/pallas_call | solution.py:121
  109.5 16.8 %all_to_all.40 = f32[128,1,768]{2,1,0:T(1,128)S(1)} all-to-all(f32[128,1,768]{2,1,0:T(1,128)} %shard_map.89), channel_id=1, replica_groups=mesh['src'=16,'tgt'=8] {'src','tgt'}, dimensions={0} | all-to-all | bytes 786432 | tf_op jit(solution)/shard_map/all_to_all | solution.py:266
  126.3 0.3 reduce_sum.38
  126.6 0.2 broadcast_in_dim.21
  126.8 0.4 copy-done
  127.2 16.6 %all_to_all.41.force_ref = f32[128,1,768]{2,1,0:T(1,128)} all-to-all(f32[128,1,768]{2,1,0:T(1,128)S(1)} %broadcast_in_dim.21), channel_id=1, replica_groups=mesh['src'=16,'tgt'=8] {'src','tgt'}, dimensions={0} | all-to-all | bytes 786432 | tf_op jit(solution)/shard_map/all_to_all | solution.py:276
  143.8 26.2 %shard_map.90 = f32[6,128]{1,0:T(8,128)} custom-call(f32[3,128,128]{2,1,0:T(8,128)} %broadcast_in_dim.16.target_ref, f32[128,1,1152]{2,1,0:T(1,128)} %all_to_all.39.place_ref.force_ref, f32[128,1,768]{2,1,0:T(1,128)} %all_to_all.41.force_ref, f32[6,128]{1,0:T(8,128)} %bitcast.40), custom_call_target="tpu_custom_call" | custom-call | flops 188743680 | bytes 786432 | tf_op jit(solution)/shard_map/pallas_call | solution.py:216
  170.0 0.9 broadcast_in_dim.45
  170.9 16.2 %all_to_all.42 = f32[128,1,768]{2,1,0:T(1,128)S(1)} all-to-all(f32[128,1,768]{2,1,0:T(1,128)S(1)} %broadcast_in_dim.45), channel_id=1, replica_groups=mesh['src'=16,'tgt'=8] {'src','tgt'}, dimensions={0} | all-to-all | bytes 786432 | tf_op jit(solution)/shard_map/all_to_all | solution.py:281
  187.1 0.4 copy.10
  187.5 0.1 fusion.7
  187.5 0.8 pad_maximum_fusion.1.parts_ref
  188.3 3.7 %shard_map.91 = f32[6,2048]{1,0:T(8,128)} custom-call(bf16[128,2048]{1,0:T(8,128)(2,1)} %get-tuple-element.24.owner_ref, bf16[128,2048]{1,0:T(8,128)(2,1)} %get-tuple-element.25.slot_ref, bf16[2,768,128]{2,1,0:T(8,128)(2,1)} %pad_maximum_fusion.1.parts_ref), custom_call_target="tpu_custom_call" | custom-call | flops 805306368 | bytes 2457600 | tf_op jit(solution)/shard_map/pallas_call | solution.py:133
  192.0 0.9 multiply_reduce_fusion
  192.9 1.2 fusion.14
  (15 shorter events, 0.1 us)
Async XLA Ops:
  2.5 1.0 copy-start.2
  2.5 1.0 copy-start.3
  3.5 0.7 copy-start.6
  33.4 0.7 copy-start.5
  33.7 0.6 copy-start.1
  81.7 4.8 %copy-start.7 = (f32[2]{0:T(128)S(1)}, f32[2]{0:T(128)}, u32[]{:S(2)}) copy-start(f32[2]{0:T(128)} %param.13) | copy-start | bytes 28
  81.7 16.7 %all-to-all-start.2 = ((f32[128,1,768]{2,1,0:T(1,128)}), f32[128,1,768]{2,1,0:T(1,128)S(1)}, u32[]{:S(2)}, u32[]{:S(2)}) async-start(f32[128,1,768]{2,1,0:T(1,128)} %broadcast_in_dim.20), calls=%async_computation.2 | async-start | bytes 786432 | tf_op jit(solution)/shard_map/all_to_all | solution.py:281
  103.4 0.9 copy-start.4
  126.6 0.6 copy-start

commit v10 on v9

--- a/solution.py
+++ b/solution.py
@@ -1,3 +1,5 @@
+import functools
+
 import jax
 import jax.numpy as jnp
 from jax import lax
@@ -139,6 +141,82 @@
     )(owner_t, slot_t, split_two(table))
 
 
+def split_pair(value):
+    high = value.astype(jnp.bfloat16)
+    low = (value - high.astype(jnp.float32)).astype(jnp.bfloat16)
+    return (high, low)
+
+
+def contact_kernel(gather, scatter, *refs):
+    owner_ref, slot_ref, rows_ref, state_ref = refs[:4]
+    refs = refs[4:]
+    if gather:
+        table_ref, refs = refs[0], refs[1:]
+    outs = refs
+    slots = slot_ref.shape[0]
+    contacts = state_ref.shape[1]
+    owner = owner_ref[...]
+    slot = slot_ref[...]
+    shifted = state_ref[1:2, :]
+    if gather:
+        slot_wide = slot.astype(jnp.float32)
+        rate = None
+        for k in range(6):
+            picked = None
+            for part in split_pair(table_ref[k * slots : (k + 1) * slots, :]):
+                term = jnp.dot(part, owner, preferred_element_type=jnp.float32)
+                picked = term if picked is None else picked + term
+            velocity = jnp.sum(picked * slot_wide, axis=0, keepdims=True)
+            term = rows_ref[k : k + 1, :] * velocity
+            rate = term if rate is None else rate + term
+        normal_rate = rate[:, :contacts] + rate[:, contacts:]
+        current = state_ref[0:1, :]
+        gaps = state_ref[2:3, :]
+        step = state_ref[3:4, :]
+        updated = jnp.maximum(shifted - step * (gaps + normal_rate), 0.0)
+        shifted = updated + MOMENTUM * (updated - current)
+        outs[0][0:1, :] = updated
+        outs[0][1:2, :] = shifted
+        outs = outs[1:]
+    if scatter:
+        out_ref = outs[0]
+        for k in range(6):
+            total = None
+            for side in range(2):
+                ends = slice(side * contacts, (side + 1) * contacts)
+                force = rows_ref[k : k + 1, ends] * shifted
+                for part in split_pair(force):
+                    weighted = slot[:, ends] * part
+                    term = lax.dot_general(
+                        owner[:, ends], weighted, (((1,), (1,)), ((), ())),
+                        preferred_element_type=jnp.float32,
+                    )
+                    total = term if total is None else total + term
+            out_ref[:, 0, k * slots : (k + 1) * slots] = total
+
+
+def contact_step(owner_t, slot_t, end_rows, state, table=None, scatter=True):
+    owners, ends = owner_t.shape
+    slots = slot_t.shape[0]
+    contacts = state.shape[1]
+    gather = table is not None
+    shapes = []
+    if gather:
+        shapes.append(jax.ShapeDtypeStruct((2, contacts), jnp.float32))
+    if scatter:
+        shapes.append(jax.ShapeDtypeStruct((owners, 1, 6 * slots), jnp.float32))
+    args = (owner_t, slot_t, end_rows, state) + ((table,) if gather else ())
+    return pl.pallas_call(
+        functools.partial(contact_kernel, gather, scatter),
+        out_shape=tuple(shapes),
+        cost_estimate=pl.CostEstimate(
+            flops=2 * 12 * owners * slots * ends * (int(gather) + int(scatter)),
+            transcendentals=0,
+            bytes_accessed=4 * ends * 300,
+        ),
+    )(*args)
+
+
 def pair_kernel(target_ref, place_ref, force_ref, own_ref, out_ref, sums_ref):
     targets = target_ref.shape[1]
     chunks = place_ref.shape[0]
@@ -257,12 +335,11 @@
         jnp.arange(own_rows, dtype=jnp.int32)[:, None] == (end_bodies % own_rows)[None, :]
     ).astype(jnp.bfloat16)
     spread = jnp.broadcast_to(positions[:, :, None], (3, own_rows, 128))
-    current = impulse_now
     shifted = impulse_now + MOMENTUM * (impulse_now - impulse_prev)
+    state = jnp.stack([impulse_now, shifted, gaps, jnp.broadcast_to(step_sizes[0], gaps.shape)])
+    (pieces,) = contact_step(owner_t, slot_t, end_rows, state)
     own_velocity = jnp.zeros((6, own_rows), jnp.float32)
     for k in range(ITERS):
-        end_force = end_rows * jnp.concatenate([shifted, shifted])[None, :]
-        pieces = scatter_forces(owner_t, slot_t, end_force)
         pieces = lax.all_to_all(pieces, AXES, 0, 0, tiled=True)
         own_forces = jnp.sum(pieces, 0).reshape(6, own_rows)
         if k == 0:
@@ -279,12 +356,15 @@
         own_velocity = mobility_own(spread, places, forces, own_forces)
         every = jnp.broadcast_to(own_velocity.reshape(1, 6 * own_rows), (devices, 6 * own_rows))
         every = lax.all_to_all(every, AXES, 0, 0, tiled=True)
-        end_velocity = gather_velocity(owner_t, slot_t, every.T)
-        end_rate = jnp.sum(end_rows * end_velocity, 0)
-        normal_rate = end_rate[:contacts] + end_rate[contacts:]
-        updated = jnp.maximum(shifted - step_sizes[k] * (gaps + normal_rate), 0.0)
-        shifted = updated + MOMENTUM * (updated - current)
-        current = updated
+        state = jnp.concatenate(
+            [state[:3], jnp.broadcast_to(step_sizes[k], (1,) + gaps.shape)]
+        )
+        last = k == ITERS - 1
+        result = contact_step(owner_t, slot_t, end_rows, state, every.T, scatter=not last)
+        state = jnp.concatenate([result[0], state[2:]])
+        if not last:
+            pieces = result[1]
+    current = state[0]
     return (current, own_velocity)
 
 

time: 195 us -> 192 us (0.985)
  local copies, waits for them, and re-layouts: 6.84 us -> 11 us
  other arithmetic: 11.4 us -> 7.88 us
  Pallas kernels: 67.5 us -> 65.4 us
    pallas_call x4 -> x3, Pallas kernels: 15.1 us -> 13.4 us  [contact_step(): pl.pallas_call(functools.partial(contact_kernel, gather, scatter), out_sh...]
  transfers between devices with their start and end apart: 1 -> 1, of which waited for: 1 -> 1; matrix products, arithmetic and copies ran while one was open for 0% -> 1% of each run, Pallas kernels for 0% -> 0%
where the time goes in v10:
time: 192 us; the launch traced here: 191 us
  blocking collectives  91.8 us (48%)
  Pallas kernels  65.4 us (34%)
  local copies, waits for them, and re-layouts  11 us (6%)
  waiting for transfers between devices  10.1 us (5%)
  other arithmetic  7.88 us (4%)
  starting transfers between devices  4.63 us (2%)
    pallas_call x2, Pallas kernels, mobility_own(): pl.pallas_call(pair_kernel, out_shape=jax.ShapeDtypeStruct((6, own_rows),...  51.9 us
    all_to_all x2, blocking collectives, per_device(): pieces = lax.all_to_all(pieces, AXES, 0, 0, tiled=True)  40.2 us
    all_to_all x1, blocking collectives, per_device(): lax.all_to_all(jnp.broadcast_to(block, (devices, 1, 9 * own_rows)), AXES,...  18.5 us
    all_to_all x1, blocking collectives, per_device(): lax.all_to_all(jnp.broadcast_to(block, (devices, 1, 6 * own_rows)), AXES,...  16.6 us
    all_to_all x1, blocking collectives, per_device(): every = lax.all_to_all(every, AXES, 0, 0, tiled=True)  16.5 us
    pallas_call x3, Pallas kernels, contact_step(): pl.pallas_call(functools.partial(contact_kernel, gather, scatter), out_sh...  13.4 us
    all_to_all x1, waiting for transfers between devices, per_device(): every = lax.all_to_all(every, AXES, 0, 0, tiled=True)  10.1 us
    all_to_all x1, starting transfers between devices, per_device(): every = lax.all_to_all(every, AXES, 0, 0, tiled=True)  4.63 us
  transfers between devices with their start and end apart: 1, of which 1 were waited for; matrix products, arithmetic and copies ran while one was open for 1% of the time, Pallas kernels for 0%

profile of v10, /device:TPU:1, one launch (start us, length us, event | category | flops | bytes accessed | tf_op | source)
XLA Modules:
  0.0 191.4 jit_solution(376767436814131455)
XLA Ops:
  0.6 1.0 multiply_subtract_fusion.2
  1.6 0.0 copy-start.9
  1.6 0.0 copy-start.5
  1.6 1.1 multiply_subtract_fusion.5
  2.7 0.0 copy-done.9
  2.7 0.6 fusion.7
  3.3 0.0 copy-done.5
  3.3 0.0 copy-start.3
  3.3 0.7 pad.9.clone
  4.1 0.0 copy-done.3
  4.1 0.0 copy-done.7
  4.1 1.2 fusion
  5.3 0.8 slice_negate_fusion
  6.1 0.0 copy-start.8
  6.1 0.7 copy-done.8
  6.8 1.3 fusion.4
  8.1 0.6 maximum_maximum_fusion.refs_2_
  8.7 3.9 %shard_map.86 = f32[128,1,768]{2,1,0:T(1,128)} custom-call(bf16[128,2048]{1,0:T(8,128)(2,1)} %get-tuple-element.22.refs_0_, bf16[128,2048]{1,0:T(8,128)(2,1)} %get-tuple-element.23.refs_1_, f32[6,2048]{1,0:T(8,128)} %maximum_maximum_fusion.refs_2_, f32[4,1024]{1,0:T(4,128)} %get-tuple-element.14.refs_3_), custom_call_target="tpu_custom_call" | custom-call | flops 805306368 | bytes 2457600 | tf_op jit(solution)/shard_map/pallas_call | solution.py:209
  12.6 23.4 %all_to_all.38 = f32[128,1,768]{2,1,0:T(1,128)S(1)} all-to-all(f32[128,1,768]{2,1,0:T(1,128)} %shard_map.86), channel_id=1, replica_groups=mesh['src'=16,'tgt'=8] {'src','tgt'}, dimensions={0} | all-to-all | bytes 786432 | tf_op jit(solution)/shard_map/all_to_all | solution.py:343
  36.0 0.3 reduce_sum.18
  36.3 0.4 copy-done.4
  36.7 0.2 copy-done.2
  36.9 0.3 broadcast_in_dim.18
  37.2 18.5 %all_to_all.39.place_ref.force_ref = f32[128,1,1152]{2,1,0:T(1,128)} all-to-all(f32[128,1,1152]{2,1,0:T(1,128)S(1)} %broadcast_in_dim.18), channel_id=1, replica_groups=mesh['src'=16,'tgt'=8] {'src','tgt'}, dimensions={0} | all-to-all | bytes 1179648 | tf_op jit(solution)/shard_map/all_to_all | solution.py:347
  55.7 0.8 broadcast_in_dim.16.target_ref
  56.5 26.0 %shard_map.87 = f32[6,128]{1,0:T(8,128)} custom-call(f32[3,128,128]{2,1,0:T(8,128)} %broadcast_in_dim.16.target_ref, f32[128,1,1152]{2,1,0:T(1,128)} %all_to_all.39.place_ref.force_ref, f32[128,1,1152]{2,1,0:T(1,128)} %all_to_all.39.place_ref.force_ref, f32[6,128]{1,0:T(8,128)} %bitcast.24), custom_call_target="tpu_custom_call" | custom-call | flops 188743680 | bytes 786432 | tf_op jit(solution)/shard_map/pallas_call | solution.py:294
  82.5 0.9 broadcast_in_dim.20
  83.4 16.5 %all_to_all.40 = f32[128,1,768]{2,1,0:T(1,128)S(1)} all-to-all(f32[128,1,768]{2,1,0:T(1,128)S(1)} %broadcast_in_dim.20), channel_id=1, replica_groups=mesh['src'=16,'tgt'=8] {'src','tgt'}, dimensions={0} | all-to-all | bytes 786432 | tf_op jit(solution)/shard_map/all_to_all | solution.py:358
  99.9 1.1 copy.9
  101.0 5.8 %shard_map.88 = (f32[2,1024]{1,0:T(2,128)}, f32[128,1,768]{2,1,0:T(1,128)}) custom-call(bf16[128,2048]{1,0:T(8,128)(2,1)} %get-tuple-element.22.refs_0_, bf16[128,2048]{1,0:T(8,128)(2,1)} %get-tuple-element.23.refs_1_, f32[6,2048]{1,0:T(8,128)} %maximum_maximum_fusion.refs_2_, f32[4,1024]{1,0:T(4,128)} %get-tuple-element.15.refs_3_, f32[768,128]{1,0:T(8,128)} %bitcast.21), custom_call_target="tpu_custom_call" | custom-call | flops 1610612736 | bytes 2457600 | tf_op jit(solution)/shard_map/pallas_call | solution.py:209
  106.8 16.8 %all_to_all.41 = f32[128,1,768]{2,1,0:T(1,128)S(1)} all-to-all(f32[128,1,768]{2,1,0:T(1,128)} %get-tuple-element.5), channel_id=1, replica_groups=mesh['src'=16,'tgt'=8] {'src','tgt'}, dimensions={0} | all-to-all | bytes 786432 | tf_op jit(solution)/shard_map/all_to_all | solution.py:343
  123.6 0.3 reduce_sum.19
  123.9 0.2 broadcast_in_dim.21
  124.1 0.4 copy-done.1
  124.4 16.6 %all_to_all.42.force_ref = f32[128,1,768]{2,1,0:T(1,128)} all-to-all(f32[128,1,768]{2,1,0:T(1,128)S(1)} %broadcast_in_dim.21), channel_id=1, replica_groups=mesh['src'=16,'tgt'=8] {'src','tgt'}, dimensions={0} | all-to-all | bytes 786432 | tf_op jit(solution)/shard_map/all_to_all | solution.py:353
  141.0 25.9 %shard_map.89 = f32[6,128]{1,0:T(8,128)} custom-call(f32[3,128,128]{2,1,0:T(8,128)} %broadcast_in_dim.16.target_ref, f32[128,1,1152]{2,1,0:T(1,128)} %all_to_all.39.place_ref.force_ref, f32[128,1,768]{2,1,0:T(1,128)} %all_to_all.42.force_ref, f32[6,128]{1,0:T(8,128)} %bitcast.22), custom_call_target="tpu_custom_call" | custom-call | flops 188743680 | bytes 786432 | tf_op jit(solution)/shard_map/pallas_call | solution.py:294
  167.0 1.6 broadcast_in_dim.45
  168.6 4.6 %all-to-all-start.5 = ((f32[128,1,768]{2,1,0:T(1,128)}), f32[128,1,768]{2,1,0:T(1,128)S(1)}, u32[]{:S(2)}, u32[]{:S(2)}) async-start(f32[128,1,768]{2,1,0:T(1,128)} %broadcast_in_dim.45), calls=%async_computation.5 | async-start | bytes 786432 | tf_op jit(solution)/shard_map/all_to_all | solution.py:358
  173.3 0.0 copy-done
  173.3 0.0 copy-start.6
  173.3 0.0 copy-start.10
  173.3 0.7 copy-done.6
  174.0 0.0 copy-done.10
  174.0 1.3 maximum_select_fusion.refs_3_
  175.3 10.1 %all-to-all-done.5 = f32[128,1,768]{2,1,0:T(1,128)S(1)} async-done(((f32[128,1,768]{2,1,0:T(1,128)}), f32[128,1,768]{2,1,0:T(1,128)S(1)}, u32[]{:S(2)}, u32[]{:S(2)}) %all-to-all-start.5) | async-done | bytes 393248 | tf_op jit(solution)/shard_map/all_to_all | solution.py:358
  185.3 1.1 copy.10
  186.4 3.8 %shard_map.90 = f32[2,1024]{1,0:T(2,128)} custom-call(bf16[128,2048]{1,0:T(8,128)(2,1)} %get-tuple-element.22.refs_0_, bf16[128,2048]{1,0:T(8,128)(2,1)} %get-tuple-element.23.refs_1_, f32[6,2048]{1,0:T(8,128)} %maximum_maximum_fusion.refs_2_, f32[4,1024]{1,0:T(4,128)} %maximum_select_fusion.refs_3_, f32[768,128]{1,0:T(8,128)} %bitcast.20), custom_call_target="tpu_custom_call" | custom-call | flops 805306368 | bytes 2457600 | tf_op jit(solution)/shard_map/pallas_call | solution.py:209
  190.1 1.3 slice.96
  (10 shorter events, 0.0 us)
Async XLA Ops:
  1.6 1.1 copy-start.9
  1.6 1.7 copy-start.5
  3.3 0.8 copy-start.3
  3.3 0.8 copy-start.7
  6.1 0.7 copy-start.8
  36.0 0.7 copy-start.4
  36.3 0.6 copy-start.2
  123.9 0.6 copy-start.1
  168.6 4.6 %copy-start = (f32[4,1024]{1,0:T(4,128)S(1)}, f32[4,1024]{1,0:T(4,128)}, u32[]{:S(2)}) copy-start(f32[4,1024]{1,0:T(4,128)} %get-tuple-element.15.refs_3_) | copy-start | bytes 49156
  168.6 16.7 %all-to-all-start.5 = ((f32[128,1,768]{2,1,0:T(1,128)}), f32[128,1,768]{2,1,0:T(1,128)S(1)}, u32[]{:S(2)}, u32[]{:S(2)}) async-start(f32[128,1,768]{2,1,0:T(1,128)} %broadcast_in_dim.45), calls=%async_computation.5 | async-start | bytes 786432 | tf_op jit(solution)/shard_map/all_to_all | solution.py:358
  173.3 0.7 copy-start.6
  173.3 0.7 copy-start.10

commit v11 on v10

--- a/solution.py
+++ b/solution.py
@@ -147,33 +147,56 @@
     return (high, low)
 
 
-def contact_kernel(gather, scatter, *refs):
-    owner_ref, slot_ref, rows_ref, state_ref = refs[:4]
-    refs = refs[4:]
+def contact_kernel(step, gather, scatter, *refs):
+    bodies_ref, frame_ref, state_ref, gaps_ref, steps_ref = refs[:5]
+    refs = refs[5:]
     if gather:
         table_ref, refs = refs[0], refs[1:]
     outs = refs
-    slots = slot_ref.shape[0]
-    contacts = state_ref.shape[1]
-    owner = owner_ref[...]
-    slot = slot_ref[...]
-    shifted = state_ref[1:2, :]
+    contacts = frame_ref.shape[1]
+    owners = outs[-1].shape[0] if scatter else table_ref.shape[1]
+    slots = outs[-1].shape[2] // 6 if scatter else table_ref.shape[0] // 6
+    frame = frame_ref[...]
+    normal = (frame[0:1], frame[1:2], frame[2:3])
+
+    def crossed(arm):
+        return (
+            arm[1] * normal[2] - arm[2] * normal[1],
+            arm[2] * normal[0] - arm[0] * normal[2],
+            arm[0] * normal[1] - arm[1] * normal[0],
+        )
+
+    first_lever = crossed((frame[3:4], frame[4:5], frame[5:6]))
+    second_lever = crossed((frame[6:7], frame[7:8], frame[8:9]))
+    rows = (
+        tuple(-v for v in normal) + tuple(-v for v in first_lever),
+        normal + second_lever,
+    )
+    owner_ids = lax.broadcasted_iota(jnp.int32, (owners, contacts), 0)
+    slot_ids = lax.broadcasted_iota(jnp.int32, (slots, contacts), 0)
+    owner_hot, slot_hot = [], []
+    for side in range(2):
+        body = bodies_ref[side : side + 1, :]
+        owner_hot.append((owner_ids == body // slots).astype(jnp.bfloat16))
+        slot_hot.append((slot_ids == body % slots).astype(jnp.bfloat16))
+    current = state_ref[0:1, :]
+    if step == 0:
+        shifted = current + MOMENTUM * (current - state_ref[1:2, :])
+    else:
+        shifted = state_ref[1:2, :]
     if gather:
-        slot_wide = slot.astype(jnp.float32)
         rate = None
-        for k in range(6):
-            picked = None
-            for part in split_pair(table_ref[k * slots : (k + 1) * slots, :]):
-                term = jnp.dot(part, owner, preferred_element_type=jnp.float32)
-                picked = term if picked is None else picked + term
-            velocity = jnp.sum(picked * slot_wide, axis=0, keepdims=True)
-            term = rows_ref[k : k + 1, :] * velocity
-            rate = term if rate is None else rate + term
-        normal_rate = rate[:, :contacts] + rate[:, contacts:]
-        current = state_ref[0:1, :]
-        gaps = state_ref[2:3, :]
-        step = state_ref[3:4, :]
-        updated = jnp.maximum(shifted - step * (gaps + normal_rate), 0.0)
+        for side in range(2):
+            slot_wide = slot_hot[side].astype(jnp.float32)
+            for k in range(6):
+                picked = None
+                for part in split_pair(table_ref[k * slots : (k + 1) * slots, :]):
+                    term = jnp.dot(part, owner_hot[side], preferred_element_type=jnp.float32)
+                    picked = term if picked is None else picked + term
+                velocity = jnp.sum(picked * slot_wide, axis=0, keepdims=True)
+                term = rows[side][k] * velocity
+                rate = term if rate is None else rate + term
+        updated = jnp.maximum(shifted - steps_ref[step] * (gaps_ref[...] + rate), 0.0)
         shifted = updated + MOMENTUM * (updated - current)
         outs[0][0:1, :] = updated
         outs[0][1:2, :] = shifted
@@ -183,39 +206,38 @@
         for k in range(6):
             total = None
             for side in range(2):
-                ends = slice(side * contacts, (side + 1) * contacts)
-                force = rows_ref[k : k + 1, ends] * shifted
-                for part in split_pair(force):
-                    weighted = slot[:, ends] * part
+                for part in split_pair(rows[side][k] * shifted):
+                    weighted = slot_hot[side] * part
                     term = lax.dot_general(
-                        owner[:, ends], weighted, (((1,), (1,)), ((), ())),
+                        owner_hot[side], weighted, (((1,), (1,)), ((), ())),
                         preferred_element_type=jnp.float32,
                     )
                     total = term if total is None else total + term
             out_ref[:, 0, k * slots : (k + 1) * slots] = total
 
 
-def contact_step(owner_t, slot_t, end_rows, state, table=None, scatter=True):
-    owners, ends = owner_t.shape
-    slots = slot_t.shape[0]
-    contacts = state.shape[1]
+def contact_step(step, owners, slots, bodies, frame, state, gaps, steps, table=None, scatter=True):
+    contacts = frame.shape[1]
     gather = table is not None
     shapes = []
     if gather:
         shapes.append(jax.ShapeDtypeStruct((2, contacts), jnp.float32))
     if scatter:
         shapes.append(jax.ShapeDtypeStruct((owners, 1, 6 * slots), jnp.float32))
-    args = (owner_t, slot_t, end_rows, state) + ((table,) if gather else ())
+    args = (bodies, frame, state, gaps, steps) + ((table,) if gather else ())
+    vmem = pl.BlockSpec(memory_space=pltpu.VMEM)
+    specs = [vmem, vmem, vmem, vmem, pl.BlockSpec(memory_space=pltpu.SMEM)] + [vmem] * int(gather)
     return pl.pallas_call(
-        functools.partial(contact_kernel, gather, scatter),
+        functools.partial(contact_kernel, step, gather, scatter),
         out_shape=tuple(shapes),
+        in_specs=specs,
+        out_specs=tuple(vmem for _ in shapes),
         cost_estimate=pl.CostEstimate(
-            flops=2 * 12 * owners * slots * ends * (int(gather) + int(scatter)),
+            flops=2 * 12 * owners * slots * 2 * contacts * (int(gather) + int(scatter)),
             transcendentals=0,
-            bytes_accessed=4 * ends * 300,
+            bytes_accessed=4 * contacts * 600,
         ),
     )(*args)
-
 
 def pair_kernel(target_ref, place_ref, force_ref, own_ref, out_ref, sums_ref):
     targets = target_ref.shape[1]
@@ -324,20 +346,10 @@
     me = lax.axis_index("src") * lax.axis_size("tgt") + lax.axis_index("tgt")
     own_rows = positions.shape[1]
     body_count = own_rows * devices
-    first_rows, second_rows = contact_rows(contact_frame)
-    contacts = contact_bodies.shape[1]
-    end_bodies = jnp.concatenate([contact_bodies[0], contact_bodies[1]])
-    end_rows = jnp.concatenate([first_rows, second_rows], axis=1)
-    owner_t = (
-        jnp.arange(devices, dtype=jnp.int32)[:, None] == (end_bodies // own_rows)[None, :]
-    ).astype(jnp.bfloat16)
-    slot_t = (
-        jnp.arange(own_rows, dtype=jnp.int32)[:, None] == (end_bodies % own_rows)[None, :]
-    ).astype(jnp.bfloat16)
     spread = jnp.broadcast_to(positions[:, :, None], (3, own_rows, 128))
-    shifted = impulse_now + MOMENTUM * (impulse_now - impulse_prev)
-    state = jnp.stack([impulse_now, shifted, gaps, jnp.broadcast_to(step_sizes[0], gaps.shape)])
-    (pieces,) = contact_step(owner_t, slot_t, end_rows, state)
+    gaps_row = gaps.reshape(1, -1)
+    state = jnp.stack([impulse_now, impulse_prev])
+    (pieces,) = contact_step(0, devices, own_rows, contact_bodies, contact_frame, state, gaps_row, step_sizes)
     own_velocity = jnp.zeros((6, own_rows), jnp.float32)
     for k in range(ITERS):
         pieces = lax.all_to_all(pieces, AXES, 0, 0, tiled=True)
@@ -356,12 +368,11 @@
         own_velocity = mobility_own(spread, places, forces, own_forces)
         every = jnp.broadcast_to(own_velocity.reshape(1, 6 * own_rows), (devices, 6 * own_rows))
         every = lax.all_to_all(every, AXES, 0, 0, tiled=True)
-        state = jnp.concatenate(
-            [state[:3], jnp.broadcast_to(step_sizes[k], (1,) + gaps.shape)]
+        last = k == ITERS - 1
+        result = contact_step(
+            k, devices, own_rows, contact_bodies, contact_frame, state, gaps_row, step_sizes, every.T, scatter=not last
         )
-        last = k == ITERS - 1
-        result = contact_step(owner_t, slot_t, end_rows, state, every.T, scatter=not last)
-        state = jnp.concatenate([result[0], state[2:]])
+        state = result[0]
         if not last:
             pieces = result[1]
     current = state[0]

time: 192 us -> 183 us (0.953)
  blocking collectives: 91.8 us -> 108 us
  waiting for transfers between devices: 10.1 us -> 0 us
  other arithmetic: 7.88 us -> 1.89 us
  starting transfers between devices: 4.63 us -> 0 us
  local copies, waits for them, and re-layouts: 11 us -> 7.46 us
    all_to_all x1 -> x2, blocking collectives: 16.5 us -> 32.7 us  [per_device(): every = lax.all_to_all(every, AXES, 0, 0, tiled=True)]
    all_to_all x1 -> x0, waiting for transfers between devices: 10.1 us -> none  [per_device(): every = lax.all_to_all(every, AXES, 0, 0, tiled=True)]
    all_to_all x1 -> x0, starting transfers between devices: 4.63 us -> none  [per_device(): every = lax.all_to_all(every, AXES, 0, 0, tiled=True)]
    sub x2 -> x0, other arithmetic: 2.05 us -> none  [cross_product(): first[1] * second[2] - first[2] * second[1]]
    concatenate x2 -> x0, other arithmetic: 1.93 us -> none  [the longest x1 1.29 us: per_device(): jnp.concatenate([state[:3], jnp.broadcast_to(step_sizes[k], (1,) + gaps.s...]
  transfers between devices with their start and end apart: 1 -> 0, of which waited for: 1 -> 0; matrix products, arithmetic and copies ran while one was open for 1% -> 0% of each run, Pallas kernels for 0% -> 0%
where the time goes in v11:
time: 183 us
  blocking collectives  108 us (59%)
  Pallas kernels  64.6 us (35%)
  local copies, waits for them, and re-layouts  7.46 us (4%)
  other arithmetic  1.89 us (1%)
    pallas_call x2, Pallas kernels, mobility_own(): pl.pallas_call(pair_kernel, out_shape=jax.ShapeDtypeStruct((6, own_rows),...  51.9 us
    all_to_all x2, blocking collectives, per_device(): pieces = lax.all_to_all(pieces, AXES, 0, 0, tiled=True)  40.2 us
    all_to_all x2, blocking collectives, per_device(): every = lax.all_to_all(every, AXES, 0, 0, tiled=True)  32.7 us
    all_to_all x1, blocking collectives, per_device(): lax.all_to_all(jnp.broadcast_to(block, (devices, 1, 9 * own_rows)), AXES,...  18.5 us
    all_to_all x1, blocking collectives, per_device(): lax.all_to_all(jnp.broadcast_to(block, (devices, 1, 6 * own_rows)), AXES,...  16.6 us
    pallas_call x3, Pallas kernels, contact_step(): pl.pallas_call(functools.partial(contact_kernel, step, gather, scatter),...  12.7 us

profile of v11, /device:TPU:1, one launch (start us, length us, event | category | flops | bytes accessed | tf_op | source)
XLA Modules:
  0.0 182.6 jit_solution(8733275666823417756)
XLA Ops:
  0.6 1.3 pad_maximum_fusion.refs_2_
  1.9 3.5 %shard_map.86 = f32[128,1,768]{2,1,0:T(1,128)} custom-call(s32[2,1024]{1,0:T(2,128)} %refs_0_.5, f32[9,1024]{1,0:T(8,128)} %refs_1_.5, f32[2,1024]{1,0:T(2,128)} %pad_maximum_fusion.refs_2_, f32[1,1024]{1,0:T(1,128)} %bitcast.26, f32[2]{0:T(128)} %refs_4_.5), custom_call_target="tpu_custom_call" | custom-call | flops 805306368 | bytes 2457600 | tf_op jit(solution)/shard_map/pallas_call | solution.py:230
  5.4 23.4 %all_to_all.38 = f32[128,1,768]{2,1,0:T(1,128)S(1)} all-to-all(f32[128,1,768]{2,1,0:T(1,128)} %shard_map.86), channel_id=1, replica_groups=mesh['src'=16,'tgt'=8] {'src','tgt'}, dimensions={0} | all-to-all | bytes 786432 | tf_op jit(solution)/shard_map/all_to_all | solution.py:355
  28.9 0.0 copy-start.2
  28.9 0.3 reduce_sum.18
  29.1 0.0 copy-start.1
  29.1 0.4 copy-done.2
  29.5 0.2 copy-done.1
  29.7 0.3 broadcast_in_dim.34
  30.0 18.5 %all_to_all.39.place_ref.force_ref = f32[128,1,1152]{2,1,0:T(1,128)} all-to-all(f32[128,1,1152]{2,1,0:T(1,128)S(1)} %broadcast_in_dim.34), channel_id=1, replica_groups=mesh['src'=16,'tgt'=8] {'src','tgt'}, dimensions={0} | all-to-all | bytes 1179648 | tf_op jit(solution)/shard_map/all_to_all | solution.py:359
  48.5 0.8 broadcast_in_dim.32.target_ref
  49.3 26.0 %shard_map.87 = f32[6,128]{1,0:T(8,128)} custom-call(f32[3,128,128]{2,1,0:T(8,128)} %broadcast_in_dim.32.target_ref, f32[128,1,1152]{2,1,0:T(1,128)} %all_to_all.39.place_ref.force_ref, f32[128,1,1152]{2,1,0:T(1,128)} %all_to_all.39.place_ref.force_ref, f32[6,128]{1,0:T(8,128)} %bitcast.20), custom_call_target="tpu_custom_call" | custom-call | flops 188743680 | bytes 786432 | tf_op jit(solution)/shard_map/pallas_call | solution.py:316
  75.3 0.9 broadcast_in_dim.36
  76.2 16.5 %all_to_all.40 = f32[128,1,768]{2,1,0:T(1,128)S(1)} all-to-all(f32[128,1,768]{2,1,0:T(1,128)S(1)} %broadcast_in_dim.36), channel_id=1, replica_groups=mesh['src'=16,'tgt'=8] {'src','tgt'}, dimensions={0} | all-to-all | bytes 786432 | tf_op jit(solution)/shard_map/all_to_all | solution.py:370
  92.7 1.1 copy.9
  93.8 5.6 %shard_map.88 = (f32[2,1024]{1,0:T(2,128)}, f32[128,1,768]{2,1,0:T(1,128)}) custom-call(s32[2,1024]{1,0:T(2,128)} %refs_0_.5, f32[9,1024]{1,0:T(8,128)} %refs_1_.5, f32[2,1024]{1,0:T(2,128)} %pad_maximum_fusion.refs_2_, f32[1,1024]{1,0:T(1,128)} %bitcast.27, f32[2]{0:T(128)} %refs_4_.5, f32[768,128]{1,0:T(8,128)} %bitcast.16), custom_call_target="tpu_custom_call" | custom-call | flops 1610612736 | bytes 2457600 | tf_op jit(solution)/shard_map/pallas_call | solution.py:230
  99.4 16.8 %all_to_all.41 = f32[128,1,768]{2,1,0:T(1,128)S(1)} all-to-all(f32[128,1,768]{2,1,0:T(1,128)} %get-tuple-element.5), channel_id=1, replica_groups=mesh['src'=16,'tgt'=8] {'src','tgt'}, dimensions={0} | all-to-all | bytes 786432 | tf_op jit(solution)/shard_map/all_to_all | solution.py:355
  116.2 0.3 reduce_sum.19
  116.5 0.0 copy-start
  116.5 0.2 broadcast_in_dim.37
  116.7 0.4 copy-done
  117.0 16.6 %all_to_all.42.force_ref = f32[128,1,768]{2,1,0:T(1,128)} all-to-all(f32[128,1,768]{2,1,0:T(1,128)S(1)} %broadcast_in_dim.37), channel_id=1, replica_groups=mesh['src'=16,'tgt'=8] {'src','tgt'}, dimensions={0} | all-to-all | bytes 786432 | tf_op jit(solution)/shard_map/all_to_all | solution.py:365
  133.7 25.9 %shard_map.89 = f32[6,128]{1,0:T(8,128)} custom-call(f32[3,128,128]{2,1,0:T(8,128)} %broadcast_in_dim.32.target_ref, f32[128,1,1152]{2,1,0:T(1,128)} %all_to_all.39.place_ref.force_ref, f32[128,1,768]{2,1,0:T(1,128)} %all_to_all.42.force_ref, f32[6,128]{1,0:T(8,128)} %bitcast.18), custom_call_target="tpu_custom_call" | custom-call | flops 188743680 | bytes 786432 | tf_op jit(solution)/shard_map/pallas_call | solution.py:316
  159.6 0.9 broadcast_in_dim.39
  160.5 16.2 %all_to_all.43 = f32[128,1,768]{2,1,0:T(1,128)S(1)} all-to-all(f32[128,1,768]{2,1,0:T(1,128)S(1)} %broadcast_in_dim.39), channel_id=1, replica_groups=mesh['src'=16,'tgt'=8] {'src','tgt'}, dimensions={0} | all-to-all | bytes 786432 | tf_op jit(solution)/shard_map/all_to_all | solution.py:370
  176.7 1.1 copy.10
  177.7 3.6 %shard_map.90 = f32[2,1024]{1,0:T(2,128)} custom-call(s32[2,1024]{1,0:T(2,128)} %refs_0_.5, f32[9,1024]{1,0:T(8,128)} %refs_1_.5, f32[2,1024]{1,0:T(2,128)} %get-tuple-element.4.refs_2_, f32[1,1024]{1,0:T(1,128)} %bitcast.28, f32[2]{0:T(128)} %refs_4_.5, f32[768,128]{1,0:T(8,128)} %bitcast.17), custom_call_target="tpu_custom_call" | custom-call | flops 805306368 | bytes 2457600 | tf_op jit(solution)/shard_map/pallas_call | solution.py:230
  181.3 1.3 slice.4
  (1 shorter events, 0.0 us)
Async XLA Ops:
  28.9 0.7 copy-start.2
  29.1 0.6 copy-start.1
  116.5 0.6 copy-start

commit v12 on v11

--- a/solution.py
+++ b/solution.py
@@ -148,8 +148,8 @@
 
 
 def contact_kernel(step, gather, scatter, *refs):
-    bodies_ref, frame_ref, state_ref, gaps_ref, steps_ref = refs[:5]
-    refs = refs[5:]
+    bodies_ref, frame_ref, current_ref, other_ref, gaps_ref, steps_ref = refs[:6]
+    refs = refs[6:]
     if gather:
         table_ref, refs = refs[0], refs[1:]
     outs = refs
@@ -179,11 +179,11 @@
         body = bodies_ref[side : side + 1, :]
         owner_hot.append((owner_ids == body // slots).astype(jnp.bfloat16))
         slot_hot.append((slot_ids == body % slots).astype(jnp.bfloat16))
-    current = state_ref[0:1, :]
+    current = current_ref[...]
     if step == 0:
-        shifted = current + MOMENTUM * (current - state_ref[1:2, :])
+        shifted = current + MOMENTUM * (current - other_ref[...])
     else:
-        shifted = state_ref[1:2, :]
+        shifted = other_ref[...]
     if gather:
         rate = None
         for side in range(2):
@@ -198,9 +198,10 @@
                 rate = term if rate is None else rate + term
         updated = jnp.maximum(shifted - steps_ref[step] * (gaps_ref[...] + rate), 0.0)
         shifted = updated + MOMENTUM * (updated - current)
-        outs[0][0:1, :] = updated
-        outs[0][1:2, :] = shifted
-        outs = outs[1:]
+        outs[0][...] = updated
+        if scatter:
+            outs[1][...] = shifted
+        outs = outs[1 + int(scatter):]
     if scatter:
         out_ref = outs[0]
         for k in range(6):
@@ -221,12 +222,12 @@
     gather = table is not None
     shapes = []
     if gather:
-        shapes.append(jax.ShapeDtypeStruct((2, contacts), jnp.float32))
+        shapes += [jax.ShapeDtypeStruct((1, contacts), jnp.float32)] * (1 + int(scatter))
     if scatter:
         shapes.append(jax.ShapeDtypeStruct((owners, 1, 6 * slots), jnp.float32))
-    args = (bodies, frame, state, gaps, steps) + ((table,) if gather else ())
+    args = (bodies, frame) + tuple(state) + (gaps, steps) + ((table,) if gather else ())
     vmem = pl.BlockSpec(memory_space=pltpu.VMEM)
-    specs = [vmem, vmem, vmem, vmem, pl.BlockSpec(memory_space=pltpu.SMEM)] + [vmem] * int(gather)
+    specs = [vmem] * 5 + [pl.BlockSpec(memory_space=pltpu.SMEM)] + [vmem] * int(gather)
     return pl.pallas_call(
         functools.partial(contact_kernel, step, gather, scatter),
         out_shape=tuple(shapes),
@@ -348,7 +349,7 @@
     body_count = own_rows * devices
     spread = jnp.broadcast_to(positions[:, :, None], (3, own_rows, 128))
     gaps_row = gaps.reshape(1, -1)
-    state = jnp.stack([impulse_now, impulse_prev])
+    state = (impulse_now.reshape(1, -1), impulse_prev.reshape(1, -1))
     (pieces,) = contact_step(0, devices, own_rows, contact_bodies, contact_frame, state, gaps_row, step_sizes)
     own_velocity = jnp.zeros((6, own_rows), jnp.float32)
     for k in range(ITERS):
@@ -372,10 +373,10 @@
         result = contact_step(
             k, devices, own_rows, contact_bodies, contact_frame, state, gaps_row, step_sizes, every.T, scatter=not last
         )
-        state = result[0]
+        state = result[:2]
         if not last:
-            pieces = result[1]
-    current = state[0]
+            pieces = result[2]
+    current = state[0].reshape(-1)
     return (current, own_velocity)
 
 

time: 183 us -> 181 us (0.989)
  no operation moved by 1% of the time
where the time goes in v12:
time: 181 us; the launch traced here: 180 us
  blocking collectives  108 us (60%)
  Pallas kernels  64.6 us (36%)
  local copies, waits for them, and re-layouts  6.17 us (3%)
    pallas_call x2, Pallas kernels, mobility_own(): pl.pallas_call(pair_kernel, out_shape=jax.ShapeDtypeStruct((6, own_rows),...  51.9 us
    all_to_all x2, blocking collectives, per_device(): pieces = lax.all_to_all(pieces, AXES, 0, 0, tiled=True)  40.2 us
    all_to_all x2, blocking collectives, per_device(): every = lax.all_to_all(every, AXES, 0, 0, tiled=True)  32.7 us
    all_to_all x1, blocking collectives, per_device(): lax.all_to_all(jnp.broadcast_to(block, (devices, 1, 9 * own_rows)), AXES,...  18.5 us
    all_to_all x1, blocking collectives, per_device(): lax.all_to_all(jnp.broadcast_to(block, (devices, 1, 6 * own_rows)), AXES,...  16.6 us
    pallas_call x3, Pallas kernels, contact_step(): pl.pallas_call(functools.partial(contact_kernel, step, gather, scatter),...  12.7 us

profile of v12, /device:TPU:1, one launch (start us, length us, event | category | flops | bytes accessed | tf_op | source)
XLA Modules:
  0.0 180.0 jit_solution(9034189120948495058)
XLA Ops:
  0.6 3.5 %shard_map.86 = f32[128,1,768]{2,1,0:T(1,128)} custom-call(s32[2,1024]{1,0:T(2,128)} %refs_0_.5, f32[9,1024]{1,0:T(8,128)} %refs_1_.5, f32[1,1024]{1,0:T(1,128)} %bitcast.23, f32[1,1024]{1,0:T(1,128)} %bitcast.25, f32[1,1024]{1,0:T(1,128)} %bitcast.27, f32[2]{0:T(128)} %refs_5_.5), custom_call_target="tpu_custom_call" | custom-call | flops 805306368 | bytes 2457600 | tf_op jit(solution)/shard_map/pallas_call | solution.py:231
  4.1 23.4 %all_to_all.38 = f32[128,1,768]{2,1,0:T(1,128)S(1)} all-to-all(f32[128,1,768]{2,1,0:T(1,128)} %shard_map.86), channel_id=1, replica_groups=mesh['src'=16,'tgt'=8] {'src','tgt'}, dimensions={0} | all-to-all | bytes 786432 | tf_op jit(solution)/shard_map/all_to_all | solution.py:356
  27.6 0.0 copy-start.2
  27.6 0.3 reduce_sum.18
  27.8 0.0 copy-start.1
  27.8 0.4 copy-done.2
  28.2 0.2 copy-done.1
  28.4 0.3 broadcast_in_dim.34
  28.7 18.5 %all_to_all.39.place_ref.force_ref = f32[128,1,1152]{2,1,0:T(1,128)} all-to-all(f32[128,1,1152]{2,1,0:T(1,128)S(1)} %broadcast_in_dim.34), channel_id=1, replica_groups=mesh['src'=16,'tgt'=8] {'src','tgt'}, dimensions={0} | all-to-all | bytes 1179648 | tf_op jit(solution)/shard_map/all_to_all | solution.py:360
  47.2 0.8 broadcast_in_dim.32.target_ref
  48.0 26.0 %shard_map.87 = f32[6,128]{1,0:T(8,128)} custom-call(f32[3,128,128]{2,1,0:T(8,128)} %broadcast_in_dim.32.target_ref, f32[128,1,1152]{2,1,0:T(1,128)} %all_to_all.39.place_ref.force_ref, f32[128,1,1152]{2,1,0:T(1,128)} %all_to_all.39.place_ref.force_ref, f32[6,128]{1,0:T(8,128)} %bitcast.20), custom_call_target="tpu_custom_call" | custom-call | flops 188743680 | bytes 786432 | tf_op jit(solution)/shard_map/pallas_call | solution.py:317
  74.0 0.9 broadcast_in_dim.36
  74.9 16.5 %all_to_all.40 = f32[128,1,768]{2,1,0:T(1,128)S(1)} all-to-all(f32[128,1,768]{2,1,0:T(1,128)S(1)} %broadcast_in_dim.36), channel_id=1, replica_groups=mesh['src'=16,'tgt'=8] {'src','tgt'}, dimensions={0} | all-to-all | bytes 786432 | tf_op jit(solution)/shard_map/all_to_all | solution.py:371
  91.4 1.1 copy.9
  92.5 5.6 %shard_map.88 = (f32[1,1024]{1,0:T(1,128)}, f32[1,1024]{1,0:T(1,128)}, f32[128,1,768]{2,1,0:T(1,128)}) custom-call(s32[2,1024]{1,0:T(2,128)} %refs_0_.5, f32[9,1024]{1,0:T(8,128)} %refs_1_.5, f32[1,1024]{1,0:T(1,128)} %bitcast.24, f32[1,1024]{1,0:T(1,128)} %bitcast.26, f32[1,1024]{1,0:T(1,128)} %bitcast.28, f32[2]{0:T(128)} %refs_5_.5, f32[768,128]{1,0:T(8,128)} %bitcast.16), custom_call_target="tpu_custom_call" | custom-call | flops 1610612736 | bytes 2457600 | tf_op jit(solution)/shard_map/pallas_call | solution.py:231
  98.1 16.8 %all_to_all.41 = f32[128,1,768]{2,1,0:T(1,128)S(1)} all-to-all(f32[128,1,768]{2,1,0:T(1,128)} %get-tuple-element.7), channel_id=1, replica_groups=mesh['src'=16,'tgt'=8] {'src','tgt'}, dimensions={0} | all-to-all | bytes 786432 | tf_op jit(solution)/shard_map/all_to_all | solution.py:356
  114.9 0.3 reduce_sum.19
  115.2 0.0 copy-start
  115.2 0.2 broadcast_in_dim.37
  115.4 0.4 copy-done
  115.8 16.6 %all_to_all.42.force_ref = f32[128,1,768]{2,1,0:T(1,128)} all-to-all(f32[128,1,768]{2,1,0:T(1,128)S(1)} %broadcast_in_dim.37), channel_id=1, replica_groups=mesh['src'=16,'tgt'=8] {'src','tgt'}, dimensions={0} | all-to-all | bytes 786432 | tf_op jit(solution)/shard_map/all_to_all | solution.py:366
  132.4 25.9 %shard_map.89 = f32[6,128]{1,0:T(8,128)} custom-call(f32[3,128,128]{2,1,0:T(8,128)} %broadcast_in_dim.32.target_ref, f32[128,1,1152]{2,1,0:T(1,128)} %all_to_all.39.place_ref.force_ref, f32[128,1,768]{2,1,0:T(1,128)} %all_to_all.42.force_ref, f32[6,128]{1,0:T(8,128)} %bitcast.18), custom_call_target="tpu_custom_call" | custom-call | flops 188743680 | bytes 786432 | tf_op jit(solution)/shard_map/pallas_call | solution.py:317
  158.3 0.9 broadcast_in_dim.39
  159.2 16.2 %all_to_all.43 = f32[128,1,768]{2,1,0:T(1,128)S(1)} all-to-all(f32[128,1,768]{2,1,0:T(1,128)S(1)} %broadcast_in_dim.39), channel_id=1, replica_groups=mesh['src'=16,'tgt'=8] {'src','tgt'}, dimensions={0} | all-to-all | bytes 786432 | tf_op jit(solution)/shard_map/all_to_all | solution.py:371
  175.4 1.1 copy.10
  176.5 3.5 %shard_map.90 = f32[1,1024]{1,0:T(1,128)} custom-call(s32[2,1024]{1,0:T(2,128)} %refs_0_.5, f32[9,1024]{1,0:T(8,128)} %refs_1_.5, f32[1,1024]{1,0:T(1,128)} %get-tuple-element.5.refs_2_, f32[1,1024]{1,0:T(1,128)} %get-tuple-element.6.refs_3_, f32[1,1024]{1,0:T(1,128)} %bitcast.29, f32[2]{0:T(128)} %refs_5_.5, f32[768,128]{1,0:T(8,128)} %bitcast.17), custom_call_target="tpu_custom_call" | custom-call | flops 805306368 | bytes 2457600 | tf_op jit(solution)/shard_map/pallas_call | solution.py:231
  (1 shorter events, 0.0 us)
Async XLA Ops:
  27.6 0.7 copy-start.2
  27.8 0.6 copy-start.1
  115.2 0.6 copy-start

commit v13 on v12

--- a/solution.py
+++ b/solution.py
@@ -264,15 +264,14 @@
             f_x, f_y, f_z = (lane_row(force, 0), lane_row(force, 1), lane_row(force, 2))
             t_x, t_y, t_z = (lane_row(force, 3), lane_row(force, 4), lane_row(force, 5))
             dist_sq = r_x * r_x + r_y * r_y + r_z * r_z
-            inverse = jnp.where(dist_sq > 0.0, lax.rsqrt(dist_sq), 0.0)
+            inverse = lax.rsqrt(jnp.maximum(dist_sq, 1.0))
             inverse_sq = inverse * inverse
-            inverse_cube = inverse_sq * inverse
-            inverse_fifth = inverse_cube * inverse_sq
-            c_cross = 0.75 * inverse_cube
-            c_iso = 0.75 * inverse + 0.5 * inverse_cube
-            c_dyad = c_cross - 1.5 * inverse_fifth
-            c_spin = 1.125 * inverse_fifth
-            c_self = 0.375 * inverse_cube
+            c_cross = inverse_sq * inverse
+            inverse_fifth = c_cross * inverse_sq
+            c_iso = inverse + (2.0 / 3.0) * c_cross
+            c_dyad = c_cross - 2.0 * inverse_fifth
+            c_spin = 1.5 * inverse_fifth
+            c_self = 0.5 * c_cross
             dyad = c_dyad * (r_x * f_x + r_y * f_y + r_z * f_z)
             spin = c_spin * (r_x * t_x + r_y * t_y + r_z * t_z)
             s_x = c_cross * r_x
@@ -307,7 +306,7 @@
                 ones, part, (((1,), (1,)), ((), ())), preferred_element_type=jnp.float32
             )
             total = term if total is None else total + term
-        scale = 1.0 if k < 3 else 0.75
+        scale = -0.25 if k < 3 else 1.125
         out_ref[k : k + 1, :] = total[0:1, :] + scale * own_ref[k : k + 1, :]
 
 
@@ -356,13 +355,13 @@
         pieces = lax.all_to_all(pieces, AXES, 0, 0, tiled=True)
         own_forces = jnp.sum(pieces, 0).reshape(6, own_rows)
         if k == 0:
-            block = jnp.concatenate([own_forces, positions]).reshape(1, 1, 9 * own_rows)
+            block = jnp.concatenate([0.75 * own_forces, positions]).reshape(1, 1, 9 * own_rows)
             places = lax.all_to_all(
                 jnp.broadcast_to(block, (devices, 1, 9 * own_rows)), AXES, 0, 0, tiled=True
             )
             forces = places
         else:
-            block = own_forces.reshape(1, 1, 6 * own_rows)
+            block = (0.75 * own_forces).reshape(1, 1, 6 * own_rows)
             forces = lax.all_to_all(
                 jnp.broadcast_to(block, (devices, 1, 6 * own_rows)), AXES, 0, 0, tiled=True
             )

time: 181 us -> 179 us (0.989)
  no operation moved by 1% of the time
where the time goes in v13:
time: 179 us
  blocking collectives  108 us (60%)
  Pallas kernels  63.1 us (35%)
  local copies, waits for them, and re-layouts  6.25 us (3%)
    pallas_call x2, Pallas kernels, mobility_own(): pl.pallas_call(pair_kernel, out_shape=jax.ShapeDtypeStruct((6, own_rows),...  50.5 us
    all_to_all x2, blocking collectives, per_device(): pieces = lax.all_to_all(pieces, AXES, 0, 0, tiled=True)  40.2 us
    all_to_all x2, blocking collectives, per_device(): every = lax.all_to_all(every, AXES, 0, 0, tiled=True)  32.7 us
    all_to_all x1, blocking collectives, per_device(): lax.all_to_all(jnp.broadcast_to(block, (devices, 1, 9 * own_rows)), AXES,...  18.5 us
    all_to_all x1, blocking collectives, per_device(): lax.all_to_all(jnp.broadcast_to(block, (devices, 1, 6 * own_rows)), AXES,...  16.6 us
    pallas_call x3, Pallas kernels, contact_step(): pl.pallas_call(functools.partial(contact_kernel, step, gather, scatter),...  12.7 us

profile of v13, /device:TPU:1, one launch (start us, length us, event | category | flops | bytes accessed | tf_op | source)
XLA Modules:
  0.0 178.6 jit_solution(14276006136543823116)
XLA Ops:
  0.6 3.5 %shard_map.86 = f32[128,1,768]{2,1,0:T(1,128)} custom-call(s32[2,1024]{1,0:T(2,128)} %refs_0_.5, f32[9,1024]{1,0:T(8,128)} %refs_1_.5, f32[1,1024]{1,0:T(1,128)} %bitcast.23, f32[1,1024]{1,0:T(1,128)} %bitcast.25, f32[1,1024]{1,0:T(1,128)} %bitcast.27, f32[2]{0:T(128)} %refs_5_.5), custom_call_target="tpu_custom_call" | custom-call | flops 805306368 | bytes 2457600 | tf_op jit(solution)/shard_map/pallas_call | solution.py:231
  4.1 23.4 %all_to_all.38 = f32[128,1,768]{2,1,0:T(1,128)S(1)} all-to-all(f32[128,1,768]{2,1,0:T(1,128)} %shard_map.86), channel_id=1, replica_groups=mesh['src'=16,'tgt'=8] {'src','tgt'}, dimensions={0} | all-to-all | bytes 786432 | tf_op jit(solution)/shard_map/all_to_all | solution.py:355
  27.6 0.3 reduce_sum.18
  27.8 0.0 copy-start
  27.8 0.0 copy-start.2
  27.9 0.6 copy-done
  28.4 0.1 copy-done.2
  28.5 0.3 broadcast_in_dim.34
  28.9 18.5 %all_to_all.39.place_ref.force_ref = f32[128,1,1152]{2,1,0:T(1,128)} all-to-all(f32[128,1,1152]{2,1,0:T(1,128)S(1)} %broadcast_in_dim.34), channel_id=1, replica_groups=mesh['src'=16,'tgt'=8] {'src','tgt'}, dimensions={0} | all-to-all | bytes 1179648 | tf_op jit(solution)/shard_map/all_to_all | solution.py:359
  47.3 0.8 broadcast_in_dim.32.target_ref
  48.1 25.3 %shard_map.87 = f32[6,128]{1,0:T(8,128)} custom-call(f32[3,128,128]{2,1,0:T(8,128)} %broadcast_in_dim.32.target_ref, f32[128,1,1152]{2,1,0:T(1,128)} %all_to_all.39.place_ref.force_ref, f32[128,1,1152]{2,1,0:T(1,128)} %all_to_all.39.place_ref.force_ref, f32[6,128]{1,0:T(8,128)} %bitcast.19), custom_call_target="tpu_custom_call" | custom-call | flops 188743680 | bytes 786432 | tf_op jit(solution)/shard_map/pallas_call | solution.py:316
  73.4 0.9 broadcast_in_dim.36
  74.3 16.5 %all_to_all.40 = f32[128,1,768]{2,1,0:T(1,128)S(1)} all-to-all(f32[128,1,768]{2,1,0:T(1,128)S(1)} %broadcast_in_dim.36), channel_id=1, replica_groups=mesh['src'=16,'tgt'=8] {'src','tgt'}, dimensions={0} | all-to-all | bytes 786432 | tf_op jit(solution)/shard_map/all_to_all | solution.py:370
  90.7 1.1 copy.9
  91.8 5.6 %shard_map.88 = (f32[1,1024]{1,0:T(1,128)}, f32[1,1024]{1,0:T(1,128)}, f32[128,1,768]{2,1,0:T(1,128)}) custom-call(s32[2,1024]{1,0:T(2,128)} %refs_0_.5, f32[9,1024]{1,0:T(8,128)} %refs_1_.5, f32[1,1024]{1,0:T(1,128)} %bitcast.24, f32[1,1024]{1,0:T(1,128)} %bitcast.26, f32[1,1024]{1,0:T(1,128)} %bitcast.28, f32[2]{0:T(128)} %refs_5_.5, f32[768,128]{1,0:T(8,128)} %bitcast.17), custom_call_target="tpu_custom_call" | custom-call | flops 1610612736 | bytes 2457600 | tf_op jit(solution)/shard_map/pallas_call | solution.py:231
  97.4 16.8 %all_to_all.41 = f32[128,1,768]{2,1,0:T(1,128)S(1)} all-to-all(f32[128,1,768]{2,1,0:T(1,128)} %get-tuple-element.7), channel_id=1, replica_groups=mesh['src'=16,'tgt'=8] {'src','tgt'}, dimensions={0} | all-to-all | bytes 786432 | tf_op jit(solution)/shard_map/all_to_all | solution.py:355
  114.2 0.3 reduce_sum.19
  114.5 0.0 copy-start.1
  114.5 0.2 broadcast_in_dim.37
  114.7 0.4 copy-done.1
  115.1 16.6 %all_to_all.42.force_ref = f32[128,1,768]{2,1,0:T(1,128)} all-to-all(f32[128,1,768]{2,1,0:T(1,128)S(1)} %broadcast_in_dim.37), channel_id=1, replica_groups=mesh['src'=16,'tgt'=8] {'src','tgt'}, dimensions={0} | all-to-all | bytes 786432 | tf_op jit(solution)/shard_map/all_to_all | solution.py:365
  131.7 25.2 %shard_map.89 = f32[6,128]{1,0:T(8,128)} custom-call(f32[3,128,128]{2,1,0:T(8,128)} %broadcast_in_dim.32.target_ref, f32[128,1,1152]{2,1,0:T(1,128)} %all_to_all.39.place_ref.force_ref, f32[128,1,768]{2,1,0:T(1,128)} %all_to_all.42.force_ref, f32[6,128]{1,0:T(8,128)} %bitcast.20), custom_call_target="tpu_custom_call" | custom-call | flops 188743680 | bytes 786432 | tf_op jit(solution)/shard_map/pallas_call | solution.py:316
  156.9 0.9 broadcast_in_dim.39
  157.8 16.2 %all_to_all.43 = f32[128,1,768]{2,1,0:T(1,128)S(1)} all-to-all(f32[128,1,768]{2,1,0:T(1,128)S(1)} %broadcast_in_dim.39), channel_id=1, replica_groups=mesh['src'=16,'tgt'=8] {'src','tgt'}, dimensions={0} | all-to-all | bytes 786432 | tf_op jit(solution)/shard_map/all_to_all | solution.py:370
  174.0 1.1 copy.10
  175.1 3.5 %shard_map.90 = f32[1,1024]{1,0:T(1,128)} custom-call(s32[2,1024]{1,0:T(2,128)} %refs_0_.5, f32[9,1024]{1,0:T(8,128)} %refs_1_.5, f32[1,1024]{1,0:T(1,128)} %get-tuple-element.5.refs_2_, f32[1,1024]{1,0:T(1,128)} %get-tuple-element.6.refs_3_, f32[1,1024]{1,0:T(1,128)} %bitcast.29, f32[2]{0:T(128)} %refs_5_.5, f32[768,128]{1,0:T(8,128)} %bitcast.18), custom_call_target="tpu_custom_call" | custom-call | flops 805306368 | bytes 2457600 | tf_op jit(solution)/shard_map/pallas_call | solution.py:231
  (3 shorter events, 0.0 us)
Async XLA Ops:
  27.8 0.6 copy-start
  27.8 0.7 copy-start.2
  114.5 0.6 copy-start.1

commit v14 on v13

--- a/solution.py
+++ b/solution.py
@@ -147,15 +147,17 @@
     return (high, low)
 
 
-def contact_kernel(step, gather, scatter, *refs):
+def contact_kernel(step, gather, scatter, carry, *refs):
     bodies_ref, frame_ref, current_ref, other_ref, gaps_ref, steps_ref = refs[:6]
     refs = refs[6:]
     if gather:
         table_ref, refs = refs[0], refs[1:]
+    if carry:
+        places_ref, refs = refs[0], refs[1:]
     outs = refs
     contacts = frame_ref.shape[1]
     owners = outs[-1].shape[0] if scatter else table_ref.shape[1]
-    slots = outs[-1].shape[2] // 6 if scatter else table_ref.shape[0] // 6
+    slots = table_ref.shape[0] // 6 if gather else outs[-1].shape[2] // (9 if carry else 6)
     frame = frame_ref[...]
     normal = (frame[0:1], frame[1:2], frame[2:3])
 
@@ -215,21 +217,27 @@
                     )
                     total = term if total is None else total + term
             out_ref[:, 0, k * slots : (k + 1) * slots] = total
-
-
-def contact_step(step, owners, slots, bodies, frame, state, gaps, steps, table=None, scatter=True):
+        if carry:
+            for c in range(3):
+                row = places_ref[c : c + 1, :]
+                out_ref[:, 0, (6 + c) * slots : (7 + c) * slots] = jnp.broadcast_to(row, (owners, slots))
+
+
+def contact_step(step, owners, slots, bodies, frame, state, gaps, steps, table=None, scatter=True, places=None):
     contacts = frame.shape[1]
     gather = table is not None
     shapes = []
     if gather:
         shapes += [jax.ShapeDtypeStruct((1, contacts), jnp.float32)] * (1 + int(scatter))
+    carry = places is not None
     if scatter:
-        shapes.append(jax.ShapeDtypeStruct((owners, 1, 6 * slots), jnp.float32))
+        shapes.append(jax.ShapeDtypeStruct((owners, 1, (9 if carry else 6) * slots), jnp.float32))
     args = (bodies, frame) + tuple(state) + (gaps, steps) + ((table,) if gather else ())
+    args += (places,) if carry else ()
     vmem = pl.BlockSpec(memory_space=pltpu.VMEM)
-    specs = [vmem] * 5 + [pl.BlockSpec(memory_space=pltpu.SMEM)] + [vmem] * int(gather)
+    specs = [vmem] * 5 + [pl.BlockSpec(memory_space=pltpu.SMEM)] + [vmem] * (int(gather) + int(carry))
     return pl.pallas_call(
-        functools.partial(contact_kernel, step, gather, scatter),
+        functools.partial(contact_kernel, step, gather, scatter, carry),
         out_shape=tuple(shapes),
         in_specs=specs,
         out_specs=tuple(vmem for _ in shapes),
@@ -349,22 +357,19 @@
     spread = jnp.broadcast_to(positions[:, :, None], (3, own_rows, 128))
     gaps_row = gaps.reshape(1, -1)
     state = (impulse_now.reshape(1, -1), impulse_prev.reshape(1, -1))
-    (pieces,) = contact_step(0, devices, own_rows, contact_bodies, contact_frame, state, gaps_row, step_sizes)
+    (pieces,) = contact_step(
+        0, devices, own_rows, contact_bodies, contact_frame, state, gaps_row, step_sizes, places=positions
+    )
     own_velocity = jnp.zeros((6, own_rows), jnp.float32)
     for k in range(ITERS):
         pieces = lax.all_to_all(pieces, AXES, 0, 0, tiled=True)
-        own_forces = jnp.sum(pieces, 0).reshape(6, own_rows)
         if k == 0:
-            block = jnp.concatenate([0.75 * own_forces, positions]).reshape(1, 1, 9 * own_rows)
-            places = lax.all_to_all(
-                jnp.broadcast_to(block, (devices, 1, 9 * own_rows)), AXES, 0, 0, tiled=True
-            )
-            forces = places
-        else:
-            block = (0.75 * own_forces).reshape(1, 1, 6 * own_rows)
-            forces = lax.all_to_all(
-                jnp.broadcast_to(block, (devices, 1, 6 * own_rows)), AXES, 0, 0, tiled=True
-            )
+            places = pieces
+        own_forces = jnp.sum(pieces[:, :, : 6 * own_rows], 0).reshape(6, own_rows)
+        block = (0.75 * own_forces).reshape(1, 1, 6 * own_rows)
+        forces = lax.all_to_all(
+            jnp.broadcast_to(block, (devices, 1, 6 * own_rows)), AXES, 0, 0, tiled=True
+        )
         own_velocity = mobility_own(spread, places, forces, own_forces)
         every = jnp.broadcast_to(own_velocity.reshape(1, 6 * own_rows), (devices, 6 * own_rows))
         every = lax.all_to_all(every, AXES, 0, 0, tiled=True)

time: 179 us -> 179 us (level)
    all_to_all x1 -> x0, blocking collectives: 18.5 us -> none  [per_device(): lax.all_to_all(jnp.broadcast_to(block, (devices, 1, 9 * own_rows)), AXES,...]
    all_to_all x1 -> x2, blocking collectives: 16.6 us -> 33.4 us  [per_device(): lax.all_to_all(jnp.broadcast_to(block, (devices, 1, 6 * own_rows)), AXES,...]
    all_to_all x2, blocking collectives: 40.2 us -> 42 us  [per_device(): pieces = lax.all_to_all(pieces, AXES, 0, 0, tiled=True)]
where the time goes in v14:
time: 179 us; the launch traced here: 178 us
  blocking collectives  108 us (60%)
  Pallas kernels  63.2 us (35%)
  local copies, waits for them, and re-layouts  5.85 us (3%)
    pallas_call x2, Pallas kernels, mobility_own(): pl.pallas_call(pair_kernel, out_shape=jax.ShapeDtypeStruct((6, own_rows),...  50.4 us
    all_to_all x2, blocking collectives, per_device(): pieces = lax.all_to_all(pieces, AXES, 0, 0, tiled=True)  42 us
    all_to_all x2, blocking collectives, per_device(): lax.all_to_all(jnp.broadcast_to(block, (devices, 1, 6 * own_rows)), AXES,...  33.4 us
    all_to_all x2, blocking collectives, per_device(): every = lax.all_to_all(every, AXES, 0, 0, tiled=True)  32.4 us
    pallas_call x3, Pallas kernels, contact_step(): pl.pallas_call(functools.partial(contact_kernel, step, gather, scatter, c...  12.8 us

profile of v14, /device:TPU:1, one launch (start us, length us, event | category | flops | bytes accessed | tf_op | source)
XLA Modules:
  0.0 178.1 jit_solution(10728355389206201413)
XLA Ops:
  0.6 3.6 %shard_map.86 = f32[128,1,1152]{2,1,0:T(1,128)} custom-call(s32[2,1024]{1,0:T(2,128)} %refs_0_.5, f32[9,1024]{1,0:T(8,128)} %refs_1_.5, f32[1,1024]{1,0:T(1,128)} %bitcast.20, f32[1,1024]{1,0:T(1,128)} %bitcast.22, f32[1,1024]{1,0:T(1,128)} %bitcast.24, f32[2]{0:T(128)} %refs_5_.5, f32[3,128]{1,0:T(4,128)} %refs_6_.1), custom_call_target="tpu_custom_call" | custom-call | flops 805306368 | bytes 2457600 | tf_op jit(solution)/shard_map/pallas_call | solution.py:239
  4.2 25.3 %all_to_all.38.place_ref = f32[128,1,1152]{2,1,0:T(1,128)S(1)} all-to-all(f32[128,1,1152]{2,1,0:T(1,128)} %shard_map.86), channel_id=1, replica_groups=mesh['src'=16,'tgt'=8] {'src','tgt'}, dimensions={0} | all-to-all | bytes 1179648 | tf_op jit(solution)/shard_map/all_to_all | solution.py:365
  29.5 0.0 copy-start
  29.5 0.2 slice_reduce_fusion
  29.7 0.0 copy-start.2
  29.7 0.2 broadcast_in_dim.15
  29.9 0.4 copy-done.2
  30.3 0.0 copy-start.3
  30.3 16.8 %all_to_all.39.force_ref = f32[128,1,768]{2,1,0:T(1,128)} all-to-all(f32[128,1,768]{2,1,0:T(1,128)S(1)} %broadcast_in_dim.15), channel_id=1, replica_groups=mesh['src'=16,'tgt'=8] {'src','tgt'}, dimensions={0} | all-to-all | bytes 786432 | tf_op jit(solution)/shard_map/all_to_all | solution.py:370
  47.1 0.0 copy-done
  47.1 0.0 copy-done.3
  47.1 0.8 broadcast_in_dim.14.target_ref
  47.9 25.2 %shard_map.87 = f32[6,128]{1,0:T(8,128)} custom-call(f32[3,128,128]{2,1,0:T(8,128)} %broadcast_in_dim.14.target_ref, f32[128,1,1152]{2,1,0:T(1,128)} %copy-done, f32[128,1,768]{2,1,0:T(1,128)} %all_to_all.39.force_ref, f32[6,128]{1,0:T(8,128)} %bitcast.17), custom_call_target="tpu_custom_call" | custom-call | flops 188743680 | bytes 786432 | tf_op jit(solution)/shard_map/pallas_call | solution.py:324
  73.1 0.9 broadcast_in_dim.33
  74.0 16.2 %all_to_all.40 = f32[128,1,768]{2,1,0:T(1,128)S(1)} all-to-all(f32[128,1,768]{2,1,0:T(1,128)S(1)} %broadcast_in_dim.33), channel_id=1, replica_groups=mesh['src'=16,'tgt'=8] {'src','tgt'}, dimensions={0} | all-to-all | bytes 786432 | tf_op jit(solution)/shard_map/all_to_all | solution.py:375
  90.2 1.1 copy.9
  91.2 5.6 %shard_map.88 = (f32[1,1024]{1,0:T(1,128)}, f32[1,1024]{1,0:T(1,128)}, f32[128,1,768]{2,1,0:T(1,128)}) custom-call(s32[2,1024]{1,0:T(2,128)} %refs_0_.5, f32[9,1024]{1,0:T(8,128)} %refs_1_.5, f32[1,1024]{1,0:T(1,128)} %bitcast.21, f32[1,1024]{1,0:T(1,128)} %bitcast.23, f32[1,1024]{1,0:T(1,128)} %bitcast.25, f32[2]{0:T(128)} %refs_5_.5, f32[768,128]{1,0:T(8,128)} %bitcast.14), custom_call_target="tpu_custom_call" | custom-call | flops 1610612736 | bytes 2457600 | tf_op jit(solution)/shard_map/pallas_call | solution.py:239
  96.9 16.8 %all_to_all.41 = f32[128,1,768]{2,1,0:T(1,128)S(1)} all-to-all(f32[128,1,768]{2,1,0:T(1,128)} %get-tuple-element.7), channel_id=1, replica_groups=mesh['src'=16,'tgt'=8] {'src','tgt'}, dimensions={0} | all-to-all | bytes 786432 | tf_op jit(solution)/shard_map/all_to_all | solution.py:365
  113.7 0.3 reduce_sum.19
  114.0 0.0 copy-start.1
  114.0 0.2 broadcast_in_dim.34
  114.2 0.4 copy-done.1
  114.6 16.6 %all_to_all.42.force_ref = f32[128,1,768]{2,1,0:T(1,128)} all-to-all(f32[128,1,768]{2,1,0:T(1,128)S(1)} %broadcast_in_dim.34), channel_id=1, replica_groups=mesh['src'=16,'tgt'=8] {'src','tgt'}, dimensions={0} | all-to-all | bytes 786432 | tf_op jit(solution)/shard_map/all_to_all | solution.py:370
  131.2 25.2 %shard_map.89 = f32[6,128]{1,0:T(8,128)} custom-call(f32[3,128,128]{2,1,0:T(8,128)} %broadcast_in_dim.14.target_ref, f32[128,1,1152]{2,1,0:T(1,128)} %copy-done, f32[128,1,768]{2,1,0:T(1,128)} %all_to_all.42.force_ref, f32[6,128]{1,0:T(8,128)} %bitcast.16), custom_call_target="tpu_custom_call" | custom-call | flops 188743680 | bytes 786432 | tf_op jit(solution)/shard_map/pallas_call | solution.py:324
  156.4 0.9 broadcast_in_dim.36
  157.3 16.2 %all_to_all.43 = f32[128,1,768]{2,1,0:T(1,128)S(1)} all-to-all(f32[128,1,768]{2,1,0:T(1,128)S(1)} %broadcast_in_dim.36), channel_id=1, replica_groups=mesh['src'=16,'tgt'=8] {'src','tgt'}, dimensions={0} | all-to-all | bytes 786432 | tf_op jit(solution)/shard_map/all_to_all | solution.py:375
  173.5 1.1 copy.10
  174.5 3.5 %shard_map.90 = f32[1,1024]{1,0:T(1,128)} custom-call(s32[2,1024]{1,0:T(2,128)} %refs_0_.5, f32[9,1024]{1,0:T(8,128)} %refs_1_.5, f32[1,1024]{1,0:T(1,128)} %get-tuple-element.5.refs_2_, f32[1,1024]{1,0:T(1,128)} %get-tuple-element.6.refs_3_, f32[1,1024]{1,0:T(1,128)} %bitcast.26, f32[2]{0:T(128)} %refs_5_.5, f32[768,128]{1,0:T(8,128)} %bitcast.15), custom_call_target="tpu_custom_call" | custom-call | flops 805306368 | bytes 2457600 | tf_op jit(solution)/shard_map/pallas_call | solution.py:239
  (2 shorter events, 0.0 us)
Async XLA Ops:
  29.5 17.6 %copy-start = (f32[128,1,1152]{2,1,0:T(1,128)}, f32[128,1,1152]{2,1,0:T(1,128)S(1)}, u32[]{:S(2)}) copy-start(f32[128,1,1152]{2,1,0:T(1,128)S(1)} %all_to_all.38.place_ref) | copy-start | bytes 1769476
  29.7 0.6 copy-start.2
  30.3 16.8 %copy-start.3 = (f32[3,128]{1,0:T(4,128)S(1)}, f32[3,128]{1,0:T(4,128)}, u32[]{:S(2)}) copy-start(f32[3,128]{1,0:T(4,128)} %refs_6_.1) | copy-start | bytes 4612
  114.0 0.6 copy-start.1

commit v15 on v13

--- a/solution.py
+++ b/solution.py
@@ -154,8 +154,8 @@
         table_ref, refs = refs[0], refs[1:]
     outs = refs
     contacts = frame_ref.shape[1]
-    owners = outs[-1].shape[0] if scatter else table_ref.shape[1]
-    slots = outs[-1].shape[2] // 6 if scatter else table_ref.shape[0] // 6
+    owners = outs[-1].shape[0] if scatter else table_ref.shape[0]
+    slots = outs[-1].shape[2] // 6 if scatter else table_ref.shape[2] // 6
     frame = frame_ref[...]
     normal = (frame[0:1], frame[1:2], frame[2:3])
 
@@ -190,8 +190,11 @@
             slot_wide = slot_hot[side].astype(jnp.float32)
             for k in range(6):
                 picked = None
-                for part in split_pair(table_ref[k * slots : (k + 1) * slots, :]):
-                    term = jnp.dot(part, owner_hot[side], preferred_element_type=jnp.float32)
+                for part in split_pair(table_ref[:, 0, k * slots : (k + 1) * slots]):
+                    term = lax.dot_general(
+                        part, owner_hot[side], (((0,), (0,)), ((), ())),
+                        preferred_element_type=jnp.float32,
+                    )
                     picked = term if picked is None else picked + term
                 velocity = jnp.sum(picked * slot_wide, axis=0, keepdims=True)
                 term = rows[side][k] * velocity
@@ -366,11 +369,11 @@
                 jnp.broadcast_to(block, (devices, 1, 6 * own_rows)), AXES, 0, 0, tiled=True
             )
         own_velocity = mobility_own(spread, places, forces, own_forces)
-        every = jnp.broadcast_to(own_velocity.reshape(1, 6 * own_rows), (devices, 6 * own_rows))
+        every = jnp.broadcast_to(own_velocity.reshape(1, 1, 6 * own_rows), (devices, 1, 6 * own_rows))
         every = lax.all_to_all(every, AXES, 0, 0, tiled=True)
         last = k == ITERS - 1
         result = contact_step(
-            k, devices, own_rows, contact_bodies, contact_frame, state, gaps_row, step_sizes, every.T, scatter=not last
+            k, devices, own_rows, contact_bodies, contact_frame, state, gaps_row, step_sizes, every, scatter=not last
         )
         state = result[:2]
         if not last:

time: 179 us -> 179 us (level)
  local copies, waits for them, and re-layouts: 6.25 us -> 4.13 us
    all_to_all x2 -> x0, local copies, waits for them, and re-layouts: 2.12 us -> none  [per_device(): every = lax.all_to_all(every, AXES, 0, 0, tiled=True)]
where the time goes in v15:
time: 179 us
  blocking collectives  109 us (61%)
  Pallas kernels  64.8 us (36%)
  local copies, waits for them, and re-layouts  4.13 us (2%)
    pallas_call x2, Pallas kernels, mobility_own(): pl.pallas_call(pair_kernel, out_shape=jax.ShapeDtypeStruct((6, own_rows),...  50.5 us
    all_to_all x2, blocking collectives, per_device(): pieces = lax.all_to_all(pieces, AXES, 0, 0, tiled=True)  40.2 us
    all_to_all x2, blocking collectives, per_device(): every = lax.all_to_all(every, AXES, 0, 0, tiled=True)  33.3 us
    all_to_all x1, blocking collectives, per_device(): lax.all_to_all(jnp.broadcast_to(block, (devices, 1, 9 * own_rows)), AXES,...  18.5 us
    all_to_all x1, blocking collectives, per_device(): lax.all_to_all(jnp.broadcast_to(block, (devices, 1, 6 * own_rows)), AXES,...  16.6 us
    pallas_call x3, Pallas kernels, contact_step(): pl.pallas_call(functools.partial(contact_kernel, step, gather, scatter),...  14.3 us

profile of v15, /device:TPU:1, one launch (start us, length us, event | category | flops | bytes accessed | tf_op | source)
XLA Modules:
  0.0 178.8 jit_solution(8008774132833601820)
XLA Ops:
  0.6 3.5 %shard_map.86 = f32[128,1,768]{2,1,0:T(1,128)} custom-call(s32[2,1024]{1,0:T(2,128)} %refs_0_.5, f32[9,1024]{1,0:T(8,128)} %refs_1_.5, f32[1,1024]{1,0:T(1,128)} %bitcast.15, f32[1,1024]{1,0:T(1,128)} %bitcast.17, f32[1,1024]{1,0:T(1,128)} %bitcast.19, f32[2]{0:T(128)} %refs_5_.5), custom_call_target="tpu_custom_call" | custom-call | flops 805306368 | bytes 2457600 | tf_op jit(solution)/shard_map/pallas_call | solution.py:234
  4.1 23.4 %all_to_all.30 = f32[128,1,768]{2,1,0:T(1,128)S(1)} all-to-all(f32[128,1,768]{2,1,0:T(1,128)} %shard_map.86), channel_id=1, replica_groups=mesh['src'=16,'tgt'=8] {'src','tgt'}, dimensions={0} | all-to-all | bytes 786432 | tf_op jit(solution)/shard_map/all_to_all | solution.py:358
  27.6 0.3 reduce_sum.18
  27.8 0.0 copy-start
  27.8 0.0 copy-start.2
  27.9 0.6 copy-done
  28.4 0.1 copy-done.2
  28.5 0.3 broadcast_in_dim.34
  28.9 18.5 %all_to_all.31.place_ref.force_ref = f32[128,1,1152]{2,1,0:T(1,128)} all-to-all(f32[128,1,1152]{2,1,0:T(1,128)S(1)} %broadcast_in_dim.34), channel_id=1, replica_groups=mesh['src'=16,'tgt'=8] {'src','tgt'}, dimensions={0} | all-to-all | bytes 1179648 | tf_op jit(solution)/shard_map/all_to_all | solution.py:362
  47.3 0.8 broadcast_in_dim.32.target_ref
  48.1 25.3 %shard_map.87 = f32[6,128]{1,0:T(8,128)} custom-call(f32[3,128,128]{2,1,0:T(8,128)} %broadcast_in_dim.32.target_ref, f32[128,1,1152]{2,1,0:T(1,128)} %all_to_all.31.place_ref.force_ref, f32[128,1,1152]{2,1,0:T(1,128)} %all_to_all.31.place_ref.force_ref, f32[6,128]{1,0:T(8,128)} %bitcast.11), custom_call_target="tpu_custom_call" | custom-call | flops 188743680 | bytes 786432 | tf_op jit(solution)/shard_map/pallas_call | solution.py:319
  73.4 0.9 broadcast_in_dim.36
  74.3 16.7 %all_to_all.32.refs_6_ = f32[128,1,768]{2,1,0:T(1,128)} all-to-all(f32[128,1,768]{2,1,0:T(1,128)S(1)} %broadcast_in_dim.36), channel_id=1, replica_groups=mesh['src'=16,'tgt'=8] {'src','tgt'}, dimensions={0} | all-to-all | bytes 786432 | tf_op jit(solution)/shard_map/all_to_all | solution.py:373
  90.9 6.5 %shard_map.88 = (f32[1,1024]{1,0:T(1,128)}, f32[1,1024]{1,0:T(1,128)}, f32[128,1,768]{2,1,0:T(1,128)}) custom-call(s32[2,1024]{1,0:T(2,128)} %refs_0_.5, f32[9,1024]{1,0:T(8,128)} %refs_1_.5, f32[1,1024]{1,0:T(1,128)} %bitcast.16, f32[1,1024]{1,0:T(1,128)} %bitcast.18, f32[1,1024]{1,0:T(1,128)} %bitcast.20, f32[2]{0:T(128)} %refs_5_.5, ...), custom_call_target="tpu_custom_call" | custom-call | flops 1610612736 | bytes 2457600 | tf_op jit(solution)/shard_map/pallas_call | solution.py:234
  97.4 16.8 %all_to_all.33 = f32[128,1,768]{2,1,0:T(1,128)S(1)} all-to-all(f32[128,1,768]{2,1,0:T(1,128)} %get-tuple-element.7), channel_id=1, replica_groups=mesh['src'=16,'tgt'=8] {'src','tgt'}, dimensions={0} | all-to-all | bytes 786432 | tf_op jit(solution)/shard_map/all_to_all | solution.py:358
  114.2 0.3 reduce_sum.19
  114.5 0.0 copy-start.1
  114.5 0.2 broadcast_in_dim.37
  114.7 0.4 copy-done.1
  115.1 16.6 %all_to_all.34.force_ref = f32[128,1,768]{2,1,0:T(1,128)} all-to-all(f32[128,1,768]{2,1,0:T(1,128)S(1)} %broadcast_in_dim.37), channel_id=1, replica_groups=mesh['src'=16,'tgt'=8] {'src','tgt'}, dimensions={0} | all-to-all | bytes 786432 | tf_op jit(solution)/shard_map/all_to_all | solution.py:368
  131.7 25.2 %shard_map.89 = f32[6,128]{1,0:T(8,128)} custom-call(f32[3,128,128]{2,1,0:T(8,128)} %broadcast_in_dim.32.target_ref, f32[128,1,1152]{2,1,0:T(1,128)} %all_to_all.31.place_ref.force_ref, f32[128,1,768]{2,1,0:T(1,128)} %all_to_all.34.force_ref, f32[6,128]{1,0:T(8,128)} %bitcast.12), custom_call_target="tpu_custom_call" | custom-call | flops 188743680 | bytes 786432 | tf_op jit(solution)/shard_map/pallas_call | solution.py:319
  156.9 0.9 broadcast_in_dim.39
  157.8 16.6 %all_to_all.35.refs_6_ = f32[128,1,768]{2,1,0:T(1,128)} all-to-all(f32[128,1,768]{2,1,0:T(1,128)S(1)} %broadcast_in_dim.39), channel_id=1, replica_groups=mesh['src'=16,'tgt'=8] {'src','tgt'}, dimensions={0} | all-to-all | bytes 786432 | tf_op jit(solution)/shard_map/all_to_all | solution.py:373
  174.4 4.4 %shard_map.90 = f32[1,1024]{1,0:T(1,128)} custom-call(s32[2,1024]{1,0:T(2,128)} %refs_0_.5, f32[9,1024]{1,0:T(8,128)} %refs_1_.5, f32[1,1024]{1,0:T(1,128)} %get-tuple-element.5.refs_2_, f32[1,1024]{1,0:T(1,128)} %get-tuple-element.6.refs_3_, f32[1,1024]{1,0:T(1,128)} %bitcast.21, f32[2]{0:T(128)} %refs_5_.5, f32[128,1,768]{2,1,0:T(1,128)} %all_to_all.35.refs_6_), custom_call_target="tpu_custom_call" | custom-call | flops 805306368 | bytes 2457600 | tf_op jit(solution)/shard_map/pallas_call | solution.py:234
  (3 shorter events, 0.0 us)
Async XLA Ops:
  27.8 0.6 copy-start
  27.8 0.7 copy-start.2
  114.5 0.6 copy-start.1

commit v16 on v13

--- a/solution.py
+++ b/solution.py
@@ -172,30 +172,29 @@
         tuple(-v for v in normal) + tuple(-v for v in first_lever),
         normal + second_lever,
     )
-    owner_ids = lax.broadcasted_iota(jnp.int32, (owners, contacts), 0)
-    slot_ids = lax.broadcasted_iota(jnp.int32, (slots, contacts), 0)
-    owner_hot, slot_hot = [], []
-    for side in range(2):
-        body = bodies_ref[side : side + 1, :]
-        owner_hot.append((owner_ids == body // slots).astype(jnp.bfloat16))
-        slot_hot.append((slot_ids == body % slots).astype(jnp.bfloat16))
+    owner_ids = lax.broadcasted_iota(jnp.int32, (owners, 2 * contacts), 0)
+    slot_ids = lax.broadcasted_iota(jnp.int32, (slots, 2 * contacts), 0)
+    body = jnp.concatenate([bodies_ref[0:1, :], bodies_ref[1:2, :]], axis=1)
+    owner_hot = (owner_ids == body // slots).astype(jnp.bfloat16)
+    slot_hot = (slot_ids == body % slots).astype(jnp.bfloat16)
+    end_rows = [jnp.concatenate([rows[0][k], rows[1][k]], axis=1) for k in range(6)]
     current = current_ref[...]
     if step == 0:
         shifted = current + MOMENTUM * (current - other_ref[...])
     else:
         shifted = other_ref[...]
     if gather:
+        slot_wide = slot_hot.astype(jnp.float32)
         rate = None
-        for side in range(2):
-            slot_wide = slot_hot[side].astype(jnp.float32)
-            for k in range(6):
-                picked = None
-                for part in split_pair(table_ref[k * slots : (k + 1) * slots, :]):
-                    term = jnp.dot(part, owner_hot[side], preferred_element_type=jnp.float32)
-                    picked = term if picked is None else picked + term
-                velocity = jnp.sum(picked * slot_wide, axis=0, keepdims=True)
-                term = rows[side][k] * velocity
-                rate = term if rate is None else rate + term
+        for k in range(6):
+            picked = None
+            for part in split_pair(table_ref[k * slots : (k + 1) * slots, :]):
+                term = jnp.dot(part, owner_hot, preferred_element_type=jnp.float32)
+                picked = term if picked is None else picked + term
+            velocity = jnp.sum(picked * slot_wide, axis=0, keepdims=True)
+            term = end_rows[k] * velocity
+            rate = term if rate is None else rate + term
+        rate = rate[:, :contacts] + rate[:, contacts:]
         updated = jnp.maximum(shifted - steps_ref[step] * (gaps_ref[...] + rate), 0.0)
         shifted = updated + MOMENTUM * (updated - current)
         outs[0][...] = updated
@@ -204,16 +203,16 @@
         outs = outs[1 + int(scatter):]
     if scatter:
         out_ref = outs[0]
+        both = jnp.concatenate([shifted, shifted], axis=1)
         for k in range(6):
             total = None
-            for side in range(2):
-                for part in split_pair(rows[side][k] * shifted):
-                    weighted = slot_hot[side] * part
-                    term = lax.dot_general(
-                        owner_hot[side], weighted, (((1,), (1,)), ((), ())),
-                        preferred_element_type=jnp.float32,
-                    )
-                    total = term if total is None else total + term
+            for part in split_pair(end_rows[k] * both):
+                weighted = slot_hot * part
+                term = lax.dot_general(
+                    owner_hot, weighted, (((1,), (1,)), ((), ())),
+                    preferred_element_type=jnp.float32,
+                )
+                total = term if total is None else total + term
             out_ref[:, 0, k * slots : (k + 1) * slots] = total
 
 

time: 179 us -> 179 us (level)
  no operation moved by 1% of the time
where the time goes in v16:
time: 179 us
  blocking collectives  108 us (60%)
  Pallas kernels  63.2 us (35%)
  local copies, waits for them, and re-layouts  6.25 us (3%)
    pallas_call x2, Pallas kernels, mobility_own(): pl.pallas_call(pair_kernel, out_shape=jax.ShapeDtypeStruct((6, own_rows),...  50.5 us
    all_to_all x2, blocking collectives, per_device(): pieces = lax.all_to_all(pieces, AXES, 0, 0, tiled=True)  40.2 us
    all_to_all x2, blocking collectives, per_device(): every = lax.all_to_all(every, AXES, 0, 0, tiled=True)  32.7 us
    all_to_all x1, blocking collectives, per_device(): lax.all_to_all(jnp.broadcast_to(block, (devices, 1, 9 * own_rows)), AXES,...  18.5 us
    all_to_all x1, blocking collectives, per_device(): lax.all_to_all(jnp.broadcast_to(block, (devices, 1, 6 * own_rows)), AXES,...  16.6 us
    pallas_call x3, Pallas kernels, contact_step(): pl.pallas_call(functools.partial(contact_kernel, step, gather, scatter),...  12.8 us

profile of v16, /device:TPU:1, one launch (start us, length us, event | category | flops | bytes accessed | tf_op | source)
XLA Modules:
  0.0 178.7 jit_solution(5813175725334036430)
XLA Ops:
  0.6 3.5 %shard_map.86 = f32[128,1,768]{2,1,0:T(1,128)} custom-call(s32[2,1024]{1,0:T(2,128)} %refs_0_.5, f32[9,1024]{1,0:T(8,128)} %refs_1_.5, f32[1,1024]{1,0:T(1,128)} %bitcast.23, f32[1,1024]{1,0:T(1,128)} %bitcast.25, f32[1,1024]{1,0:T(1,128)} %bitcast.27, f32[2]{0:T(128)} %refs_5_.5), custom_call_target="tpu_custom_call" | custom-call | flops 805306368 | bytes 2457600 | tf_op jit(solution)/shard_map/pallas_call | solution.py:230
  4.2 23.4 %all_to_all.38 = f32[128,1,768]{2,1,0:T(1,128)S(1)} all-to-all(f32[128,1,768]{2,1,0:T(1,128)} %shard_map.86), channel_id=1, replica_groups=mesh['src'=16,'tgt'=8] {'src','tgt'}, dimensions={0} | all-to-all | bytes 786432 | tf_op jit(solution)/shard_map/all_to_all | solution.py:354
  27.6 0.3 reduce_sum.18
  27.9 0.0 copy-start
  27.9 0.0 copy-start.2
  27.9 0.6 copy-done
  28.5 0.1 copy-done.2
  28.6 0.3 broadcast_in_dim.34
  28.9 18.5 %all_to_all.39.place_ref.force_ref = f32[128,1,1152]{2,1,0:T(1,128)} all-to-all(f32[128,1,1152]{2,1,0:T(1,128)S(1)} %broadcast_in_dim.34), channel_id=1, replica_groups=mesh['src'=16,'tgt'=8] {'src','tgt'}, dimensions={0} | all-to-all | bytes 1179648 | tf_op jit(solution)/shard_map/all_to_all | solution.py:358
  47.4 0.8 broadcast_in_dim.32.target_ref
  48.2 25.3 %shard_map.87 = f32[6,128]{1,0:T(8,128)} custom-call(f32[3,128,128]{2,1,0:T(8,128)} %broadcast_in_dim.32.target_ref, f32[128,1,1152]{2,1,0:T(1,128)} %all_to_all.39.place_ref.force_ref, f32[128,1,1152]{2,1,0:T(1,128)} %all_to_all.39.place_ref.force_ref, f32[6,128]{1,0:T(8,128)} %bitcast.19), custom_call_target="tpu_custom_call" | custom-call | flops 188743680 | bytes 786432 | tf_op jit(solution)/shard_map/pallas_call | solution.py:315
  73.4 0.9 broadcast_in_dim.36
  74.3 16.5 %all_to_all.40 = f32[128,1,768]{2,1,0:T(1,128)S(1)} all-to-all(f32[128,1,768]{2,1,0:T(1,128)S(1)} %broadcast_in_dim.36), channel_id=1, replica_groups=mesh['src'=16,'tgt'=8] {'src','tgt'}, dimensions={0} | all-to-all | bytes 786432 | tf_op jit(solution)/shard_map/all_to_all | solution.py:369
  90.8 1.1 copy.9
  91.8 5.7 %shard_map.88 = (f32[1,1024]{1,0:T(1,128)}, f32[1,1024]{1,0:T(1,128)}, f32[128,1,768]{2,1,0:T(1,128)}) custom-call(s32[2,1024]{1,0:T(2,128)} %refs_0_.5, f32[9,1024]{1,0:T(8,128)} %refs_1_.5, f32[1,1024]{1,0:T(1,128)} %bitcast.24, f32[1,1024]{1,0:T(1,128)} %bitcast.26, f32[1,1024]{1,0:T(1,128)} %bitcast.28, f32[2]{0:T(128)} %refs_5_.5, f32[768,128]{1,0:T(8,128)} %bitcast.17), custom_call_target="tpu_custom_call" | custom-call | flops 1610612736 | bytes 2457600 | tf_op jit(solution)/shard_map/pallas_call | solution.py:230
  97.5 16.8 %all_to_all.41 = f32[128,1,768]{2,1,0:T(1,128)S(1)} all-to-all(f32[128,1,768]{2,1,0:T(1,128)} %get-tuple-element.7), channel_id=1, replica_groups=mesh['src'=16,'tgt'=8] {'src','tgt'}, dimensions={0} | all-to-all | bytes 786432 | tf_op jit(solution)/shard_map/all_to_all | solution.py:354
  114.3 0.3 reduce_sum.19
  114.6 0.0 copy-start.1
  114.6 0.2 broadcast_in_dim.37
  114.8 0.4 copy-done.1
  115.2 16.6 %all_to_all.42.force_ref = f32[128,1,768]{2,1,0:T(1,128)} all-to-all(f32[128,1,768]{2,1,0:T(1,128)S(1)} %broadcast_in_dim.37), channel_id=1, replica_groups=mesh['src'=16,'tgt'=8] {'src','tgt'}, dimensions={0} | all-to-all | bytes 786432 | tf_op jit(solution)/shard_map/all_to_all | solution.py:364
  131.8 25.2 %shard_map.89 = f32[6,128]{1,0:T(8,128)} custom-call(f32[3,128,128]{2,1,0:T(8,128)} %broadcast_in_dim.32.target_ref, f32[128,1,1152]{2,1,0:T(1,128)} %all_to_all.39.place_ref.force_ref, f32[128,1,768]{2,1,0:T(1,128)} %all_to_all.42.force_ref, f32[6,128]{1,0:T(8,128)} %bitcast.20), custom_call_target="tpu_custom_call" | custom-call | flops 188743680 | bytes 786432 | tf_op jit(solution)/shard_map/pallas_call | solution.py:315
  157.0 0.9 broadcast_in_dim.39
  157.9 16.2 %all_to_all.43 = f32[128,1,768]{2,1,0:T(1,128)S(1)} all-to-all(f32[128,1,768]{2,1,0:T(1,128)S(1)} %broadcast_in_dim.39), channel_id=1, replica_groups=mesh['src'=16,'tgt'=8] {'src','tgt'}, dimensions={0} | all-to-all | bytes 786432 | tf_op jit(solution)/shard_map/all_to_all | solution.py:369
  174.1 1.1 copy.10
  175.2 3.6 %shard_map.90 = f32[1,1024]{1,0:T(1,128)} custom-call(s32[2,1024]{1,0:T(2,128)} %refs_0_.5, f32[9,1024]{1,0:T(8,128)} %refs_1_.5, f32[1,1024]{1,0:T(1,128)} %get-tuple-element.5.refs_2_, f32[1,1024]{1,0:T(1,128)} %get-tuple-element.6.refs_3_, f32[1,1024]{1,0:T(1,128)} %bitcast.29, f32[2]{0:T(128)} %refs_5_.5, f32[768,128]{1,0:T(8,128)} %bitcast.18), custom_call_target="tpu_custom_call" | custom-call | flops 805306368 | bytes 2457600 | tf_op jit(solution)/shard_map/pallas_call | solution.py:230
  (3 shorter events, 0.0 us)
Async XLA Ops:
  27.9 0.6 copy-start
  27.9 0.7 copy-start.2
  114.6 0.6 copy-start.1

commit v17 on v13

--- a/solution.py
+++ b/solution.py
@@ -240,7 +240,7 @@
         ),
     )(*args)
 
-def pair_kernel(target_ref, place_ref, force_ref, own_ref, out_ref, sums_ref):
+def pair_kernel(target_ref, place_ref, force_ref, own_ref, out_ref, every_ref, sums_ref):
     targets = target_ref.shape[1]
     chunks = place_ref.shape[0]
     first_place = place_ref.shape[2] // 128 - 3
@@ -307,7 +307,11 @@
             )
             total = term if total is None else total + term
         scale = -0.25 if k < 3 else 1.125
-        out_ref[k : k + 1, :] = total[0:1, :] + scale * own_ref[k : k + 1, :]
+        row = total[0:1, :] + scale * own_ref[k : k + 1, :]
+        out_ref[k : k + 1, :] = row
+        every_ref[:, 0, k * targets : (k + 1) * targets] = jnp.broadcast_to(
+            row, (every_ref.shape[0], targets)
+        )
 
 
 def mobility_own(spread, places, forces, own_forces):
@@ -315,7 +319,10 @@
     sources = places.shape[0] * 128
     return pl.pallas_call(
         pair_kernel,
-        out_shape=jax.ShapeDtypeStruct((6, own_rows), jnp.float32),
+        out_shape=(
+            jax.ShapeDtypeStruct((6, own_rows), jnp.float32),
+            jax.ShapeDtypeStruct((places.shape[0], 1, 6 * own_rows), jnp.float32),
+        ),
         scratch_shapes=[pltpu.VMEM((6, own_rows, 128), jnp.float32)],
         cost_estimate=pl.CostEstimate(
             flops=90 * own_rows * sources,
@@ -365,9 +372,8 @@
             forces = lax.all_to_all(
                 jnp.broadcast_to(block, (devices, 1, 6 * own_rows)), AXES, 0, 0, tiled=True
             )
-        own_velocity = mobility_own(spread, places, forces, own_forces)
-        every = jnp.broadcast_to(own_velocity.reshape(1, 6 * own_rows), (devices, 6 * own_rows))
-        every = lax.all_to_all(every, AXES, 0, 0, tiled=True)
+        own_velocity, every = mobility_own(spread, places, forces, own_forces)
+        every = lax.all_to_all(every, AXES, 0, 0, tiled=True).reshape(devices, 6 * own_rows)
         last = k == ITERS - 1
         result = contact_step(
             k, devices, own_rows, contact_bodies, contact_frame, state, gaps_row, step_sizes, every.T, scatter=not last

time: 179 us -> 179 us (level)
  no operation moved by 1% of the time
where the time goes in v17:
time: 179 us; the launch traced here: 178 us
  blocking collectives  109 us (61%)
  Pallas kernels  63.5 us (35%)
  local copies, waits for them, and re-layouts  4.47 us (2%)
    pallas_call x2, Pallas kernels, mobility_own(): pl.pallas_call(pair_kernel, out_shape=(jax.ShapeDtypeStruct((6, own_rows)...  50.9 us
    all_to_all x2, blocking collectives, per_device(): pieces = lax.all_to_all(pieces, AXES, 0, 0, tiled=True)  40.2 us
    all_to_all x2, blocking collectives, per_device(): lax.all_to_all(every, AXES, 0, 0, tiled=True).reshape(devices, 6 * own_rows)  33.8 us
    all_to_all x1, blocking collectives, per_device(): lax.all_to_all(jnp.broadcast_to(block, (devices, 1, 9 * own_rows)), AXES,...  18.4 us
    all_to_all x1, blocking collectives, per_device(): lax.all_to_all(jnp.broadcast_to(block, (devices, 1, 6 * own_rows)), AXES,...  16.6 us
    pallas_call x3, Pallas kernels, contact_step(): pl.pallas_call(functools.partial(contact_kernel, step, gather, scatter),...  12.7 us

profile of v17, /device:TPU:1, one launch (start us, length us, event | category | flops | bytes accessed | tf_op | source)
XLA Modules:
  0.0 178.3 jit_solution(10239746132223001295)
XLA Ops:
  0.6 3.5 %shard_map.86 = f32[128,1,768]{2,1,0:T(1,128)} custom-call(s32[2,1024]{1,0:T(2,128)} %refs_0_.5, f32[9,1024]{1,0:T(8,128)} %refs_1_.5, f32[1,1024]{1,0:T(1,128)} %bitcast.19, f32[1,1024]{1,0:T(1,128)} %bitcast.21, f32[1,1024]{1,0:T(1,128)} %bitcast.23, f32[2]{0:T(128)} %refs_5_.5), custom_call_target="tpu_custom_call" | custom-call | flops 805306368 | bytes 2457600 | tf_op jit(solution)/shard_map/pallas_call | solution.py:231
  4.1 23.4 %all_to_all.30 = f32[128,1,768]{2,1,0:T(1,128)S(1)} all-to-all(f32[128,1,768]{2,1,0:T(1,128)} %shard_map.86), channel_id=1, replica_groups=mesh['src'=16,'tgt'=8] {'src','tgt'}, dimensions={0} | all-to-all | bytes 786432 | tf_op jit(solution)/shard_map/all_to_all | solution.py:362
  27.6 0.3 reduce_sum.18
  27.8 0.0 copy-start
  27.8 0.0 copy-start.2
  27.9 0.6 copy-done
  28.4 0.1 copy-done.2
  28.5 0.3 broadcast_in_dim.20
  28.8 18.4 %all_to_all.31.place_ref.force_ref = f32[128,1,1152]{2,1,0:T(1,128)} all-to-all(f32[128,1,1152]{2,1,0:T(1,128)S(1)} %broadcast_in_dim.20), channel_id=1, replica_groups=mesh['src'=16,'tgt'=8] {'src','tgt'}, dimensions={0} | all-to-all | bytes 1179648 | tf_op jit(solution)/shard_map/all_to_all | solution.py:366
  47.3 0.8 broadcast_in_dim.8.target_ref
  48.1 25.5 %shard_map.87 = (f32[6,128]{1,0:T(8,128)}, f32[128,1,768]{2,1,0:T(1,128)}) custom-call(f32[3,128,128]{2,1,0:T(8,128)} %broadcast_in_dim.8.target_ref, f32[128,1,1152]{2,1,0:T(1,128)} %all_to_all.31.place_ref.force_ref, f32[128,1,1152]{2,1,0:T(1,128)} %all_to_all.31.place_ref.force_ref, f32[6,128]{1,0:T(8,128)} %bitcast.17), custom_call_target="tpu_custom_call" | custom-call | flops 188743680 | bytes 786432 | tf_op jit(solution)/shard_map/pallas_call | solution.py:320
  73.6 16.8 %all_to_all.32 = f32[128,1,768]{2,1,0:T(1,128)S(1)} all-to-all(f32[128,1,768]{2,1,0:T(1,128)} %get-tuple-element.8), channel_id=1, replica_groups=mesh['src'=16,'tgt'=8] {'src','tgt'}, dimensions={0} | all-to-all | bytes 786432 | tf_op jit(solution)/shard_map/all_to_all | solution.py:376
  90.4 1.1 copy.11
  91.4 5.6 %shard_map.88 = (f32[1,1024]{1,0:T(1,128)}, f32[1,1024]{1,0:T(1,128)}, f32[128,1,768]{2,1,0:T(1,128)}) custom-call(s32[2,1024]{1,0:T(2,128)} %refs_0_.5, f32[9,1024]{1,0:T(8,128)} %refs_1_.5, f32[1,1024]{1,0:T(1,128)} %bitcast.20, f32[1,1024]{1,0:T(1,128)} %bitcast.22, f32[1,1024]{1,0:T(1,128)} %bitcast.24, f32[2]{0:T(128)} %refs_5_.5, f32[768,128]{1,0:T(8,128)} %bitcast.15), custom_call_target="tpu_custom_call" | custom-call | flops 1610612736 | bytes 2457600 | tf_op jit(solution)/shard_map/pallas_call | solution.py:231
  97.1 16.8 %all_to_all.33 = f32[128,1,768]{2,1,0:T(1,128)S(1)} all-to-all(f32[128,1,768]{2,1,0:T(1,128)} %get-tuple-element.11), channel_id=1, replica_groups=mesh['src'=16,'tgt'=8] {'src','tgt'}, dimensions={0} | all-to-all | bytes 786432 | tf_op jit(solution)/shard_map/all_to_all | solution.py:362
  113.9 0.3 reduce_sum.19
  114.2 0.0 copy-start.1
  114.2 0.2 broadcast_in_dim.21
  114.4 0.4 copy-done.1
  114.7 16.6 %all_to_all.34.force_ref = f32[128,1,768]{2,1,0:T(1,128)} all-to-all(f32[128,1,768]{2,1,0:T(1,128)S(1)} %broadcast_in_dim.21), channel_id=1, replica_groups=mesh['src'=16,'tgt'=8] {'src','tgt'}, dimensions={0} | all-to-all | bytes 786432 | tf_op jit(solution)/shard_map/all_to_all | solution.py:372
  131.3 25.4 %shard_map.89 = (f32[6,128]{1,0:T(8,128)}, f32[128,1,768]{2,1,0:T(1,128)}) custom-call(f32[3,128,128]{2,1,0:T(8,128)} %broadcast_in_dim.8.target_ref, f32[128,1,1152]{2,1,0:T(1,128)} %all_to_all.31.place_ref.force_ref, f32[128,1,768]{2,1,0:T(1,128)} %all_to_all.34.force_ref, f32[6,128]{1,0:T(8,128)} %bitcast.18), custom_call_target="tpu_custom_call" | custom-call | flops 188743680 | bytes 786432 | tf_op jit(solution)/shard_map/pallas_call | solution.py:320
  156.8 17.0 %all_to_all.35 = f32[128,1,768]{2,1,0:T(1,128)S(1)} all-to-all(f32[128,1,768]{2,1,0:T(1,128)} %get-tuple-element.12), channel_id=1, replica_groups=mesh['src'=16,'tgt'=8] {'src','tgt'}, dimensions={0} | all-to-all | bytes 786432 | tf_op jit(solution)/shard_map/all_to_all | solution.py:376
  173.7 1.1 copy.12
  174.8 3.5 %shard_map.90 = f32[1,1024]{1,0:T(1,128)} custom-call(s32[2,1024]{1,0:T(2,128)} %refs_0_.5, f32[9,1024]{1,0:T(8,128)} %refs_1_.5, f32[1,1024]{1,0:T(1,128)} %get-tuple-element.9.refs_2_, f32[1,1024]{1,0:T(1,128)} %get-tuple-element.10.refs_3_, f32[1,1024]{1,0:T(1,128)} %bitcast.25, f32[2]{0:T(128)} %refs_5_.5, f32[768,128]{1,0:T(8,128)} %bitcast.16), custom_call_target="tpu_custom_call" | custom-call | flops 805306368 | bytes 2457600 | tf_op jit(solution)/shard_map/pallas_call | solution.py:231
  (3 shorter events, 0.0 us)
Async XLA Ops:
  27.8 0.6 copy-start
  27.8 0.7 copy-start.2
  114.2 0.6 copy-start.1

commit v18 on v13

--- a/solution.py
+++ b/solution.py
@@ -287,7 +287,7 @@
             )
 
         zero = jnp.zeros((8, 128), jnp.float32)
-        sums = lax.fori_loop(0, chunks, chunk, (zero,) * 6, unroll=32)
+        sums = lax.fori_loop(0, chunks, chunk, (zero,) * 6, unroll=64)
         for k in range(6):
             sums_ref[k, rows, :] = sums[k]
         return carry

time: 179 us -> 178 us (level)
  no operation moved by 1% of the time
where the time goes in v18:
time: 178 us
  blocking collectives  108 us (61%)
  Pallas kernels  62.5 us (35%)
  local copies, waits for them, and re-layouts  6.25 us (4%)
    pallas_call x2, Pallas kernels, mobility_own(): pl.pallas_call(pair_kernel, out_shape=jax.ShapeDtypeStruct((6, own_rows),...  49.8 us
    all_to_all x2, blocking collectives, per_device(): pieces = lax.all_to_all(pieces, AXES, 0, 0, tiled=True)  40.2 us
    all_to_all x2, blocking collectives, per_device(): every = lax.all_to_all(every, AXES, 0, 0, tiled=True)  32.7 us
    all_to_all x1, blocking collectives, per_device(): lax.all_to_all(jnp.broadcast_to(block, (devices, 1, 9 * own_rows)), AXES,...  18.5 us
    all_to_all x1, blocking collectives, per_device(): lax.all_to_all(jnp.broadcast_to(block, (devices, 1, 6 * own_rows)), AXES,...  16.6 us
    pallas_call x3, Pallas kernels, contact_step(): pl.pallas_call(functools.partial(contact_kernel, step, gather, scatter),...  12.7 us

profile of v18, /device:TPU:1, one launch (start us, length us, event | category | flops | bytes accessed | tf_op | source)
XLA Modules:
  0.0 178.0 jit_solution(16557782954290216017)
XLA Ops:
  0.6 3.5 %shard_map.86 = f32[128,1,768]{2,1,0:T(1,128)} custom-call(s32[2,1024]{1,0:T(2,128)} %refs_0_.5, f32[9,1024]{1,0:T(8,128)} %refs_1_.5, f32[1,1024]{1,0:T(1,128)} %bitcast.23, f32[1,1024]{1,0:T(1,128)} %bitcast.25, f32[1,1024]{1,0:T(1,128)} %bitcast.27, f32[2]{0:T(128)} %refs_5_.5), custom_call_target="tpu_custom_call" | custom-call | flops 805306368 | bytes 2457600 | tf_op jit(solution)/shard_map/pallas_call | solution.py:231
  4.1 23.4 %all_to_all.38 = f32[128,1,768]{2,1,0:T(1,128)S(1)} all-to-all(f32[128,1,768]{2,1,0:T(1,128)} %shard_map.86), channel_id=1, replica_groups=mesh['src'=16,'tgt'=8] {'src','tgt'}, dimensions={0} | all-to-all | bytes 786432 | tf_op jit(solution)/shard_map/all_to_all | solution.py:355
  27.6 0.3 reduce_sum.18
  27.8 0.0 copy-start
  27.8 0.0 copy-start.2
  27.9 0.6 copy-done
  28.4 0.1 copy-done.2
  28.5 0.3 broadcast_in_dim.34
  28.9 18.5 %all_to_all.39.place_ref.force_ref = f32[128,1,1152]{2,1,0:T(1,128)} all-to-all(f32[128,1,1152]{2,1,0:T(1,128)S(1)} %broadcast_in_dim.34), channel_id=1, replica_groups=mesh['src'=16,'tgt'=8] {'src','tgt'}, dimensions={0} | all-to-all | bytes 1179648 | tf_op jit(solution)/shard_map/all_to_all | solution.py:359
  47.3 0.8 broadcast_in_dim.32.target_ref
  48.1 24.9 %shard_map.87 = f32[6,128]{1,0:T(8,128)} custom-call(f32[3,128,128]{2,1,0:T(8,128)} %broadcast_in_dim.32.target_ref, f32[128,1,1152]{2,1,0:T(1,128)} %all_to_all.39.place_ref.force_ref, f32[128,1,1152]{2,1,0:T(1,128)} %all_to_all.39.place_ref.force_ref, f32[6,128]{1,0:T(8,128)} %bitcast.19), custom_call_target="tpu_custom_call" | custom-call | flops 188743680 | bytes 786432 | tf_op jit(solution)/shard_map/pallas_call | solution.py:316
  73.0 0.9 broadcast_in_dim.36
  73.9 16.5 %all_to_all.40 = f32[128,1,768]{2,1,0:T(1,128)S(1)} all-to-all(f32[128,1,768]{2,1,0:T(1,128)S(1)} %broadcast_in_dim.36), channel_id=1, replica_groups=mesh['src'=16,'tgt'=8] {'src','tgt'}, dimensions={0} | all-to-all | bytes 786432 | tf_op jit(solution)/shard_map/all_to_all | solution.py:370
  90.4 1.1 copy.9
  91.5 5.6 %shard_map.88 = (f32[1,1024]{1,0:T(1,128)}, f32[1,1024]{1,0:T(1,128)}, f32[128,1,768]{2,1,0:T(1,128)}) custom-call(s32[2,1024]{1,0:T(2,128)} %refs_0_.5, f32[9,1024]{1,0:T(8,128)} %refs_1_.5, f32[1,1024]{1,0:T(1,128)} %bitcast.24, f32[1,1024]{1,0:T(1,128)} %bitcast.26, f32[1,1024]{1,0:T(1,128)} %bitcast.28, f32[2]{0:T(128)} %refs_5_.5, f32[768,128]{1,0:T(8,128)} %bitcast.17), custom_call_target="tpu_custom_call" | custom-call | flops 1610612736 | bytes 2457600 | tf_op jit(solution)/shard_map/pallas_call | solution.py:231
  97.1 16.8 %all_to_all.41 = f32[128,1,768]{2,1,0:T(1,128)S(1)} all-to-all(f32[128,1,768]{2,1,0:T(1,128)} %get-tuple-element.7), channel_id=1, replica_groups=mesh['src'=16,'tgt'=8] {'src','tgt'}, dimensions={0} | all-to-all | bytes 786432 | tf_op jit(solution)/shard_map/all_to_all | solution.py:355
  113.9 0.3 reduce_sum.19
  114.2 0.0 copy-start.1
  114.2 0.2 broadcast_in_dim.37
  114.4 0.4 copy-done.1
  114.8 16.6 %all_to_all.42.force_ref = f32[128,1,768]{2,1,0:T(1,128)} all-to-all(f32[128,1,768]{2,1,0:T(1,128)S(1)} %broadcast_in_dim.37), channel_id=1, replica_groups=mesh['src'=16,'tgt'=8] {'src','tgt'}, dimensions={0} | all-to-all | bytes 786432 | tf_op jit(solution)/shard_map/all_to_all | solution.py:365
  131.4 24.9 %shard_map.89 = f32[6,128]{1,0:T(8,128)} custom-call(f32[3,128,128]{2,1,0:T(8,128)} %broadcast_in_dim.32.target_ref, f32[128,1,1152]{2,1,0:T(1,128)} %all_to_all.39.place_ref.force_ref, f32[128,1,768]{2,1,0:T(1,128)} %all_to_all.42.force_ref, f32[6,128]{1,0:T(8,128)} %bitcast.20), custom_call_target="tpu_custom_call" | custom-call | flops 188743680 | bytes 786432 | tf_op jit(solution)/shard_map/pallas_call | solution.py:316
  156.3 0.9 broadcast_in_dim.39
  157.1 16.2 %all_to_all.43 = f32[128,1,768]{2,1,0:T(1,128)S(1)} all-to-all(f32[128,1,768]{2,1,0:T(1,128)S(1)} %broadcast_in_dim.39), channel_id=1, replica_groups=mesh['src'=16,'tgt'=8] {'src','tgt'}, dimensions={0} | all-to-all | bytes 786432 | tf_op jit(solution)/shard_map/all_to_all | solution.py:370
  173.4 1.1 copy.10
  174.4 3.5 %shard_map.90 = f32[1,1024]{1,0:T(1,128)} custom-call(s32[2,1024]{1,0:T(2,128)} %refs_0_.5, f32[9,1024]{1,0:T(8,128)} %refs_1_.5, f32[1,1024]{1,0:T(1,128)} %get-tuple-element.5.refs_2_, f32[1,1024]{1,0:T(1,128)} %get-tuple-element.6.refs_3_, f32[1,1024]{1,0:T(1,128)} %bitcast.29, f32[2]{0:T(128)} %refs_5_.5, f32[768,128]{1,0:T(8,128)} %bitcast.18), custom_call_target="tpu_custom_call" | custom-call | flops 805306368 | bytes 2457600 | tf_op jit(solution)/shard_map/pallas_call | solution.py:231
  (3 shorter events, 0.0 us)
Async XLA Ops:
  27.8 0.6 copy-start
  27.8 0.7 copy-start.2
  114.2 0.6 copy-start.1

commit v19 on v13

--- a/solution.py
+++ b/solution.py
@@ -240,9 +240,12 @@
         ),
     )(*args)
 
-def pair_kernel(target_ref, place_ref, force_ref, own_ref, out_ref, sums_ref):
+def pair_kernel(position_ref, place_ref, force_ref, own_ref, out_ref, sums_ref, target_ref):
     targets = target_ref.shape[1]
     chunks = place_ref.shape[0]
+    for c in range(3):
+        row = position_ref[c : c + 1, :]
+        target_ref[c] = jnp.broadcast_to(row, (128, targets)).T
     first_place = place_ref.shape[2] // 128 - 3
 
     def group(g, carry):
@@ -310,19 +313,22 @@
         out_ref[k : k + 1, :] = total[0:1, :] + scale * own_ref[k : k + 1, :]
 
 
-def mobility_own(spread, places, forces, own_forces):
+def mobility_own(positions, places, forces, own_forces):
     own_rows = own_forces.shape[1]
     sources = places.shape[0] * 128
     return pl.pallas_call(
         pair_kernel,
         out_shape=jax.ShapeDtypeStruct((6, own_rows), jnp.float32),
-        scratch_shapes=[pltpu.VMEM((6, own_rows, 128), jnp.float32)],
+        scratch_shapes=[
+            pltpu.VMEM((6, own_rows, 128), jnp.float32),
+            pltpu.VMEM((3, own_rows, 128), jnp.float32),
+        ],
         cost_estimate=pl.CostEstimate(
             flops=90 * own_rows * sources,
             transcendentals=own_rows * sources,
             bytes_accessed=4 * (9 * sources + 3 * own_rows * 128),
         ),
-    )(spread, places, forces, own_forces)
+    )(positions, places, forces, own_forces)
 
 def gather_all(block, devices):
     rows, width = block.shape
@@ -346,7 +352,6 @@
     me = lax.axis_index("src") * lax.axis_size("tgt") + lax.axis_index("tgt")
     own_rows = positions.shape[1]
     body_count = own_rows * devices
-    spread = jnp.broadcast_to(positions[:, :, None], (3, own_rows, 128))
     gaps_row = gaps.reshape(1, -1)
     state = (impulse_now.reshape(1, -1), impulse_prev.reshape(1, -1))
     (pieces,) = contact_step(0, devices, own_rows, contact_bodies, contact_frame, state, gaps_row, step_sizes)
@@ -365,7 +370,7 @@
             forces = lax.all_to_all(
                 jnp.broadcast_to(block, (devices, 1, 6 * own_rows)), AXES, 0, 0, tiled=True
             )
-        own_velocity = mobility_own(spread, places, forces, own_forces)
+        own_velocity = mobility_own(positions, places, forces, own_forces)
         every = jnp.broadcast_to(own_velocity.reshape(1, 6 * own_rows), (devices, 6 * own_rows))
         every = lax.all_to_all(every, AXES, 0, 0, tiled=True)
         last = k == ITERS - 1

time: 179 us -> 179 us (level)
  no operation moved by 1% of the time
where the time goes in v19:
time: 179 us; the launch traced here: 178 us
  blocking collectives  108 us (60%)
  Pallas kernels  63.7 us (36%)
  local copies, waits for them, and re-layouts  5.44 us (3%)
    pallas_call x2, Pallas kernels, mobility_own(): pl.pallas_call(pair_kernel, out_shape=jax.ShapeDtypeStruct((6, own_rows),...  51.1 us
    all_to_all x2, blocking collectives, per_device(): pieces = lax.all_to_all(pieces, AXES, 0, 0, tiled=True)  40.2 us
    all_to_all x2, blocking collectives, per_device(): every = lax.all_to_all(every, AXES, 0, 0, tiled=True)  32.7 us
    all_to_all x1, blocking collectives, per_device(): lax.all_to_all(jnp.broadcast_to(block, (devices, 1, 9 * own_rows)), AXES,...  18.5 us
    all_to_all x1, blocking collectives, per_device(): lax.all_to_all(jnp.broadcast_to(block, (devices, 1, 6 * own_rows)), AXES,...  16.6 us
    pallas_call x3, Pallas kernels, contact_step(): pl.pallas_call(functools.partial(contact_kernel, step, gather, scatter),...  12.7 us

profile of v19, /device:TPU:1, one launch (start us, length us, event | category | flops | bytes accessed | tf_op | source)
XLA Modules:
  0.0 178.4 jit_solution(3470888816846618935)
XLA Ops:
  0.6 3.5 %shard_map.86 = f32[128,1,768]{2,1,0:T(1,128)} custom-call(s32[2,1024]{1,0:T(2,128)} %refs_0_.5, f32[9,1024]{1,0:T(8,128)} %refs_1_.5, f32[1,1024]{1,0:T(1,128)} %bitcast.23, f32[1,1024]{1,0:T(1,128)} %bitcast.25, f32[1,1024]{1,0:T(1,128)} %bitcast.27, f32[2]{0:T(128)} %refs_5_.5), custom_call_target="tpu_custom_call" | custom-call | flops 805306368 | bytes 2457600 | tf_op jit(solution)/shard_map/pallas_call | solution.py:231
  4.1 23.4 %all_to_all.38 = f32[128,1,768]{2,1,0:T(1,128)S(1)} all-to-all(f32[128,1,768]{2,1,0:T(1,128)} %shard_map.86), channel_id=1, replica_groups=mesh['src'=16,'tgt'=8] {'src','tgt'}, dimensions={0} | all-to-all | bytes 786432 | tf_op jit(solution)/shard_map/all_to_all | solution.py:360
  27.6 0.3 reduce_sum.18
  27.8 0.0 copy-start
  27.8 0.0 copy-start.2
  27.9 0.6 copy-done
  28.4 0.1 copy-done.2
  28.5 0.3 broadcast_in_dim.27
  28.9 18.5 %all_to_all.39.place_ref.force_ref = f32[128,1,1152]{2,1,0:T(1,128)} all-to-all(f32[128,1,1152]{2,1,0:T(1,128)S(1)} %broadcast_in_dim.27), channel_id=1, replica_groups=mesh['src'=16,'tgt'=8] {'src','tgt'}, dimensions={0} | all-to-all | bytes 1179648 | tf_op jit(solution)/shard_map/all_to_all | solution.py:364
  47.3 25.6 %shard_map.87 = f32[6,128]{1,0:T(8,128)} custom-call(f32[3,128]{1,0:T(4,128)} %position_ref.3, f32[128,1,1152]{2,1,0:T(1,128)} %all_to_all.39.place_ref.force_ref, f32[128,1,1152]{2,1,0:T(1,128)} %all_to_all.39.place_ref.force_ref, f32[6,128]{1,0:T(8,128)} %bitcast.19), custom_call_target="tpu_custom_call" | custom-call | flops 188743680 | bytes 786432 | tf_op jit(solution)/shard_map/pallas_call | solution.py:319
  72.9 0.9 broadcast_in_dim.29
  73.8 16.5 %all_to_all.40 = f32[128,1,768]{2,1,0:T(1,128)S(1)} all-to-all(f32[128,1,768]{2,1,0:T(1,128)S(1)} %broadcast_in_dim.29), channel_id=1, replica_groups=mesh['src'=16,'tgt'=8] {'src','tgt'}, dimensions={0} | all-to-all | bytes 786432 | tf_op jit(solution)/shard_map/all_to_all | solution.py:375
  90.3 1.1 copy.9
  91.3 5.6 %shard_map.88 = (f32[1,1024]{1,0:T(1,128)}, f32[1,1024]{1,0:T(1,128)}, f32[128,1,768]{2,1,0:T(1,128)}) custom-call(s32[2,1024]{1,0:T(2,128)} %refs_0_.5, f32[9,1024]{1,0:T(8,128)} %refs_1_.5, f32[1,1024]{1,0:T(1,128)} %bitcast.24, f32[1,1024]{1,0:T(1,128)} %bitcast.26, f32[1,1024]{1,0:T(1,128)} %bitcast.28, f32[2]{0:T(128)} %refs_5_.5, f32[768,128]{1,0:T(8,128)} %bitcast.17), custom_call_target="tpu_custom_call" | custom-call | flops 1610612736 | bytes 2457600 | tf_op jit(solution)/shard_map/pallas_call | solution.py:231
  96.9 16.8 %all_to_all.41 = f32[128,1,768]{2,1,0:T(1,128)S(1)} all-to-all(f32[128,1,768]{2,1,0:T(1,128)} %get-tuple-element.7), channel_id=1, replica_groups=mesh['src'=16,'tgt'=8] {'src','tgt'}, dimensions={0} | all-to-all | bytes 786432 | tf_op jit(solution)/shard_map/all_to_all | solution.py:360
  113.7 0.3 reduce_sum.19
  114.0 0.0 copy-start.1
  114.0 0.2 broadcast_in_dim.30
  114.3 0.4 copy-done.1
  114.6 16.6 %all_to_all.42.force_ref = f32[128,1,768]{2,1,0:T(1,128)} all-to-all(f32[128,1,768]{2,1,0:T(1,128)S(1)} %broadcast_in_dim.30), channel_id=1, replica_groups=mesh['src'=16,'tgt'=8] {'src','tgt'}, dimensions={0} | all-to-all | bytes 786432 | tf_op jit(solution)/shard_map/all_to_all | solution.py:370
  131.2 25.5 %shard_map.89 = f32[6,128]{1,0:T(8,128)} custom-call(f32[3,128]{1,0:T(4,128)} %position_ref.3, f32[128,1,1152]{2,1,0:T(1,128)} %all_to_all.39.place_ref.force_ref, f32[128,1,768]{2,1,0:T(1,128)} %all_to_all.42.force_ref, f32[6,128]{1,0:T(8,128)} %bitcast.20), custom_call_target="tpu_custom_call" | custom-call | flops 188743680 | bytes 786432 | tf_op jit(solution)/shard_map/pallas_call | solution.py:319
  156.7 0.9 broadcast_in_dim.32
  157.6 16.2 %all_to_all.43 = f32[128,1,768]{2,1,0:T(1,128)S(1)} all-to-all(f32[128,1,768]{2,1,0:T(1,128)S(1)} %broadcast_in_dim.32), channel_id=1, replica_groups=mesh['src'=16,'tgt'=8] {'src','tgt'}, dimensions={0} | all-to-all | bytes 786432 | tf_op jit(solution)/shard_map/all_to_all | solution.py:375
  173.8 1.1 copy.10
  174.9 3.5 %shard_map.90 = f32[1,1024]{1,0:T(1,128)} custom-call(s32[2,1024]{1,0:T(2,128)} %refs_0_.5, f32[9,1024]{1,0:T(8,128)} %refs_1_.5, f32[1,1024]{1,0:T(1,128)} %get-tuple-element.5.refs_2_, f32[1,1024]{1,0:T(1,128)} %get-tuple-element.6.refs_3_, f32[1,1024]{1,0:T(1,128)} %bitcast.29, f32[2]{0:T(128)} %refs_5_.5, f32[768,128]{1,0:T(8,128)} %bitcast.18), custom_call_target="tpu_custom_call" | custom-call | flops 805306368 | bytes 2457600 | tf_op jit(solution)/shard_map/pallas_call | solution.py:231
  (3 shorter events, 0.0 us)
Async XLA Ops:
  27.8 0.6 copy-start
  27.8 0.7 copy-start.2
  114.0 0.6 copy-start.1

commit v20 on v19

--- a/solution.py
+++ b/solution.py
@@ -290,7 +290,7 @@
             )
 
         zero = jnp.zeros((8, 128), jnp.float32)
-        sums = lax.fori_loop(0, chunks, chunk, (zero,) * 6, unroll=32)
+        sums = lax.fori_loop(0, chunks, chunk, (zero,) * 6, unroll=64)
         for k in range(6):
             sums_ref[k, rows, :] = sums[k]
         return carry

time: 179 us -> 178 us (level)
  no operation moved by 1% of the time
where the time goes in v20:
time: 178 us
  blocking collectives  108 us (61%)
  Pallas kernels  62.8 us (35%)
  local copies, waits for them, and re-layouts  5.44 us (3%)
    pallas_call x2, Pallas kernels, mobility_own(): pl.pallas_call(pair_kernel, out_shape=jax.ShapeDtypeStruct((6, own_rows),...  50.2 us
    all_to_all x2, blocking collectives, per_device(): pieces = lax.all_to_all(pieces, AXES, 0, 0, tiled=True)  40.2 us
    all_to_all x2, blocking collectives, per_device(): every = lax.all_to_all(every, AXES, 0, 0, tiled=True)  32.7 us
    all_to_all x1, blocking collectives, per_device(): lax.all_to_all(jnp.broadcast_to(block, (devices, 1, 9 * own_rows)), AXES,...  18.5 us
    all_to_all x1, blocking collectives, per_device(): lax.all_to_all(jnp.broadcast_to(block, (devices, 1, 6 * own_rows)), AXES,...  16.6 us
    pallas_call x3, Pallas kernels, contact_step(): pl.pallas_call(functools.partial(contact_kernel, step, gather, scatter),...  12.7 us

profile of v20, /device:TPU:1, one launch (start us, length us, event | category | flops | bytes accessed | tf_op | source)
XLA Modules:
  0.0 177.5 jit_solution(8708157676483466768)
XLA Ops:
  0.6 3.5 %shard_map.86 = f32[128,1,768]{2,1,0:T(1,128)} custom-call(s32[2,1024]{1,0:T(2,128)} %refs_0_.5, f32[9,1024]{1,0:T(8,128)} %refs_1_.5, f32[1,1024]{1,0:T(1,128)} %bitcast.23, f32[1,1024]{1,0:T(1,128)} %bitcast.25, f32[1,1024]{1,0:T(1,128)} %bitcast.27, f32[2]{0:T(128)} %refs_5_.5), custom_call_target="tpu_custom_call" | custom-call | flops 805306368 | bytes 2457600 | tf_op jit(solution)/shard_map/pallas_call | solution.py:231
  4.1 23.4 %all_to_all.38 = f32[128,1,768]{2,1,0:T(1,128)S(1)} all-to-all(f32[128,1,768]{2,1,0:T(1,128)} %shard_map.86), channel_id=1, replica_groups=mesh['src'=16,'tgt'=8] {'src','tgt'}, dimensions={0} | all-to-all | bytes 786432 | tf_op jit(solution)/shard_map/all_to_all | solution.py:360
  27.6 0.3 reduce_sum.18
  27.8 0.0 copy-start
  27.8 0.0 copy-start.2
  27.9 0.6 copy-done
  28.4 0.1 copy-done.2
  28.5 0.3 broadcast_in_dim.27
  28.9 18.5 %all_to_all.39.place_ref.force_ref = f32[128,1,1152]{2,1,0:T(1,128)} all-to-all(f32[128,1,1152]{2,1,0:T(1,128)S(1)} %broadcast_in_dim.27), channel_id=1, replica_groups=mesh['src'=16,'tgt'=8] {'src','tgt'}, dimensions={0} | all-to-all | bytes 1179648 | tf_op jit(solution)/shard_map/all_to_all | solution.py:364
  47.3 25.1 %shard_map.87 = f32[6,128]{1,0:T(8,128)} custom-call(f32[3,128]{1,0:T(4,128)} %position_ref.3, f32[128,1,1152]{2,1,0:T(1,128)} %all_to_all.39.place_ref.force_ref, f32[128,1,1152]{2,1,0:T(1,128)} %all_to_all.39.place_ref.force_ref, f32[6,128]{1,0:T(8,128)} %bitcast.19), custom_call_target="tpu_custom_call" | custom-call | flops 188743680 | bytes 786432 | tf_op jit(solution)/shard_map/pallas_call | solution.py:319
  72.4 0.9 broadcast_in_dim.29
  73.3 16.5 %all_to_all.40 = f32[128,1,768]{2,1,0:T(1,128)S(1)} all-to-all(f32[128,1,768]{2,1,0:T(1,128)S(1)} %broadcast_in_dim.29), channel_id=1, replica_groups=mesh['src'=16,'tgt'=8] {'src','tgt'}, dimensions={0} | all-to-all | bytes 786432 | tf_op jit(solution)/shard_map/all_to_all | solution.py:375
  89.8 1.1 copy.9
  90.8 5.6 %shard_map.88 = (f32[1,1024]{1,0:T(1,128)}, f32[1,1024]{1,0:T(1,128)}, f32[128,1,768]{2,1,0:T(1,128)}) custom-call(s32[2,1024]{1,0:T(2,128)} %refs_0_.5, f32[9,1024]{1,0:T(8,128)} %refs_1_.5, f32[1,1024]{1,0:T(1,128)} %bitcast.24, f32[1,1024]{1,0:T(1,128)} %bitcast.26, f32[1,1024]{1,0:T(1,128)} %bitcast.28, f32[2]{0:T(128)} %refs_5_.5, f32[768,128]{1,0:T(8,128)} %bitcast.17), custom_call_target="tpu_custom_call" | custom-call | flops 1610612736 | bytes 2457600 | tf_op jit(solution)/shard_map/pallas_call | solution.py:231
  96.5 16.8 %all_to_all.41 = f32[128,1,768]{2,1,0:T(1,128)S(1)} all-to-all(f32[128,1,768]{2,1,0:T(1,128)} %get-tuple-element.7), channel_id=1, replica_groups=mesh['src'=16,'tgt'=8] {'src','tgt'}, dimensions={0} | all-to-all | bytes 786432 | tf_op jit(solution)/shard_map/all_to_all | solution.py:360
  113.3 0.3 reduce_sum.19
  113.6 0.0 copy-start.1
  113.6 0.2 broadcast_in_dim.30
  113.8 0.4 copy-done.1
  114.2 16.6 %all_to_all.42.force_ref = f32[128,1,768]{2,1,0:T(1,128)} all-to-all(f32[128,1,768]{2,1,0:T(1,128)S(1)} %broadcast_in_dim.30), channel_id=1, replica_groups=mesh['src'=16,'tgt'=8] {'src','tgt'}, dimensions={0} | all-to-all | bytes 786432 | tf_op jit(solution)/shard_map/all_to_all | solution.py:370
  130.8 25.0 %shard_map.89 = f32[6,128]{1,0:T(8,128)} custom-call(f32[3,128]{1,0:T(4,128)} %position_ref.3, f32[128,1,1152]{2,1,0:T(1,128)} %all_to_all.39.place_ref.force_ref, f32[128,1,768]{2,1,0:T(1,128)} %all_to_all.42.force_ref, f32[6,128]{1,0:T(8,128)} %bitcast.20), custom_call_target="tpu_custom_call" | custom-call | flops 188743680 | bytes 786432 | tf_op jit(solution)/shard_map/pallas_call | solution.py:319
  155.8 0.9 broadcast_in_dim.32
  156.7 16.2 %all_to_all.43 = f32[128,1,768]{2,1,0:T(1,128)S(1)} all-to-all(f32[128,1,768]{2,1,0:T(1,128)S(1)} %broadcast_in_dim.32), channel_id=1, replica_groups=mesh['src'=16,'tgt'=8] {'src','tgt'}, dimensions={0} | all-to-all | bytes 786432 | tf_op jit(solution)/shard_map/all_to_all | solution.py:375
  172.9 1.1 copy.10
  174.0 3.5 %shard_map.90 = f32[1,1024]{1,0:T(1,128)} custom-call(s32[2,1024]{1,0:T(2,128)} %refs_0_.5, f32[9,1024]{1,0:T(8,128)} %refs_1_.5, f32[1,1024]{1,0:T(1,128)} %get-tuple-element.5.refs_2_, f32[1,1024]{1,0:T(1,128)} %get-tuple-element.6.refs_3_, f32[1,1024]{1,0:T(1,128)} %bitcast.29, f32[2]{0:T(128)} %refs_5_.5, f32[768,128]{1,0:T(8,128)} %bitcast.18), custom_call_target="tpu_custom_call" | custom-call | flops 805306368 | bytes 2457600 | tf_op jit(solution)/shard_map/pallas_call | solution.py:231
  (3 shorter events, 0.0 us)
Async XLA Ops:
  27.8 0.6 copy-start
  27.8 0.7 copy-start.2
  113.6 0.6 copy-start.1

commit v21 on v20

--- a/solution.py
+++ b/solution.py
@@ -290,7 +290,7 @@
             )
 
         zero = jnp.zeros((8, 128), jnp.float32)
-        sums = lax.fori_loop(0, chunks, chunk, (zero,) * 6, unroll=64)
+        sums = lax.fori_loop(0, chunks, chunk, (zero,) * 6, unroll=True)
         for k in range(6):
             sums_ref[k, rows, :] = sums[k]
         return carry

time: 178 us -> 184 us (1.034)
  Pallas kernels: 62.8 us -> 68.2 us
    pallas_call x2, Pallas kernels: 50.2 us -> 55.5 us  [mobility_own(): pl.pallas_call(pair_kernel, out_shape=jax.ShapeDtypeStruct((6, own_rows),...]
where the time goes in v21:
time: 184 us; the launch traced here: 183 us
  blocking collectives  108 us (59%)
  Pallas kernels  68.2 us (37%)
  local copies, waits for them, and re-layouts  5.44 us (3%)
    pallas_call x2, Pallas kernels, mobility_own(): pl.pallas_call(pair_kernel, out_shape=jax.ShapeDtypeStruct((6, own_rows),...  55.5 us
    all_to_all x2, blocking collectives, per_device(): pieces = lax.all_to_all(pieces, AXES, 0, 0, tiled=True)  40.2 us
    all_to_all x2, blocking collectives, per_device(): every = lax.all_to_all(every, AXES, 0, 0, tiled=True)  32.7 us
    all_to_all x1, blocking collectives, per_device(): lax.all_to_all(jnp.broadcast_to(block, (devices, 1, 9 * own_rows)), AXES,...  18.5 us
    all_to_all x1, blocking collectives, per_device(): lax.all_to_all(jnp.broadcast_to(block, (devices, 1, 6 * own_rows)), AXES,...  16.8 us
    pallas_call x3, Pallas kernels, contact_step(): pl.pallas_call(functools.partial(contact_kernel, step, gather, scatter),...  12.7 us

profile of v21, /device:TPU:1, one launch (start us, length us, event | category | flops | bytes accessed | tf_op | source)
XLA Modules:
  0.0 183.0 jit_solution(15554514879323930853)
XLA Ops:
  0.6 3.5 %shard_map.86 = f32[128,1,768]{2,1,0:T(1,128)} custom-call(s32[2,1024]{1,0:T(2,128)} %refs_0_.5, f32[9,1024]{1,0:T(8,128)} %refs_1_.5, f32[1,1024]{1,0:T(1,128)} %bitcast.23, f32[1,1024]{1,0:T(1,128)} %bitcast.25, f32[1,1024]{1,0:T(1,128)} %bitcast.27, f32[2]{0:T(128)} %refs_5_.5), custom_call_target="tpu_custom_call" | custom-call | flops 805306368 | bytes 2457600 | tf_op jit(solution)/shard_map/pallas_call | solution.py:231
  4.1 23.4 %all_to_all.38 = f32[128,1,768]{2,1,0:T(1,128)S(1)} all-to-all(f32[128,1,768]{2,1,0:T(1,128)} %shard_map.86), channel_id=1, replica_groups=mesh['src'=16,'tgt'=8] {'src','tgt'}, dimensions={0} | all-to-all | bytes 786432 | tf_op jit(solution)/shard_map/all_to_all | solution.py:360
  27.6 0.3 reduce_sum.18
  27.8 0.0 copy-start
  27.8 0.0 copy-start.2
  27.9 0.6 copy-done
  28.4 0.1 copy-done.2
  28.5 0.3 broadcast_in_dim.27
  28.9 18.5 %all_to_all.39.place_ref.force_ref = f32[128,1,1152]{2,1,0:T(1,128)} all-to-all(f32[128,1,1152]{2,1,0:T(1,128)S(1)} %broadcast_in_dim.27), channel_id=1, replica_groups=mesh['src'=16,'tgt'=8] {'src','tgt'}, dimensions={0} | all-to-all | bytes 1179648 | tf_op jit(solution)/shard_map/all_to_all | solution.py:364
  47.3 27.8 %shard_map.87 = f32[6,128]{1,0:T(8,128)} custom-call(f32[3,128]{1,0:T(4,128)} %position_ref.3, f32[128,1,1152]{2,1,0:T(1,128)} %all_to_all.39.place_ref.force_ref, f32[128,1,1152]{2,1,0:T(1,128)} %all_to_all.39.place_ref.force_ref, f32[6,128]{1,0:T(8,128)} %bitcast.19), custom_call_target="tpu_custom_call" | custom-call | flops 188743680 | bytes 786432 | tf_op jit(solution)/shard_map/pallas_call | solution.py:319
  75.1 0.9 broadcast_in_dim.29
  76.0 16.5 %all_to_all.40 = f32[128,1,768]{2,1,0:T(1,128)S(1)} all-to-all(f32[128,1,768]{2,1,0:T(1,128)S(1)} %broadcast_in_dim.29), channel_id=1, replica_groups=mesh['src'=16,'tgt'=8] {'src','tgt'}, dimensions={0} | all-to-all | bytes 786432 | tf_op jit(solution)/shard_map/all_to_all | solution.py:375
  92.5 1.1 copy.9
  93.5 5.6 %shard_map.88 = (f32[1,1024]{1,0:T(1,128)}, f32[1,1024]{1,0:T(1,128)}, f32[128,1,768]{2,1,0:T(1,128)}) custom-call(s32[2,1024]{1,0:T(2,128)} %refs_0_.5, f32[9,1024]{1,0:T(8,128)} %refs_1_.5, f32[1,1024]{1,0:T(1,128)} %bitcast.24, f32[1,1024]{1,0:T(1,128)} %bitcast.26, f32[1,1024]{1,0:T(1,128)} %bitcast.28, f32[2]{0:T(128)} %refs_5_.5, f32[768,128]{1,0:T(8,128)} %bitcast.17), custom_call_target="tpu_custom_call" | custom-call | flops 1610612736 | bytes 2457600 | tf_op jit(solution)/shard_map/pallas_call | solution.py:231
  99.2 16.8 %all_to_all.41 = f32[128,1,768]{2,1,0:T(1,128)S(1)} all-to-all(f32[128,1,768]{2,1,0:T(1,128)} %get-tuple-element.7), channel_id=1, replica_groups=mesh['src'=16,'tgt'=8] {'src','tgt'}, dimensions={0} | all-to-all | bytes 786432 | tf_op jit(solution)/shard_map/all_to_all | solution.py:360
  116.0 0.3 reduce_sum.19
  116.2 0.0 copy-start.1
  116.3 0.2 broadcast_in_dim.30
  116.5 0.4 copy-done.1
  116.8 16.8 %all_to_all.42.force_ref = f32[128,1,768]{2,1,0:T(1,128)} all-to-all(f32[128,1,768]{2,1,0:T(1,128)S(1)} %broadcast_in_dim.30), channel_id=1, replica_groups=mesh['src'=16,'tgt'=8] {'src','tgt'}, dimensions={0} | all-to-all | bytes 786432 | tf_op jit(solution)/shard_map/all_to_all | solution.py:370
  133.6 27.7 %shard_map.89 = f32[6,128]{1,0:T(8,128)} custom-call(f32[3,128]{1,0:T(4,128)} %position_ref.3, f32[128,1,1152]{2,1,0:T(1,128)} %all_to_all.39.place_ref.force_ref, f32[128,1,768]{2,1,0:T(1,128)} %all_to_all.42.force_ref, f32[6,128]{1,0:T(8,128)} %bitcast.20), custom_call_target="tpu_custom_call" | custom-call | flops 188743680 | bytes 786432 | tf_op jit(solution)/shard_map/pallas_call | solution.py:319
  161.3 0.9 broadcast_in_dim.32
  162.2 16.2 %all_to_all.43 = f32[128,1,768]{2,1,0:T(1,128)S(1)} all-to-all(f32[128,1,768]{2,1,0:T(1,128)S(1)} %broadcast_in_dim.32), channel_id=1, replica_groups=mesh['src'=16,'tgt'=8] {'src','tgt'}, dimensions={0} | all-to-all | bytes 786432 | tf_op jit(solution)/shard_map/all_to_all | solution.py:375
  178.4 1.1 copy.10
  179.5 3.5 %shard_map.90 = f32[1,1024]{1,0:T(1,128)} custom-call(s32[2,1024]{1,0:T(2,128)} %refs_0_.5, f32[9,1024]{1,0:T(8,128)} %refs_1_.5, f32[1,1024]{1,0:T(1,128)} %get-tuple-element.5.refs_2_, f32[1,1024]{1,0:T(1,128)} %get-tuple-element.6.refs_3_, f32[1,1024]{1,0:T(1,128)} %bitcast.29, f32[2]{0:T(128)} %refs_5_.5, f32[768,128]{1,0:T(8,128)} %bitcast.18), custom_call_target="tpu_custom_call" | custom-call | flops 805306368 | bytes 2457600 | tf_op jit(solution)/shard_map/pallas_call | solution.py:231
  (3 shorter events, 0.0 us)
Async XLA Ops:
  27.8 0.6 copy-start
  27.8 0.7 copy-start.2
  116.2 0.6 copy-start.1

commit v22 on v20

--- a/solution.py
+++ b/solution.py
@@ -295,7 +295,7 @@
             sums_ref[k, rows, :] = sums[k]
         return carry
 
-    lax.fori_loop(0, targets // 8, group, 0)
+    lax.fori_loop(0, targets // 8, group, 0, unroll=2)
     ones = jnp.ones((8, 128), jnp.bfloat16)
     for k in range(6):
         value = sums_ref[k]

time: 178 us -> 178 us (level)
  no operation moved by 1% of the time
where the time goes in v22:
time: 178 us; the launch traced here: 177 us
  blocking collectives  108 us (61%)
  Pallas kernels  62.7 us (35%)
  local copies, waits for them, and re-layouts  5.44 us (3%)
    pallas_call x2, Pallas kernels, mobility_own(): pl.pallas_call(pair_kernel, out_shape=jax.ShapeDtypeStruct((6, own_rows),...  50 us
    all_to_all x2, blocking collectives, per_device(): pieces = lax.all_to_all(pieces, AXES, 0, 0, tiled=True)  40.2 us
    all_to_all x2, blocking collectives, per_device(): every = lax.all_to_all(every, AXES, 0, 0, tiled=True)  32.7 us
    all_to_all x1, blocking collectives, per_device(): lax.all_to_all(jnp.broadcast_to(block, (devices, 1, 9 * own_rows)), AXES,...  18.5 us
    all_to_all x1, blocking collectives, per_device(): lax.all_to_all(jnp.broadcast_to(block, (devices, 1, 6 * own_rows)), AXES,...  16.6 us
    pallas_call x3, Pallas kernels, contact_step(): pl.pallas_call(functools.partial(contact_kernel, step, gather, scatter),...  12.7 us

profile of v22, /device:TPU:1, one launch (start us, length us, event | category | flops | bytes accessed | tf_op | source)
XLA Modules:
  0.0 177.4 jit_solution(10505976228289606197)
XLA Ops:
  0.6 3.5 %shard_map.86 = f32[128,1,768]{2,1,0:T(1,128)} custom-call(s32[2,1024]{1,0:T(2,128)} %refs_0_.5, f32[9,1024]{1,0:T(8,128)} %refs_1_.5, f32[1,1024]{1,0:T(1,128)} %bitcast.23, f32[1,1024]{1,0:T(1,128)} %bitcast.25, f32[1,1024]{1,0:T(1,128)} %bitcast.27, f32[2]{0:T(128)} %refs_5_.5), custom_call_target="tpu_custom_call" | custom-call | flops 805306368 | bytes 2457600 | tf_op jit(solution)/shard_map/pallas_call | solution.py:231
  4.1 23.4 %all_to_all.38 = f32[128,1,768]{2,1,0:T(1,128)S(1)} all-to-all(f32[128,1,768]{2,1,0:T(1,128)} %shard_map.86), channel_id=1, replica_groups=mesh['src'=16,'tgt'=8] {'src','tgt'}, dimensions={0} | all-to-all | bytes 786432 | tf_op jit(solution)/shard_map/all_to_all | solution.py:360
  27.6 0.3 reduce_sum.18
  27.8 0.0 copy-start
  27.8 0.0 copy-start.2
  27.9 0.6 copy-done
  28.4 0.1 copy-done.2
  28.5 0.3 broadcast_in_dim.27
  28.9 18.5 %all_to_all.39.place_ref.force_ref = f32[128,1,1152]{2,1,0:T(1,128)} all-to-all(f32[128,1,1152]{2,1,0:T(1,128)S(1)} %broadcast_in_dim.27), channel_id=1, replica_groups=mesh['src'=16,'tgt'=8] {'src','tgt'}, dimensions={0} | all-to-all | bytes 1179648 | tf_op jit(solution)/shard_map/all_to_all | solution.py:364
  47.3 25.0 %shard_map.87 = f32[6,128]{1,0:T(8,128)} custom-call(f32[3,128]{1,0:T(4,128)} %position_ref.3, f32[128,1,1152]{2,1,0:T(1,128)} %all_to_all.39.place_ref.force_ref, f32[128,1,1152]{2,1,0:T(1,128)} %all_to_all.39.place_ref.force_ref, f32[6,128]{1,0:T(8,128)} %bitcast.19), custom_call_target="tpu_custom_call" | custom-call | flops 188743680 | bytes 786432 | tf_op jit(solution)/shard_map/pallas_call | solution.py:319
  72.3 0.9 broadcast_in_dim.29
  73.2 16.5 %all_to_all.40 = f32[128,1,768]{2,1,0:T(1,128)S(1)} all-to-all(f32[128,1,768]{2,1,0:T(1,128)S(1)} %broadcast_in_dim.29), channel_id=1, replica_groups=mesh['src'=16,'tgt'=8] {'src','tgt'}, dimensions={0} | all-to-all | bytes 786432 | tf_op jit(solution)/shard_map/all_to_all | solution.py:375
  89.7 1.1 copy.9
  90.8 5.6 %shard_map.88 = (f32[1,1024]{1,0:T(1,128)}, f32[1,1024]{1,0:T(1,128)}, f32[128,1,768]{2,1,0:T(1,128)}) custom-call(s32[2,1024]{1,0:T(2,128)} %refs_0_.5, f32[9,1024]{1,0:T(8,128)} %refs_1_.5, f32[1,1024]{1,0:T(1,128)} %bitcast.24, f32[1,1024]{1,0:T(1,128)} %bitcast.26, f32[1,1024]{1,0:T(1,128)} %bitcast.28, f32[2]{0:T(128)} %refs_5_.5, f32[768,128]{1,0:T(8,128)} %bitcast.17), custom_call_target="tpu_custom_call" | custom-call | flops 1610612736 | bytes 2457600 | tf_op jit(solution)/shard_map/pallas_call | solution.py:231
  96.4 16.8 %all_to_all.41 = f32[128,1,768]{2,1,0:T(1,128)S(1)} all-to-all(f32[128,1,768]{2,1,0:T(1,128)} %get-tuple-element.7), channel_id=1, replica_groups=mesh['src'=16,'tgt'=8] {'src','tgt'}, dimensions={0} | all-to-all | bytes 786432 | tf_op jit(solution)/shard_map/all_to_all | solution.py:360
  113.2 0.3 reduce_sum.19
  113.5 0.0 copy-start.1
  113.5 0.2 broadcast_in_dim.30
  113.7 0.4 copy-done.1
  114.1 16.6 %all_to_all.42.force_ref = f32[128,1,768]{2,1,0:T(1,128)} all-to-all(f32[128,1,768]{2,1,0:T(1,128)S(1)} %broadcast_in_dim.30), channel_id=1, replica_groups=mesh['src'=16,'tgt'=8] {'src','tgt'}, dimensions={0} | all-to-all | bytes 786432 | tf_op jit(solution)/shard_map/all_to_all | solution.py:370
  130.7 25.0 %shard_map.89 = f32[6,128]{1,0:T(8,128)} custom-call(f32[3,128]{1,0:T(4,128)} %position_ref.3, f32[128,1,1152]{2,1,0:T(1,128)} %all_to_all.39.place_ref.force_ref, f32[128,1,768]{2,1,0:T(1,128)} %all_to_all.42.force_ref, f32[6,128]{1,0:T(8,128)} %bitcast.20), custom_call_target="tpu_custom_call" | custom-call | flops 188743680 | bytes 786432 | tf_op jit(solution)/shard_map/pallas_call | solution.py:319
  155.7 0.9 broadcast_in_dim.32
  156.6 16.2 %all_to_all.43 = f32[128,1,768]{2,1,0:T(1,128)S(1)} all-to-all(f32[128,1,768]{2,1,0:T(1,128)S(1)} %broadcast_in_dim.32), channel_id=1, replica_groups=mesh['src'=16,'tgt'=8] {'src','tgt'}, dimensions={0} | all-to-all | bytes 786432 | tf_op jit(solution)/shard_map/all_to_all | solution.py:375
  172.8 1.1 copy.10
  173.8 3.5 %shard_map.90 = f32[1,1024]{1,0:T(1,128)} custom-call(s32[2,1024]{1,0:T(2,128)} %refs_0_.5, f32[9,1024]{1,0:T(8,128)} %refs_1_.5, f32[1,1024]{1,0:T(1,128)} %get-tuple-element.5.refs_2_, f32[1,1024]{1,0:T(1,128)} %get-tuple-element.6.refs_3_, f32[1,1024]{1,0:T(1,128)} %bitcast.29, f32[2]{0:T(128)} %refs_5_.5, f32[768,128]{1,0:T(8,128)} %bitcast.18), custom_call_target="tpu_custom_call" | custom-call | flops 805306368 | bytes 2457600 | tf_op jit(solution)/shard_map/pallas_call | solution.py:231
  (3 shorter events, 0.0 us)
Async XLA Ops:
  27.8 0.6 copy-start
  27.8 0.7 copy-start.2
  113.5 0.6 copy-start.1

commit v23 on v20

--- a/solution.py
+++ b/solution.py
@@ -154,8 +154,8 @@
         table_ref, refs = refs[0], refs[1:]
     outs = refs
     contacts = frame_ref.shape[1]
-    owners = outs[-1].shape[0] if scatter else table_ref.shape[1]
-    slots = outs[-1].shape[2] // 6 if scatter else table_ref.shape[0] // 6
+    owners = outs[-1].shape[0] if scatter else table_ref.shape[2]
+    slots = outs[-1].shape[2] // 6 if scatter else table_ref.shape[1] // 6
     frame = frame_ref[...]
     normal = (frame[0:1], frame[1:2], frame[2:3])
 
@@ -190,7 +190,7 @@
             slot_wide = slot_hot[side].astype(jnp.float32)
             for k in range(6):
                 picked = None
-                for part in split_pair(table_ref[k * slots : (k + 1) * slots, :]):
+                for part in (table_ref[0, k * slots : (k + 1) * slots, :], table_ref[1, k * slots : (k + 1) * slots, :]):
                     term = jnp.dot(part, owner_hot[side], preferred_element_type=jnp.float32)
                     picked = term if picked is None else picked + term
                 velocity = jnp.sum(picked * slot_wide, axis=0, keepdims=True)
@@ -375,7 +375,7 @@
         every = lax.all_to_all(every, AXES, 0, 0, tiled=True)
         last = k == ITERS - 1
         result = contact_step(
-            k, devices, own_rows, contact_bodies, contact_frame, state, gaps_row, step_sizes, every.T, scatter=not last
+            k, devices, own_rows, contact_bodies, contact_frame, state, gaps_row, step_sizes, split_two(every.T), scatter=not last
         )
         state = result[:2]
         if not last:

time: 178 us -> 178 us (level)
  no operation moved by 1% of the time
where the time goes in v23:
time: 178 us
  blocking collectives  108 us (61%)
  Pallas kernels  62.8 us (35%)
  local copies, waits for them, and re-layouts  4.09 us (2%)
  other arithmetic  2.26 us (1%)
    pallas_call x2, Pallas kernels, mobility_own(): pl.pallas_call(pair_kernel, out_shape=jax.ShapeDtypeStruct((6, own_rows),...  50.2 us
    all_to_all x2, blocking collectives, per_device(): pieces = lax.all_to_all(pieces, AXES, 0, 0, tiled=True)  40.2 us
    all_to_all x2, blocking collectives, per_device(): every = lax.all_to_all(every, AXES, 0, 0, tiled=True)  32.7 us
    all_to_all x1, blocking collectives, per_device(): lax.all_to_all(jnp.broadcast_to(block, (devices, 1, 9 * own_rows)), AXES,...  18.4 us
    all_to_all x1, blocking collectives, per_device(): lax.all_to_all(jnp.broadcast_to(block, (devices, 1, 6 * own_rows)), AXES,...  16.6 us
    pallas_call x3, Pallas kernels, contact_step(): pl.pallas_call(functools.partial(contact_kernel, step, gather, scatter),...  12.7 us

profile of v23, /device:TPU:1, one launch (start us, length us, event | category | flops | bytes accessed | tf_op | source)
XLA Modules:
  0.0 177.8 jit_solution(2943510938412990062)
XLA Ops:
  0.6 3.5 %shard_map.86 = f32[128,1,768]{2,1,0:T(1,128)} custom-call(s32[2,1024]{1,0:T(2,128)} %refs_0_.5, f32[9,1024]{1,0:T(8,128)} %refs_1_.5, f32[1,1024]{1,0:T(1,128)} %bitcast.41, f32[1,1024]{1,0:T(1,128)} %bitcast.43, f32[1,1024]{1,0:T(1,128)} %bitcast.45, f32[2]{0:T(128)} %refs_5_.5), custom_call_target="tpu_custom_call" | custom-call | flops 805306368 | bytes 2457600 | tf_op jit(solution)/shard_map/pallas_call | solution.py:231
  4.1 23.4 %all_to_all.38 = f32[128,1,768]{2,1,0:T(1,128)S(1)} all-to-all(f32[128,1,768]{2,1,0:T(1,128)} %shard_map.86), channel_id=1, replica_groups=mesh['src'=16,'tgt'=8] {'src','tgt'}, dimensions={0} | all-to-all | bytes 786432 | tf_op jit(solution)/shard_map/all_to_all | solution.py:360
  27.6 0.3 reduce_sum.18
  27.8 0.0 copy-start
  27.8 0.0 copy-start.2
  27.9 0.6 copy-done
  28.4 0.1 copy-done.2
  28.5 0.3 broadcast_in_dim.27
  28.8 18.4 %all_to_all.39.place_ref.force_ref = f32[128,1,1152]{2,1,0:T(1,128)} all-to-all(f32[128,1,1152]{2,1,0:T(1,128)S(1)} %broadcast_in_dim.27), channel_id=1, replica_groups=mesh['src'=16,'tgt'=8] {'src','tgt'}, dimensions={0} | all-to-all | bytes 1179648 | tf_op jit(solution)/shard_map/all_to_all | solution.py:364
  47.3 25.1 %shard_map.87 = f32[6,128]{1,0:T(8,128)} custom-call(f32[3,128]{1,0:T(4,128)} %position_ref.3, f32[128,1,1152]{2,1,0:T(1,128)} %all_to_all.39.place_ref.force_ref, f32[128,1,1152]{2,1,0:T(1,128)} %all_to_all.39.place_ref.force_ref, f32[6,128]{1,0:T(8,128)} %bitcast.37), custom_call_target="tpu_custom_call" | custom-call | flops 188743680 | bytes 786432 | tf_op jit(solution)/shard_map/pallas_call | solution.py:319
  72.4 0.9 broadcast_in_dim.29
  73.3 16.5 %all_to_all.40 = f32[128,1,768]{2,1,0:T(1,128)S(1)} all-to-all(f32[128,1,768]{2,1,0:T(1,128)S(1)} %broadcast_in_dim.29), channel_id=1, replica_groups=mesh['src'=16,'tgt'=8] {'src','tgt'}, dimensions={0} | all-to-all | bytes 786432 | tf_op jit(solution)/shard_map/all_to_all | solution.py:375
  89.8 0.4 copy.9
  90.2 0.1 fusion.4
  90.2 0.8 pad_maximum_fusion.refs_6_
  91.0 5.6 %shard_map.88 = (f32[1,1024]{1,0:T(1,128)}, f32[1,1024]{1,0:T(1,128)}, f32[128,1,768]{2,1,0:T(1,128)}) custom-call(s32[2,1024]{1,0:T(2,128)} %refs_0_.5, f32[9,1024]{1,0:T(8,128)} %refs_1_.5, f32[1,1024]{1,0:T(1,128)} %bitcast.42, f32[1,1024]{1,0:T(1,128)} %bitcast.44, f32[1,1024]{1,0:T(1,128)} %bitcast.46, f32[2]{0:T(128)} %refs_5_.5, ...), custom_call_target="tpu_custom_call" | custom-call | flops 1610612736 | bytes 2457600 | tf_op jit(solution)/shard_map/pallas_call | solution.py:231
  96.7 16.8 %all_to_all.41 = f32[128,1,768]{2,1,0:T(1,128)S(1)} all-to-all(f32[128,1,768]{2,1,0:T(1,128)} %get-tuple-element.7), channel_id=1, replica_groups=mesh['src'=16,'tgt'=8] {'src','tgt'}, dimensions={0} | all-to-all | bytes 786432 | tf_op jit(solution)/shard_map/all_to_all | solution.py:360
  113.4 0.3 reduce_sum.19
  113.7 0.0 copy-start.1
  113.7 0.2 broadcast_in_dim.30
  113.9 0.4 copy-done.1
  114.3 16.6 %all_to_all.42.force_ref = f32[128,1,768]{2,1,0:T(1,128)} all-to-all(f32[128,1,768]{2,1,0:T(1,128)S(1)} %broadcast_in_dim.30), channel_id=1, replica_groups=mesh['src'=16,'tgt'=8] {'src','tgt'}, dimensions={0} | all-to-all | bytes 786432 | tf_op jit(solution)/shard_map/all_to_all | solution.py:370
  130.9 25.0 %shard_map.89 = f32[6,128]{1,0:T(8,128)} custom-call(f32[3,128]{1,0:T(4,128)} %position_ref.3, f32[128,1,1152]{2,1,0:T(1,128)} %all_to_all.39.place_ref.force_ref, f32[128,1,768]{2,1,0:T(1,128)} %all_to_all.42.force_ref, f32[6,128]{1,0:T(8,128)} %bitcast.38), custom_call_target="tpu_custom_call" | custom-call | flops 188743680 | bytes 786432 | tf_op jit(solution)/shard_map/pallas_call | solution.py:319
  156.0 0.9 broadcast_in_dim.32
  156.8 16.2 %all_to_all.43 = f32[128,1,768]{2,1,0:T(1,128)S(1)} all-to-all(f32[128,1,768]{2,1,0:T(1,128)S(1)} %broadcast_in_dim.32), channel_id=1, replica_groups=mesh['src'=16,'tgt'=8] {'src','tgt'}, dimensions={0} | all-to-all | bytes 786432 | tf_op jit(solution)/shard_map/all_to_all | solution.py:375
  173.1 0.4 copy.10
  173.4 0.1 fusion.5
  173.5 0.8 pad_maximum_fusion.1.refs_6_
  174.3 3.5 %shard_map.90 = f32[1,1024]{1,0:T(1,128)} custom-call(s32[2,1024]{1,0:T(2,128)} %refs_0_.5, f32[9,1024]{1,0:T(8,128)} %refs_1_.5, f32[1,1024]{1,0:T(1,128)} %get-tuple-element.5.refs_2_, f32[1,1024]{1,0:T(1,128)} %get-tuple-element.6.refs_3_, f32[1,1024]{1,0:T(1,128)} %bitcast.47, f32[2]{0:T(128)} %refs_5_.5, bf16[2,768,128]{2,1,0:T(8,128)(2,1)} %pad_maximum_fusion.1.refs_6_), custom_call_target="tpu_custom_call" | custom-call | flops 805306368 | bytes 2457600 | tf_op jit(solution)/shard_map/pallas_call | solution.py:231
  (3 shorter events, 0.0 us)
Async XLA Ops:
  27.8 0.6 copy-start
  27.8 0.7 copy-start.2
  113.7 0.6 copy-start.1

commit v24 on v20

--- a/solution.py
+++ b/solution.py
@@ -187,13 +187,13 @@
     if gather:
         rate = None
         for side in range(2):
-            slot_wide = slot_hot[side].astype(jnp.float32)
+            slot_mask = slot_hot[side] > 0
             for k in range(6):
                 picked = None
                 for part in split_pair(table_ref[k * slots : (k + 1) * slots, :]):
                     term = jnp.dot(part, owner_hot[side], preferred_element_type=jnp.float32)
                     picked = term if picked is None else picked + term
-                velocity = jnp.sum(picked * slot_wide, axis=0, keepdims=True)
+                velocity = jnp.sum(jnp.where(slot_mask, picked, 0.0), axis=0, keepdims=True)
                 term = rows[side][k] * velocity
                 rate = term if rate is None else rate + term
         updated = jnp.maximum(shifted - steps_ref[step] * (gaps_ref[...] + rate), 0.0)

time: 178 us -> 178 us (level)
  no operation moved by 1% of the time
where the time goes in v24:
time: 178 us
  blocking collectives  108 us (61%)
  Pallas kernels  63.2 us (36%)
  local copies, waits for them, and re-layouts  5.44 us (3%)
    pallas_call x2, Pallas kernels, mobility_own(): pl.pallas_call(pair_kernel, out_shape=jax.ShapeDtypeStruct((6, own_rows),...  50.2 us
    all_to_all x2, blocking collectives, per_device(): pieces = lax.all_to_all(pieces, AXES, 0, 0, tiled=True)  40.2 us
    all_to_all x2, blocking collectives, per_device(): every = lax.all_to_all(every, AXES, 0, 0, tiled=True)  32.7 us
    all_to_all x1, blocking collectives, per_device(): lax.all_to_all(jnp.broadcast_to(block, (devices, 1, 9 * own_rows)), AXES,...  18.5 us
    all_to_all x1, blocking collectives, per_device(): lax.all_to_all(jnp.broadcast_to(block, (devices, 1, 6 * own_rows)), AXES,...  16.6 us
    pallas_call x3, Pallas kernels, contact_step(): pl.pallas_call(functools.partial(contact_kernel, step, gather, scatter),...  13.1 us

profile of v24, /device:TPU:1, one launch (start us, length us, event | category | flops | bytes accessed | tf_op | source)
XLA Modules:
  0.0 177.9 jit_solution(14030430873526069685)
XLA Ops:
  0.6 3.5 %shard_map.86 = f32[128,1,768]{2,1,0:T(1,128)} custom-call(s32[2,1024]{1,0:T(2,128)} %refs_0_.5, f32[9,1024]{1,0:T(8,128)} %refs_1_.5, f32[1,1024]{1,0:T(1,128)} %bitcast.23, f32[1,1024]{1,0:T(1,128)} %bitcast.25, f32[1,1024]{1,0:T(1,128)} %bitcast.27, f32[2]{0:T(128)} %refs_5_.5), custom_call_target="tpu_custom_call" | custom-call | flops 805306368 | bytes 2457600 | tf_op jit(solution)/shard_map/pallas_call | solution.py:231
  4.1 23.4 %all_to_all.38 = f32[128,1,768]{2,1,0:T(1,128)S(1)} all-to-all(f32[128,1,768]{2,1,0:T(1,128)} %shard_map.86), channel_id=1, replica_groups=mesh['src'=16,'tgt'=8] {'src','tgt'}, dimensions={0} | all-to-all | bytes 786432 | tf_op jit(solution)/shard_map/all_to_all | solution.py:360
  27.6 0.3 reduce_sum.18
  27.8 0.0 copy-start
  27.8 0.0 copy-start.2
  27.9 0.6 copy-done
  28.4 0.1 copy-done.2
  28.5 0.3 broadcast_in_dim.27
  28.9 18.5 %all_to_all.39.place_ref.force_ref = f32[128,1,1152]{2,1,0:T(1,128)} all-to-all(f32[128,1,1152]{2,1,0:T(1,128)S(1)} %broadcast_in_dim.27), channel_id=1, replica_groups=mesh['src'=16,'tgt'=8] {'src','tgt'}, dimensions={0} | all-to-all | bytes 1179648 | tf_op jit(solution)/shard_map/all_to_all | solution.py:364
  47.3 25.1 %shard_map.87 = f32[6,128]{1,0:T(8,128)} custom-call(f32[3,128]{1,0:T(4,128)} %position_ref.3, f32[128,1,1152]{2,1,0:T(1,128)} %all_to_all.39.place_ref.force_ref, f32[128,1,1152]{2,1,0:T(1,128)} %all_to_all.39.place_ref.force_ref, f32[6,128]{1,0:T(8,128)} %bitcast.19), custom_call_target="tpu_custom_call" | custom-call | flops 188743680 | bytes 786432 | tf_op jit(solution)/shard_map/pallas_call | solution.py:319
  72.4 0.9 broadcast_in_dim.29
  73.3 16.5 %all_to_all.40 = f32[128,1,768]{2,1,0:T(1,128)S(1)} all-to-all(f32[128,1,768]{2,1,0:T(1,128)S(1)} %broadcast_in_dim.29), channel_id=1, replica_groups=mesh['src'=16,'tgt'=8] {'src','tgt'}, dimensions={0} | all-to-all | bytes 786432 | tf_op jit(solution)/shard_map/all_to_all | solution.py:375
  89.8 1.1 copy.9
  90.8 5.8 %shard_map.88 = (f32[1,1024]{1,0:T(1,128)}, f32[1,1024]{1,0:T(1,128)}, f32[128,1,768]{2,1,0:T(1,128)}) custom-call(s32[2,1024]{1,0:T(2,128)} %refs_0_.5, f32[9,1024]{1,0:T(8,128)} %refs_1_.5, f32[1,1024]{1,0:T(1,128)} %bitcast.24, f32[1,1024]{1,0:T(1,128)} %bitcast.26, f32[1,1024]{1,0:T(1,128)} %bitcast.28, f32[2]{0:T(128)} %refs_5_.5, f32[768,128]{1,0:T(8,128)} %bitcast.17), custom_call_target="tpu_custom_call" | custom-call | flops 1610612736 | bytes 2457600 | tf_op jit(solution)/shard_map/pallas_call | solution.py:231
  96.7 16.8 %all_to_all.41 = f32[128,1,768]{2,1,0:T(1,128)S(1)} all-to-all(f32[128,1,768]{2,1,0:T(1,128)} %get-tuple-element.7), channel_id=1, replica_groups=mesh['src'=16,'tgt'=8] {'src','tgt'}, dimensions={0} | all-to-all | bytes 786432 | tf_op jit(solution)/shard_map/all_to_all | solution.py:360
  113.4 0.3 reduce_sum.19
  113.7 0.0 copy-start.1
  113.7 0.2 broadcast_in_dim.30
  113.9 0.4 copy-done.1
  114.3 16.6 %all_to_all.42.force_ref = f32[128,1,768]{2,1,0:T(1,128)} all-to-all(f32[128,1,768]{2,1,0:T(1,128)S(1)} %broadcast_in_dim.30), channel_id=1, replica_groups=mesh['src'=16,'tgt'=8] {'src','tgt'}, dimensions={0} | all-to-all | bytes 786432 | tf_op jit(solution)/shard_map/all_to_all | solution.py:370
  130.9 25.0 %shard_map.89 = f32[6,128]{1,0:T(8,128)} custom-call(f32[3,128]{1,0:T(4,128)} %position_ref.3, f32[128,1,1152]{2,1,0:T(1,128)} %all_to_all.39.place_ref.force_ref, f32[128,1,768]{2,1,0:T(1,128)} %all_to_all.42.force_ref, f32[6,128]{1,0:T(8,128)} %bitcast.20), custom_call_target="tpu_custom_call" | custom-call | flops 188743680 | bytes 786432 | tf_op jit(solution)/shard_map/pallas_call | solution.py:319
  156.0 0.9 broadcast_in_dim.32
  156.9 16.2 %all_to_all.43 = f32[128,1,768]{2,1,0:T(1,128)S(1)} all-to-all(f32[128,1,768]{2,1,0:T(1,128)S(1)} %broadcast_in_dim.32), channel_id=1, replica_groups=mesh['src'=16,'tgt'=8] {'src','tgt'}, dimensions={0} | all-to-all | bytes 786432 | tf_op jit(solution)/shard_map/all_to_all | solution.py:375
  173.1 1.1 copy.10
  174.1 3.8 %shard_map.90 = f32[1,1024]{1,0:T(1,128)} custom-call(s32[2,1024]{1,0:T(2,128)} %refs_0_.5, f32[9,1024]{1,0:T(8,128)} %refs_1_.5, f32[1,1024]{1,0:T(1,128)} %get-tuple-element.5.refs_2_, f32[1,1024]{1,0:T(1,128)} %get-tuple-element.6.refs_3_, f32[1,1024]{1,0:T(1,128)} %bitcast.29, f32[2]{0:T(128)} %refs_5_.5, f32[768,128]{1,0:T(8,128)} %bitcast.18), custom_call_target="tpu_custom_call" | custom-call | flops 805306368 | bytes 2457600 | tf_op jit(solution)/shard_map/pallas_call | solution.py:231
  (3 shorter events, 0.0 us)
Async XLA Ops:
  27.8 0.6 copy-start
  27.8 0.7 copy-start.2
  113.7 0.6 copy-start.1
